TPU v7x, 256 devices: a whole 4x4x8 slice. The times are simulated.
256 devices in a mesh: pair: 16 (over z, core), virt: 16 (over x, y).
Axes of the slice: x: 4, y: 4, z: 8, core: 2. Of those that a mesh axis runs over, the one named last changes fastest.
Arguments:
- amplitudes: float32 [64, 2048, 4096], P('virt', 'pair'), may hold values from -0.9 to 0.9
- integrals: float32 [64, 384, 4096], P('virt', 'pair'), may hold values from -0.09375 to 0.09375
- tile_flags: int32 [64], P('virt'), may hold values 0 or 1
- live_count: int32 [16], replicated, may hold values from 1 to 4, as said below
- pair_occ: int32 [2048, 2], P(('pair', 'virt')), may hold values from 0 to 199
- occ_energy: float32 [200], replicated, may hold values from -2.5 to -0.3
- ab_energy: float32 [384], replicated, may hold values from 0.6 to 3
Outputs:
- ladder: float32 [2048, 384], P(('pair', 'virt'))
- update: float32 [2048, 384], P(('pair', 'virt'))
Inputs may be any that keep to these rules, and one draw needn't show every extreme that they name: `live_count`: entry v is how many of the 4 slots of virt index v hold tile pairs: its slots below that number do, and the contents of the others are not to be used. At some index it is 4, and at the index half the axis away it is 1.
All inputs are finite; a program needn't handle non-finite values. No bound on the sum of `tile_flags` on one device may be relied on, other than what follows from the above.
Results may differ from a plain program's by a relative error of at most 0.0001.
Values sent between devices are 32-bit elements; how exact they have to be, the bound alone decides.
No kernel may reach another device: no remote copies, remote signals or barrier semaphores. Data moves between devices by JAX's collectives and lax.ppermute only.
A program may use at most 128 MiB of HBM per device.

v0:
```python
import jax
import jax.numpy as jnp
from jax import lax
from jax.sharding import PartitionSpec as P

TILE = 64


def symmetric(integrals, tile_flags):
    shaped = integrals.reshape(integrals.shape[0], integrals.shape[1], TILE, TILE)
    swapped = jnp.swapaxes(shaped, 2, 3).reshape(integrals.shape)
    return integrals + tile_flags.astype(jnp.float32)[:, None, None] * swapped


def tile_product(amp_tile, int_rows):
    return lax.dot_general(
        amp_tile,
        int_rows,
        (((1,), (1,)), ((), ())),
        precision=lax.Precision.HIGHEST,
        preferred_element_type=jnp.float32,
    )


def take_slot(stack, slot_at):
    return lax.dynamic_index_in_dim(stack, slot_at, 0, keepdims=False)


def contract(amp_stack, int_stack, first_slot, last_slot, pair_rows):
    piece_rows = lax.all_gather(int_stack, "pair", axis=1, tiled=True)

    def add_tile(slot_at, running):
        return running + tile_product(take_slot(amp_stack, slot_at), take_slot(piece_rows, slot_at))

    return lax.fori_loop(
        first_slot, last_slot, add_tile, jnp.zeros((pair_rows, piece_rows.shape[1]), jnp.float32)
    )


def on_device(amplitudes, integrals, tile_flags, live_count, pair_occ, occ_energy, ab_energy):
    pair_rows = amplitudes.shape[1]
    virt_index = lax.axis_index("virt")
    own_count = live_count[virt_index]
    sym_integrals = symmetric(integrals, tile_flags)
    partial_value = contract(amplitudes, sym_integrals, 0, own_count, pair_rows)
    ladder = lax.psum_scatter(partial_value, "virt", scatter_dimension=0, tiled=True)
    occ_range = jnp.arange(occ_energy.shape[0], dtype=jnp.int32)
    first_energy = jnp.sum(
        jnp.where(pair_occ[:, 0:1] == occ_range[None, :], occ_energy[None, :], 0.0), axis=1
    )
    second_energy = jnp.sum(
        jnp.where(pair_occ[:, 1:2] == occ_range[None, :], occ_energy[None, :], 0.0), axis=1
    )
    denominator = ab_energy[None, :] - first_energy[:, None] - second_energy[:, None]
    return (ladder, ladder / denominator)


def solution(mesh):
    return jax.shard_map(
        on_device,
        mesh=mesh,
        in_specs=(
            P("virt", "pair", None),
            P("virt", "pair", None),
            P("virt"),
            P(),
            P(("pair", "virt"), None),
            P(),
            P(),
        ),
        out_specs=(P(("pair", "virt"), None), P(("pair", "virt"), None)),
        check_vma=False,
    )
```

profile of v0, /device:TPU:2, one launch (start us, length us, event | category | flops | bytes accessed | tf_op | source)
XLA Modules:
  0.0 297.7 jit_solution(7873648471273782009)
XLA Ops:
  7.2 0.0 all-gather.2.cloned.1.call-start
  7.2 3.6 %reshape.15 = f32[4,24,64,64]{3,2,1,0:T(8,128)} reshape(f32[4,24,4096]{2,1,0:T(8,128)} %param.10) | data formatting | bytes 3145728 | tf_op jit(solution)/shard_map/reshape | solution.py:10
  10.8 2.4 copy.11
  13.1 0.0 copy-start.4
  13.2 1.9 reshape.16
  15.1 0.0 copy-done.4
  15.1 0.0 copy-start.5
  15.1 3.3 %multiply_add_fusion = f32[4,24,4096]{2,1,0:T(8,128)} fusion(f32[4,24,4096]{2,1,0:T(8,128)} %param.10, f32[4,24,4096]{2,1,0:T(8,128)} %reshape.16, f32[4]{0:T(128)S(1)} %convert_element_type.3), kind=kLoop, calls=%fused_computation.7 | loop fusion | flops 786432 | bytes 4718608 | tf_op jit(solution)/shard_map/add | solution.py:12
  18.4 0.0 all-gather.2.cloned.1.call-update
  18.4 0.0 all-reduce.3.cloned.1.call-start
  18.5 0.0 copy-done.5
  18.5 0.6 dynamic_slice.11
  19.1 137.3 %all-gather.2.cloned.1.call-done = f32[4,384,4096]{2,1,0:T(8,128)} async-done(((f32[4,24,4096]{2,1,0:T(8,128)}), f32[4,384,4096]{2,1,0:T(8,128)}) %all-gather.2.cloned.1.call-update) | async-done | bytes 25165840 | tf_op jit(solution)/shard_map/all_gather | solution.py:30
  156.4 0.0 copy-start.3
  156.4 0.0 copy-start.6
  156.4 0.0 copy-start.2
  156.5 0.0 copy-start.1
  156.5 40.0 %while.10 = (s32[]{:T(128)}, f32[128,384]{1,0:T(8,128)S(1)}, s32[]{:T(128)}, f32[4,128,4096]{2,1,0:T(8,128)}, f32[4,384,4096]{2,1,0:T(8,128)}, /*index=5*/s32[]{:T(128)}, s32[]{:T(128)}, s32[]{:T(128)}) while((s32[]{:T(128)}, f32[128,384]{1,0:T(8,128)S(1)}, s32[]{:T(128)}, f32[4,128,4096]{2,1,0:T(8,128)}, f32[4,384,4096]{2,1,0:T(8,128)}, ...), condition=%wide.region_1.2_spmd, body=%wide.region_0.1_spmd.sunk | while | flops 2415968256 | bytes 8782967 | solution.py:35
  157.2 9.2 %fusion.16 = f32[128,384]{1,0:T(8,128)S(1)} fusion(f32[128,384]{1,0:T(8,128)S(1)} %get-tuple-element.88, f32[4,384,4096]{2,1,0:T(8,128)} %get-tuple-element.99, s32[]{:T(128)S(6)} %select_n.22, f32[4,128,4096]{2,1,0:T(8,128)} %get-tuple-element.98), kind=kOutput, calls=%fused_computation.5.clone.1 | convolution fusion | flops 2415968256 | bytes 8782848 | tf_op jit(solution)/shard_map/while/body/dot_general | solution.py:16
  167.0 9.2 %fusion.16 = f32[128,384]{1,0:T(8,128)S(1)} fusion(f32[128,384]{1,0:T(8,128)S(1)} %get-tuple-element.88, f32[4,384,4096]{2,1,0:T(8,128)} %get-tuple-element.99, s32[]{:T(128)S(6)} %select_n.22, f32[4,128,4096]{2,1,0:T(8,128)} %get-tuple-element.98), kind=kOutput, calls=%fused_computation.5.clone.1 | convolution fusion | flops 2415968256 | bytes 8782848 | tf_op jit(solution)/shard_map/while/body/dot_general | solution.py:16
  176.8 9.2 %fusion.16 = f32[128,384]{1,0:T(8,128)S(1)} fusion(f32[128,384]{1,0:T(8,128)S(1)} %get-tuple-element.88, f32[4,384,4096]{2,1,0:T(8,128)} %get-tuple-element.99, s32[]{:T(128)S(6)} %select_n.22, f32[4,128,4096]{2,1,0:T(8,128)} %get-tuple-element.98), kind=kOutput, calls=%fused_computation.5.clone.1 | convolution fusion | flops 2415968256 | bytes 8782848 | tf_op jit(solution)/shard_map/while/body/dot_general | solution.py:16
  186.6 9.2 %fusion.16 = f32[128,384]{1,0:T(8,128)S(1)} fusion(f32[128,384]{1,0:T(8,128)S(1)} %get-tuple-element.88, f32[4,384,4096]{2,1,0:T(8,128)} %get-tuple-element.99, s32[]{:T(128)S(6)} %select_n.22, f32[4,128,4096]{2,1,0:T(8,128)} %get-tuple-element.98), kind=kOutput, calls=%fused_computation.5.clone.1 | convolution fusion | flops 2415968256 | bytes 8782848 | tf_op jit(solution)/shard_map/while/body/dot_general | solution.py:16
  196.5 0.0 copy-start
  196.5 0.7 copy-done
  197.1 0.0 all-reduce.3.cloned.1.call-update
  197.2 0.0 copy-done.3
  197.2 0.0 copy-done.6
  197.2 0.6 dynamic-slice
  198.4 0.0 copy-done.2
  198.4 0.2 select_reduce_fusion.1
  198.7 90.9 %all-reduce.3.cloned.1.call-done = f32[128,384]{1,0:T(8,128)} async-done(((f32[128,384]{1,0:T(8,128)}), f32[128,384]{1,0:T(8,128)}) %all-reduce.3.cloned.1.call-update) | async-done | bytes 196624
  289.5 0.0 copy-done.1
  289.5 1.4 subtract_divide_fusion
  (3 shorter events, 0.0 us)
Async XLA Ops:
  7.2 149.2 %all-gather.2.cloned.1.call-start = ((), (), s32[]{:S(2)}) async-start(), calls=%async_computation | async-start | bytes 26738688 | tf_op jit(solution)/shard_map/all_gather | solution.py:30
  13.1 1.9 copy-start.4
  15.1 3.4 %copy-start.5 = (s32[16]{0:T(128)S(1)}, s32[16]{0:T(128)}, u32[]{:S(2)}) copy-start(s32[16]{0:T(128)} %param.12) | copy-start | bytes 196
  18.4 271.1 %all-reduce.3.cloned.1.call-start = ((), (), s32[]{:S(2)}) async-start(), calls=%async_computation.1 | async-start | bytes 393216
  156.4 40.7 %copy-start.3 = (s32[8,2]{0,1:T(2,128)S(1)}, s32[8,2]{0,1:T(2,128)}, u32[]{:S(2)}) copy-start(s32[8,2]{0,1:T(2,128)} %param.13) | copy-start | bytes 196
  156.4 40.8 %copy-start.6 = (u32[256]{0:T(256)S(1)}, u32[256]{0:T(256)}, u32[]{:S(2)}) copy-start(u32[256]{0:T(256)} %constant.29) | copy-start | bytes 3076
  156.4 42.0 %copy-start.2 = (f32[200]{0:T(256)S(1)}, f32[200]{0:T(256)}, u32[]{:S(2)}) copy-start(f32[200]{0:T(256)} %param.14) | copy-start | bytes 2404
  156.5 133.1 %copy-start.1 = (f32[384]{0:T(512)S(1)}, f32[384]{0:T(512)}, u32[]{:S(2)}) copy-start(f32[384]{0:T(512)} %param.15) | copy-start | bytes 4612
  196.5 0.7 copy-start
Sparse Core Ops, SparseCore 0:
  18.6 137.7 all-gather.1
  197.3 92.1 all-reduce.2
where the time goes:
time: 298 us
  waiting for transfers between devices  228 us (77%)
  matrix products  36.6 us (12%)
  between operations  14.8 us (5%)
  local copies, waits for them, and re-layouts  9.74 us (3%)
  other arithmetic  4.93 us (2%)
  loops' own time  3.36 us (1%)
    all_gather x1, waiting for transfers between devices, contract(): piece_rows = lax.all_gather(int_stack, 'pair', axis=1, tiled=True)  137 us
    unnamed x3, waiting for transfers between devices  90.9 us
    dot_general x4, matrix products, tile_product(): lax.dot_general(amp_tile, int_rows, (((1,), (1,)), ((), ())), precision=l...  36.6 us
  transfers between devices with their start and end apart: 2, of which 2 were waited for; matrix products, arithmetic and copies ran while one was open for 0% of the time, Pallas kernels for 0%

commit v1 on v0

v1 whole, which is shorter than its diff:
```python
import jax
import jax.numpy as jnp
from jax import lax
from jax.sharding import PartitionSpec as P

TILE = 64


def symmetric_rows(rows, flag):
    shaped = rows.reshape(rows.shape[0], TILE, TILE)
    swapped = jnp.swapaxes(shaped, 1, 2).reshape(rows.shape)
    return rows + flag.astype(jnp.float32) * swapped


def tile_product(amp_tile, int_rows):
    return lax.dot_general(
        amp_tile,
        int_rows,
        (((1,), (1,)), ((), ())),
        precision=lax.Precision.HIGHEST,
        preferred_element_type=jnp.float32,
    )


def on_device(amplitudes, integrals, tile_flags, live_count, pair_occ, occ_energy, ab_energy):
    slots, pair_rows, _ = amplitudes.shape
    virt_index = lax.axis_index("virt")
    n_virt = lax.axis_size("virt")
    own_count = live_count[virt_index]

    running = None
    for slot in range(slots):
        sym_rows = symmetric_rows(integrals[slot], tile_flags[slot])
        gathered = lax.all_gather(sym_rows, "pair", axis=0, tiled=True)
        term = tile_product(amplitudes[slot], gathered)
        term = jnp.where(slot < own_count, term, jnp.zeros_like(term))
        running = term if running is None else running + term

    ab = running.shape[1]
    blocks = running.reshape(n_virt, pair_rows // n_virt, ab)
    received = lax.all_to_all(blocks, "virt", 0, 0, tiled=False)
    ladder = jnp.sum(received, axis=0)

    occ_range = jnp.arange(occ_energy.shape[0], dtype=jnp.int32)
    first_energy = jnp.sum(
        jnp.where(pair_occ[:, 0:1] == occ_range[None, :], occ_energy[None, :], 0.0), axis=1
    )
    second_energy = jnp.sum(
        jnp.where(pair_occ[:, 1:2] == occ_range[None, :], occ_energy[None, :], 0.0), axis=1
    )
    denominator = ab_energy[None, :] - first_energy[:, None] - second_energy[:, None]
    return (ladder, ladder / denominator)


def solution(mesh):
    return jax.shard_map(
        on_device,
        mesh=mesh,
        in_specs=(
            P("virt", "pair", None),
            P("virt", "pair", None),
            P("virt"),
            P(),
            P(("pair", "virt"), None),
            P(),
            P(),
        ),
        out_specs=(P(("pair", "virt"), None), P(("pair", "virt"), None)),
        check_vma=False,
    )
```

time: 298 us -> 244 us (0.82)
  waiting for transfers between devices: 228 us -> 163 us
  starting transfers between devices: 0.08 us -> 7.61 us
  between operations: 14.8 us -> 19 us
  loops' own time: 3.36 us -> 0 us
    unnamed x3 -> x4, waiting for transfers between devices: 90.9 us -> 1.73 us
    all_gather x1 -> x4, waiting for transfers between devices: 137 us -> 155 us  [on_device(): gathered = lax.all_gather(sym_rows, 'pair', axis=0, tiled=True)]
    reshape x3 -> x0, local copies, waits for them, and re-layouts: 7.85 us -> none  [the longest x2 5.93 us: symmetric(): integrals.reshape(integrals.shape[0], integrals.shape[1], TILE, TILE)]
    all_to_all x0 -> x1, starting transfers between devices: none -> 7.28 us  [on_device(): received = lax.all_to_all(blocks, 'virt', 0, 0, tiled=False)]
    mul x0 -> x12, local copies, waits for them, and re-layouts: none -> 6.94 us  [symmetric_rows(): return rows + flag.astype(jnp.float32) * swapped]
    all_to_all x0 -> x1, waiting for transfers between devices: none -> 6.38 us  [on_device(): received = lax.all_to_all(blocks, 'virt', 0, 0, tiled=False)]
    another operation x1 -> x0, loops' own time: 3.36 us -> none  [contract(): lax.fori_loop(first_slot, last_slot, add_tile, jnp.zeros((pair_rows, piec...]
  transfers between devices with their start and end apart: 2 -> 5, of which waited for: 2 -> 5; matrix products, arithmetic and copies ran while one was open for 0% -> 12% of each run, Pallas kernels for 0% -> 0%
where the time goes in v1:
time: 244 us; the launch traced here: 243 us
  waiting for transfers between devices  163 us (67%)
  matrix products  37.9 us (16%)
  between operations  19 us (8%)
  local copies, waits for them, and re-layouts  8.98 us (4%)
  starting transfers between devices  7.61 us (3%)
  other arithmetic  5.67 us (2%)
    all_gather x4, waiting for transfers between devices, on_device(): gathered = lax.all_gather(sym_rows, 'pair', axis=0, tiled=True)  155 us
    dot_general x4, matrix products, tile_product(): lax.dot_general(amp_tile, int_rows, (((1,), (1,)), ((), ())), precision=l...  37.9 us
    all_to_all x1, starting transfers between devices, on_device(): received = lax.all_to_all(blocks, 'virt', 0, 0, tiled=False)  7.28 us
    mul x12, local copies, waits for them, and re-layouts, symmetric_rows(): return rows + flag.astype(jnp.float32) * swapped  6.94 us
    all_to_all x1, waiting for transfers between devices, on_device(): received = lax.all_to_all(blocks, 'virt', 0, 0, tiled=False)  6.38 us
  transfers between devices with their start and end apart: 5, of which 5 were waited for; matrix products, arithmetic and copies ran while one was open for 12% of the time, Pallas kernels for 0%

profile of v1, /device:TPU:2, one launch (start us, length us, event | category | flops | bytes accessed | tf_op | source)
XLA Modules:
  0.0 242.6 jit_solution(8998881442713806201)
XLA Ops:
  7.2 0.0 all-gather.7.cloned.1.call-start
  7.2 1.4 fusion.36
  11.1 2.4 slice_multiply_fusion
  13.5 0.3 mul.62
  13.8 0.3 copy.13
  14.1 0.0 copy-start
  14.1 0.3 mul.64
  14.4 0.3 mul.67
  14.7 0.3 copy.14
  15.0 1.0 mul.69
  16.0 1.3 mul.72
  17.3 0.0 copy-start.5
  17.3 0.3 copy.15
  17.6 1.0 mul.74
  18.7 1.3 mul.77
  20.0 0.3 copy.16
  20.2 0.3 mul.79
  20.5 0.0 copy-done
  20.5 2.4 bitcast_add_fusion
  22.9 0.0 all-gather.7.cloned.1.call-update
  22.9 0.0 all-gather.9.cloned.1.call-start
  23.0 0.7 all-gather.9.cloned.1.call-update
  23.7 0.0 all-gather.5.cloned.1.call-start
  23.7 0.7 all-gather.5.cloned.1.call-update
  24.4 0.2 all-gather.11.cloned.1.call-start
  24.6 0.3 all-gather.11.cloned.1.call-update
  25.0 0.0 copy-done.5
  25.0 0.6 dynamic_slice.3
  28.2 43.9 %all-gather.7.cloned.1.call-done = f32[384,4096]{1,0:T(8,128)} async-done(((f32[24,4096]{1,0:T(8,128)}), f32[384,4096]{1,0:T(8,128)}) %all-gather.7.cloned.1.call-update) | async-done | bytes 6291472 | tf_op jit(solution)/shard_map/all_gather | solution.py:34
  72.1 9.3 %fusion.21 = f32[384,128]{0,1:T(8,128)S(1)} fusion(f32[384,4096]{1,0:T(8,128)} %all-gather.7.cloned.1.call-done, f32[4,128,4096]{2,1,0:T(8,128)} %param.7, pred[]{:T(512)} %bitcast.5), kind=kOutput, calls=%fused_computation.15 | convolution fusion | flops 2415968256 | bytes 8585728 | tf_op jit(solution)/shard_map/dot_general | solution.py:16
  81.3 37.3 %all-gather.9.cloned.1.call-done = f32[384,4096]{1,0:T(8,128)} async-done(((f32[24,4096]{1,0:T(8,128)}), f32[384,4096]{1,0:T(8,128)}) %all-gather.9.cloned.1.call-update) | async-done | bytes 6291472 | tf_op jit(solution)/shard_map/all_gather | solution.py:34
  118.6 9.3 %fusion.24 = f32[384,128]{0,1:T(8,128)S(1)} fusion(f32[384,4096]{1,0:T(8,128)} %all-gather.9.cloned.1.call-done, f32[4,128,4096]{2,1,0:T(8,128)} %param.7, pred[]{:T(512)} %bitcast.10), kind=kOutput, calls=%fused_computation.16 | convolution fusion | flops 2415968256 | bytes 8585728 | tf_op jit(solution)/shard_map/dot_general | solution.py:16
  127.9 37.3 %all-gather.5.cloned.1.call-done = f32[384,4096]{1,0:T(8,128)} async-done(((f32[24,4096]{1,0:T(8,128)}), f32[384,4096]{1,0:T(8,128)}) %all-gather.5.cloned.1.call-update) | async-done | bytes 6291472 | tf_op jit(solution)/shard_map/all_gather | solution.py:34
  165.1 9.5 %fusion.18 = f32[384,128]{0,1:T(8,128)S(1)} fusion(f32[384,128]{0,1:T(8,128)S(1)} %fusion.24, f32[384,128]{0,1:T(8,128)S(1)} %fusion.21, f32[384,4096]{1,0:T(8,128)} %all-gather.5.cloned.1.call-done, f32[4,128,4096]{2,1,0:T(8,128)} %param.7, pred[]{:T(512)} %bitcast), kind=kOutput, calls=%fused_computation.14 | convolution fusion | flops 2416066560 | bytes 8978944 | tf_op jit(solution)/shard_map/dot_general | solution.py:16
  174.6 0.0 copy-start.4
  174.6 0.0 copy-start.3
  174.7 0.0 copy-start.2
  174.7 36.8 %all-gather.11.cloned.1.call-done = f32[384,4096]{1,0:T(8,128)} async-done(((f32[24,4096]{1,0:T(8,128)}), f32[384,4096]{1,0:T(8,128)}) %all-gather.11.cloned.1.call-update) | async-done | bytes 6291472 | tf_op jit(solution)/shard_map/all_gather | solution.py:34
  211.5 9.9 %fusion.33 = f32[16,8,384]{2,1,0:T(8,128)} fusion(f32[384,128]{0,1:T(8,128)S(1)} %fusion.18, f32[384,4096]{1,0:T(8,128)} %all-gather.11.cloned.1.call-done, f32[4,128,4096]{2,1,0:T(8,128)} %param.7, pred[]{:T(512)} %bitcast.15), kind=kOutput, calls=%fused_computation.19 | convolution fusion | flops 2416017408 | bytes 8782336 | tf_op jit(solution)/shard_map/dot_general | solution.py:16
  221.5 7.3 %all-to-all-start = ((f32[16,8,384]{2,1,0:T(8,128)}), f32[16,8,384]{2,1,0:T(8,128)S(1)}, u32[]{:S(2)}, u32[]{:S(2)}) async-start(f32[16,8,384]{2,1,0:T(8,128)} %fusion.33), calls=%async_computation | async-start | bytes 393216 | tf_op jit(solution)/shard_map/all_to_all | solution.py:41
  228.7 0.0 copy-done.4
  228.8 0.0 copy-done.3
  228.8 0.2 select_reduce_fusion.1
  229.0 6.4 %all-to-all-done = f32[16,8,384]{2,1,0:T(8,128)S(1)} async-done(((f32[16,8,384]{2,1,0:T(8,128)}), f32[16,8,384]{2,1,0:T(8,128)S(1)}, u32[]{:S(2)}, u32[]{:S(2)}) %all-to-all-start) | async-done | bytes 196640 | tf_op jit(solution)/shard_map/all_to_all | solution.py:41
  235.4 0.0 copy-start.1
  235.4 0.0 copy-done.2
  235.4 0.7 subtract_divide_fusion
  236.1 0.0 copy-done.1
  (2 shorter events, 0.0 us)
Async XLA Ops:
  7.2 64.9 %all-gather.7.cloned.1.call-start = ((), (), s32[]{:S(2)}) async-start(), calls=%async_computation.2 | async-start | bytes 6684672 | tf_op jit(solution)/shard_map/all_gather | solution.py:34
  14.1 6.4 %copy-start = (f32[4,24,4096]{2,1,0:T(8,128)S(1)}, f32[4,24,4096]{2,1,0:T(8,128)}, u32[]{:S(2)}) copy-start(f32[4,24,4096]{2,1,0:T(8,128)} %param.8) | copy-start | bytes 4718596
  17.3 7.7 %copy-start.5 = (s32[16]{0:T(128)S(1)}, s32[16]{0:T(128)}, u32[]{:S(2)}) copy-start(s32[16]{0:T(128)} %param.10) | copy-start | bytes 196
  22.9 95.7 %all-gather.9.cloned.1.call-start = ((), (), s32[]{:S(2)}) async-start(), calls=%async_computation.3 | async-start | bytes 6684672 | tf_op jit(solution)/shard_map/all_gather | solution.py:34
  23.7 141.5 %all-gather.5.cloned.1.call-start = ((), (), s32[]{:S(2)}) async-start(), calls=%async_computation.1 | async-start | bytes 6684672 | tf_op jit(solution)/shard_map/all_gather | solution.py:34
  24.4 187.1 %all-gather.11.cloned.1.call-start = ((), (), s32[]{:S(2)}) async-start(), calls=%async_computation.4 | async-start | bytes 6684672 | tf_op jit(solution)/shard_map/all_gather | solution.py:34
  174.6 54.1 %copy-start.4 = (s32[8,2]{0,1:T(2,128)S(1)}, s32[8,2]{0,1:T(2,128)}, u32[]{:S(2)}) copy-start(s32[8,2]{0,1:T(2,128)} %param.11) | copy-start | bytes 196
  174.6 54.1 %copy-start.3 = (f32[200]{0:T(256)S(1)}, f32[200]{0:T(256)}, u32[]{:S(2)}) copy-start(f32[200]{0:T(256)} %param.12) | copy-start | bytes 2404
  174.7 60.7 %copy-start.2 = (f32[384]{0:T(512)S(1)}, f32[384]{0:T(512)}, u32[]{:S(2)}) copy-start(f32[384]{0:T(512)} %param.13) | copy-start | bytes 4612
  221.5 13.9 %all-to-all-start = ((f32[16,8,384]{2,1,0:T(8,128)}), f32[16,8,384]{2,1,0:T(8,128)S(1)}, u32[]{:S(2)}, u32[]{:S(2)}) async-start(f32[16,8,384]{2,1,0:T(8,128)} %fusion.33), calls=%async_computation | async-start | bytes 393216 | tf_op jit(solution)/shard_map/all_to_all | solution.py:41
  235.4 0.7 copy-start.1
Sparse Core Ops, SparseCore 0:
  23.0 48.9 all-gather.6
  73.9 44.6 all-gather.8
  120.4 44.6 all-gather.4
  166.8 44.6 all-gather.10

commit v2 on v1

--- a/solution.py
+++ b/solution.py
@@ -6,10 +6,13 @@
 TILE = 64
 
 
-def symmetric_rows(rows, flag):
+def swap_in_tile(rows):
     shaped = rows.reshape(rows.shape[0], TILE, TILE)
-    swapped = jnp.swapaxes(shaped, 1, 2).reshape(rows.shape)
-    return rows + flag.astype(jnp.float32) * swapped
+    return jnp.swapaxes(shaped, 1, 2).reshape(rows.shape)
+
+
+def symmetric_amps(amp_rows, flag):
+    return amp_rows + flag.astype(jnp.float32) * swap_in_tile(amp_rows)
 
 
 def tile_product(amp_tile, int_rows):
@@ -24,17 +27,49 @@
 
 def on_device(amplitudes, integrals, tile_flags, live_count, pair_occ, occ_energy, ab_energy):
     slots, pair_rows, _ = amplitudes.shape
+    n_virt = lax.axis_size("virt")
+    half = n_virt // 2
     virt_index = lax.axis_index("virt")
-    n_virt = lax.axis_size("virt")
+    partner = (virt_index + half) % n_virt
     own_count = live_count[virt_index]
+    partner_count = live_count[partner]
+    give = jnp.clip((own_count - partner_count) // 2, 0, 1)
+    take = jnp.clip((partner_count - own_count) // 2, 0, 1)
+    keep = own_count - give
+    work = keep + take
+
+    send_at = own_count - 1
+    send_amp = symmetric_amps(
+        lax.dynamic_index_in_dim(amplitudes, send_at, 0, keepdims=False),
+        lax.dynamic_index_in_dim(tile_flags, send_at, 0, keepdims=False),
+    )
+    send_int = lax.dynamic_index_in_dim(integrals, send_at, 0, keepdims=False)
+    perm = [(v, (v + half) % n_virt) for v in range(n_virt)]
+    recv_int = lax.ppermute(send_int, "virt", perm)
+    recv_amp = lax.ppermute(send_amp, "virt", perm)
+
+    def work_rows(slot):
+        own_int = integrals[slot]
+        own_amp = symmetric_amps(amplitudes[slot], tile_flags[slot])
+        if slot == 0:
+            return own_int, own_amp
+        mine = slot < keep
+        return jnp.where(mine, own_int, recv_int), jnp.where(mine, own_amp, recv_amp)
+
+    def slot_term(slot):
+        int_rows, amp_rows = work_rows(slot)
+        gathered = lax.all_gather(int_rows, "pair", axis=0, tiled=True)
+        return tile_product(amp_rows, gathered)
 
     running = None
-    for slot in range(slots):
-        sym_rows = symmetric_rows(integrals[slot], tile_flags[slot])
-        gathered = lax.all_gather(sym_rows, "pair", axis=0, tiled=True)
-        term = tile_product(amplitudes[slot], gathered)
-        term = jnp.where(slot < own_count, term, jnp.zeros_like(term))
+    for slot in range(slots - 1):
+        term = slot_term(slot)
+        term = jnp.where(slot < work, term, jnp.zeros_like(term))
         running = term if running is None else running + term
+    last = slots - 1
+    running = lax.cond(
+        last < work, lambda acc: acc + slot_term(last), lambda acc: acc, running
+    )
 
     ab = running.shape[1]
     blocks = running.reshape(n_virt, pair_rows // n_virt, ab)

time: 244 us -> 187 us (0.77)
  waiting for transfers between devices: 163 us -> 77.2 us
  local copies, waits for them, and re-layouts: 8.98 us -> 29.7 us
  other arithmetic: 5.67 us -> 14.9 us
  matrix products: 37.9 us -> 30.5 us
  starting transfers between devices: 7.61 us -> 12 us
    all_gather x4 -> x3, waiting for transfers between devices: 155 us -> 40.7 us  [slot_term(): gathered = lax.all_gather(int_rows, 'pair', axis=0, tiled=True)]
    ppermute x0 -> x2, waiting for transfers between devices: none -> 29.5 us  [the longest x1 21.3 us: on_device(): recv_amp = lax.ppermute(send_amp, 'virt', perm)]
    unnamed x12 -> x34, local copies, waits for them, and re-layouts: 0.04 us -> 9.86 us
    dot_general x4 -> x3, matrix products: 37.9 us -> 30.5 us  [tile_product(): lax.dot_general(amp_tile, int_rows, (((1,), (1,)), ((), ())), precision=l...]
    slice x1 -> x2, local copies, waits for them, and re-layouts: 1.41 us -> 7.76 us  [work_rows(): own_amp = symmetric_amps(amplitudes[slot], tile_flags[slot])]
    select_n x0 -> x2, other arithmetic: none -> 5.82 us  [the longest x1 4.85 us: work_rows(): jnp.where(mine, own_amp, recv_amp)]
    ppermute x0 -> x2, starting transfers between devices: none -> 4.45 us  [the longest x1 2.27 us: on_device(): recv_int = lax.ppermute(send_int, 'virt', perm)]
    add x1 -> x2, other arithmetic: 2.36 us -> 4.97 us  [symmetric_amps(): return amp_rows + flag.astype(jnp.float32) * swap_in_tile(amp_rows)]
  transfers between devices with their start and end apart: 5 -> 6, of which waited for: 5 -> 5; matrix products, arithmetic and copies ran while one was open for 12% -> 32% of each run, Pallas kernels for 0% -> 0%
where the time goes in v2:
time: 187 us; the launch traced here: 185 us
  waiting for transfers between devices  77.2 us (41%)
  matrix products  30.5 us (16%)
  local copies, waits for them, and re-layouts  29.7 us (16%)
  between operations  21.1 us (11%)
  other arithmetic  14.9 us (8%)
  starting transfers between devices  12 us (6%)
    all_gather x3, waiting for transfers between devices, slot_term(): gathered = lax.all_gather(int_rows, 'pair', axis=0, tiled=True)  40.7 us
    dot_general x3, matrix products, tile_product(): lax.dot_general(amp_tile, int_rows, (((1,), (1,)), ((), ())), precision=l...  30.5 us
    ppermute x1, waiting for transfers between devices, on_device(): recv_amp = lax.ppermute(send_amp, 'virt', perm)  21.3 us
    unnamed x34, local copies, waits for them, and re-layouts  9.86 us
    mul x4, local copies, waits for them, and re-layouts, symmetric_amps(): return amp_rows + flag.astype(jnp.float32) * swap_in_tile(amp_rows)  8.8 us
    ppermute x1, waiting for transfers between devices, on_device(): recv_int = lax.ppermute(send_int, 'virt', perm)  8.21 us
    slice x2, local copies, waits for them, and re-layouts, work_rows(): own_amp = symmetric_amps(amplitudes[slot], tile_flags[slot])  7.76 us
    all_to_all x1, starting transfers between devices, on_device(): received = lax.all_to_all(blocks, 'virt', 0, 0, tiled=False)  7.39 us
  transfers between devices with their start and end apart: 6, of which 5 were waited for; matrix products, arithmetic and copies ran while one was open for 32% of the time, Pallas kernels for 0%

profile of v2, /device:TPU:2, one launch (start us, length us, event | category | flops | bytes accessed | tf_op | source)
XLA Modules:
  0.0 185.4 jit_solution(17793083856472654558)
XLA Ops:
  7.2 0.0 copy-start.9
  7.2 0.0 all-gather.12.cloned.1.call-start
  7.2 1.4 fusion.12
  9.9 1.9 %dynamic-slice_bitcast_fusion = (f32[24,4096]{1,0:T(8,128)S(1)}, f32[1,24,4096]{2,1,0:T(8,128)}) fusion(f32[4,24,4096]{2,1,0:T(8,128)} %param.10, s32[]{:T(128)S(6)} %select_n.104), kind=kLoop, calls=%fused_computation.24 | loop fusion | bytes 1572868 | tf_op jit(solution)/shard_map/jit(dynamic_index_in_dim)/squeeze | solution.py:46
  11.8 0.0 all-gather.12.cloned.1.call-update
  11.9 0.0 all-gather.8.cloned.1.call-start
  11.9 2.3 %collective-permute-start.1 = (f32[24,4096]{1,0:T(8,128)S(1)}, f32[24,4096]{1,0:T(8,128)S(1)}, u32[]{:S(2)}, u32[]{:S(2)}) collective-permute-start(f32[24,4096]{1,0:T(8,128)S(1)} %get-tuple-element.51), channel_id=1, source_target_pairs={{0,8},{1,9},{2,10},{3,11},{4,12},{5,13},{6,14},{7,15},{8,0},{9,1},... | collective-permute-start | bytes 1179656 | tf_op jit(solution)/shard_map/ppermute | solution.py:48
  16.2 8.2 %collective-permute-done.1 = f32[24,4096]{1,0:T(8,128)S(1)} collective-permute-done((f32[24,4096]{1,0:T(8,128)S(1)}, f32[24,4096]{1,0:T(8,128)S(1)}, u32[]{:S(2)}, u32[]{:S(2)}) %collective-permute-start.1) | collective-permute-done | bytes 393248 | tf_op jit(solution)/shard_map/ppermute | solution.py:48
  24.4 0.0 copy-done.9
  24.4 1.0 bitcast_select_fusion.1
  25.3 0.0 all-gather.8.cloned.1.call-update
  25.4 0.0 all-gather.10.cloned.1.call-start
  25.4 0.7 all-gather.10.cloned.1.call-update
  26.1 7.1 %fusion.10 = (f32[1,128,4096]{2,1,0:T(8,128)}, f32[1,128,4096]{2,1,0:T(8,128)}, f32[1,128,4096]{2,1,0:T(8,128)}, f32[1,128,4096]{2,1,0:T(8,128)}) fusion(f32[4,128,4096]{2,1,0:T(8,128)} %param.9, s32[]{:T(128)S(6)} %select_n.104), kind=kLoop, calls=%fused_computation.33 | loop fusion | bytes 16777220 | tf_op jit(solution)/shard_map/slice | solution.py:53
  33.2 0.0 copy-start.11
  33.2 1.9 %copy.36 = f32[1,128,4096]{1,2,0:T(8,128)S(1)} copy(f32[1,128,4096]{2,1,0:T(8,128)} %get-tuple-element.44) | data formatting | bytes 4194304
  35.1 0.0 copy-done.11
  35.2 0.7 fusion.11
  36.5 0.1 broadcast_multiply_fusion.1
  36.6 1.2 copy.30
  37.8 1.7 bitcast_add_fusion.2
  39.5 2.2 %collective-permute-start = (f32[128,4096]{0,1:T(8,128)}, f32[128,4096]{0,1:T(8,128)}, u32[]{:S(2)}, u32[]{:S(2)}) collective-permute-start(f32[128,4096]{0,1:T(8,128)} %bitcast_add_fusion.2), channel_id=1, source_target_pairs={{0,8},{1,9},{2,10},{3,11},{4,12},{5,13},{6,14},{7,15},{8,0},{9,1},... | collective-permute-start | bytes 6291464 | tf_op jit(solution)/shard_map/ppermute | solution.py:49
  41.7 1.9 %copy.35 = f32[1,128,4096]{1,2,0:T(8,128)S(1)} copy(f32[1,128,4096]{2,1,0:T(8,128)} %get-tuple-element.45) | data formatting | bytes 4194304
  43.6 0.0 copy-start
  44.2 3.1 %copy.37 = f32[1,128,4096]{1,2,0:T(8,128)} copy(f32[1,128,4096]{2,1,0:T(8,128)} %get-tuple-element.43) | data formatting | bytes 4194304
  48.0 0.0 copy-done
  48.0 0.0 copy-start.2
  48.0 1.5 broadcast_multiply_fusion.2
  49.5 0.9 copy-done.2
  50.4 0.0 copy-start.4
  50.4 1.4 broadcast_multiply_fusion
  53.1 0.0 copy-done.4
  53.2 0.0 copy-start.5
  53.2 2.5 %copy.28 = f32[128,64,64]{0,2,1:T(8,128)} copy(f32[128,64,64]{0,1,2:T(8,128)S(1)} %bitcast.73) | data formatting | bytes 4194304 | tf_op jit(solution)/shard_map/mul | solution.py:15
  55.7 0.0 copy-done.5
  55.7 2.5 %copy.32 = f32[128,64,64]{0,2,1:T(8,128)} copy(f32[128,64,64]{0,1,2:T(8,128)S(1)} %bitcast.74) | data formatting | bytes 4194304 | tf_op jit(solution)/shard_map/mul | solution.py:15
  58.2 1.9 %copy.34 = f32[1,128,4096]{1,2,0:T(8,128)S(1)} copy(f32[1,128,4096]{2,1,0:T(8,128)} %get-tuple-element.46) | data formatting | bytes 4194304
  60.8 0.1 broadcast_multiply_fusion.3
  60.9 2.5 %copy.26 = f32[128,64,64]{0,2,1:T(8,128)} copy(f32[128,64,64]{0,1,2:T(8,128)S(1)} %bitcast.76) | data formatting | bytes 4194304 | tf_op jit(solution)/shard_map/mul | solution.py:15
  63.5 0.0 copy-start.1
  63.5 0.0 copy-start.3
  63.5 0.0 copy-start.8
  63.5 3.3 %bitcast_add_fusion.4 = f32[128,4096]{0,1:T(8,128)} fusion(f32[128,64,64]{0,2,1:T(8,128)} %copy.26, f32[1,128,4096]{1,2,0:T(8,128)S(1)} %copy.34), kind=kLoop, calls=%fused_computation.12 | loop fusion | flops 524288 | bytes 6291456 | tf_op jit(solution)/shard_map/add | solution.py:15
  66.8 21.3 %collective-permute-done = f32[128,4096]{0,1:T(8,128)} collective-permute-done((f32[128,4096]{0,1:T(8,128)}, f32[128,4096]{0,1:T(8,128)}, u32[]{:S(2)}, u32[]{:S(2)}) %collective-permute-start) | collective-permute-done | bytes 2097184 | tf_op jit(solution)/shard_map/ppermute | solution.py:49
  88.1 0.0 copy-done.1
  88.1 0.0 copy-done.3
  88.1 0.0 copy-done.8
  88.1 4.9 %fusion.3 = (f32[128,4096]{0,1:T(8,128)}, f32[128,4096]{0,1:T(8,128)}) fusion(f32[128,4096]{0,1:T(8,128)} %collective-permute-done, f32[128,64,64]{0,2,1:T(8,128)} %copy.32, f32[1,128,4096]{1,2,0:T(8,128)S(1)} %copy-done.3, pred[]{:T(512)S(6)} %gt.26, f32[128,64,64]{0,2,1:T(8,128)S(1)} %copy-done.8, f32[1,128,4096]{1,2,0:T(8,128)S(1)} %copy-done.1, pred[]{:T(512)S(6)} %gt.24), kind=kLoop, calls=%fused_computation.8 | loop fusion | flops 2097152 | bytes 14680066 | tf_op jit(solution)/shard_map/jit(_where)/select_n | solution.py:57
  92.9 0.0 copy-done.6
  92.9 9.7 %fusion.5 = f32[128,384]{1,0:T(8,128)S(1)} fusion(f32[128,4096]{0,1:T(8,128)S(1)} %copy-done.6, f32[1,384,4096]{2,1,0:T(8,128)} %all-gather.12.cloned.1.call-done, pred[]{:T(512)S(6)} %gt.22), kind=kOutput, calls=%fused_computation.13 | convolution fusion | flops 2415968256 | bytes 8585217 | tf_op jit(solution)/shard_map/dot_general | solution.py:19
  102.6 5.0 %all-gather.8.cloned.1.call-done = f32[384,4096]{1,0:T(8,128)} async-done(((f32[24,4096]{1,0:T(8,128)}), f32[384,4096]{1,0:T(8,128)}) %all-gather.8.cloned.1.call-update) | async-done | bytes 6291472 | tf_op jit(solution)/shard_map/all_gather | solution.py:61
  107.5 10.8 %fusion.9 = f32[128,384]{1,0:T(8,128)S(1)} fusion(f32[128,384]{1,0:T(8,128)S(1)} %fusion.5, f32[128,4096]{0,1:T(8,128)} %get-tuple-element.48, f32[384,4096]{1,0:T(8,128)} %all-gather.8.cloned.1.call-done, pred[]{:T(512)S(6)} %gt.23), kind=kOutput, calls=%fused_computation.17 | convolution fusion | flops 2416017408 | bytes 8781825 | tf_op jit(solution)/shard_map/dot_general | solution.py:19
  118.4 35.7 %all-gather.10.cloned.1.call-done = f32[384,4096]{1,0:T(8,128)} async-done(((f32[24,4096]{1,0:T(8,128)}), f32[384,4096]{1,0:T(8,128)}) %all-gather.10.cloned.1.call-update) | async-done | bytes 6291472 | tf_op jit(solution)/shard_map/all_gather | solution.py:61
  154.1 0.0 copy-done.7
  154.1 10.0 %fusion.8 = f32[128,384]{1,0:T(8,128)} fusion(f32[128,384]{1,0:T(8,128)S(1)} %fusion.9, f32[128,4096]{0,1:T(8,128)S(1)} %copy-done.7, f32[384,4096]{1,0:T(8,128)} %all-gather.10.cloned.1.call-done, pred[]{:T(512)S(6)} %gt.25), kind=kOutput, calls=%fused_computation.15 | convolution fusion | flops 2416017408 | bytes 8781825 | tf_op jit(solution)/shard_map/dot_general | solution.py:19
  164.2 7.4 %all-to-all-start = ((f32[16,8,384]{2,1,0:T(8,128)}), f32[16,8,384]{2,1,0:T(8,128)S(1)}, u32[]{:S(2)}, u32[]{:S(2)}) async-start(f32[16,8,384]{2,1,0:T(8,128)} %bitcast.32), calls=%async_computation | async-start | bytes 393216 | tf_op jit(solution)/shard_map/all_to_all | solution.py:76
  171.5 0.0 copy-done.14
  171.6 0.0 copy-done.13
  171.6 0.2 select_reduce_fusion.1
  171.8 6.4 %all-to-all-done = f32[16,8,384]{2,1,0:T(8,128)S(1)} async-done(((f32[16,8,384]{2,1,0:T(8,128)}), f32[16,8,384]{2,1,0:T(8,128)S(1)}, u32[]{:S(2)}, u32[]{:S(2)}) %all-to-all-start) | async-done | bytes 196640 | tf_op jit(solution)/shard_map/all_to_all | solution.py:76
  178.2 0.0 copy-start.10
  178.2 0.0 copy-done.12
  178.2 0.7 subtract_divide_fusion
  178.9 0.0 copy-done.10
  (9 shorter events, 0.0 us)
Async XLA Ops:
  7.2 17.2 %copy-start.9 = (f32[4,24,4096]{2,1,0:T(8,128)S(1)}, f32[4,24,4096]{2,1,0:T(8,128)}, u32[]{:S(2)}) copy-start(f32[4,24,4096]{2,1,0:T(8,128)} %param.10) | copy-start | bytes 4718596
  7.2 85.7 %all-gather.12.cloned.1.call-start = ((), (), s32[]{:S(2)}) async-start(), calls=%async_computation.4 | async-start | bytes 6684672 | tf_op jit(solution)/shard_map/all_gather | solution.py:61
  11.9 95.7 %all-gather.8.cloned.1.call-start = ((), (), s32[]{:S(2)}) async-start(), calls=%async_computation.2 | async-start | bytes 6684672 | tf_op jit(solution)/shard_map/all_gather | solution.py:61
  11.9 12.4 %collective-permute-start.1 = (f32[24,4096]{1,0:T(8,128)S(1)}, f32[24,4096]{1,0:T(8,128)S(1)}, u32[]{:S(2)}, u32[]{:S(2)}) collective-permute-start(f32[24,4096]{1,0:T(8,128)S(1)} %get-tuple-element.51), channel_id=1, source_target_pairs={{0,8},{1,9},{2,10},{3,11},{4,12},{5,13},{6,14},{7,15},{8,0},{9,1},... | collective-permute-start | bytes 1179656 | tf_op jit(solution)/shard_map/ppermute | solution.py:48
  25.4 128.7 %all-gather.10.cloned.1.call-start = ((), (), s32[]{:S(2)}) async-start(), calls=%async_computation.3 | async-start | bytes 6684672 | tf_op jit(solution)/shard_map/all_gather | solution.py:61
  33.2 2.0 %copy-start.11 = (s32[4]{0:T(128)S(1)}, s32[4]{0:T(128)}, u32[]{:S(2)}) copy-start(s32[4]{0:T(128)} %param.11) | copy-start | bytes 52
  39.5 48.6 %collective-permute-start = (f32[128,4096]{0,1:T(8,128)}, f32[128,4096]{0,1:T(8,128)}, u32[]{:S(2)}, u32[]{:S(2)}) collective-permute-start(f32[128,4096]{0,1:T(8,128)} %bitcast_add_fusion.2), channel_id=1, source_target_pairs={{0,8},{1,9},{2,10},{3,11},{4,12},{5,13},{6,14},{7,15},{8,0},{9,1},... | collective-permute-start | bytes 6291464 | tf_op jit(solution)/shard_map/ppermute | solution.py:49
  43.6 4.4 %copy-start = (f32[1,128,4096]{1,2,0:T(8,128)}, f32[1,128,4096]{1,2,0:T(8,128)S(1)}, u32[]{:S(2)}) copy-start(f32[1,128,4096]{1,2,0:T(8,128)S(1)} %copy.35) | copy-start | bytes 6291460
  48.0 2.4 %copy-start.2 = (f32[1,128,4096]{1,2,0:T(8,128)S(1)}, f32[1,128,4096]{1,2,0:T(8,128)}, u32[]{:S(2)}) copy-start(f32[1,128,4096]{1,2,0:T(8,128)} %copy.37) | copy-start | bytes 6291460
  50.4 2.8 %copy-start.4 = (f32[1,128,4096]{1,2,0:T(8,128)S(1)}, f32[1,128,4096]{1,2,0:T(8,128)}, u32[]{:S(2)}) copy-start(f32[1,128,4096]{1,2,0:T(8,128)} %broadcast_multiply_fusion.2) | copy-start | bytes 6291460
  53.2 2.6 %copy-start.5 = (f32[1,128,4096]{1,2,0:T(8,128)S(1)}, f32[1,128,4096]{1,2,0:T(8,128)}, u32[]{:S(2)}) copy-start(f32[1,128,4096]{1,2,0:T(8,128)} %broadcast_multiply_fusion) | copy-start | bytes 6291460
  63.5 24.6 %copy-start.1 = (f32[1,128,4096]{1,2,0:T(8,128)S(1)}, f32[1,128,4096]{1,2,0:T(8,128)}, u32[]{:S(2)}) copy-start(f32[1,128,4096]{1,2,0:T(8,128)} %copy-done) | copy-start | bytes 6291460
  63.5 24.6 %copy-start.3 = (f32[1,128,4096]{1,2,0:T(8,128)S(1)}, f32[1,128,4096]{1,2,0:T(8,128)}, u32[]{:S(2)}) copy-start(f32[1,128,4096]{1,2,0:T(8,128)} %copy.37) | copy-start | bytes 6291460
  63.5 24.6 %copy-start.8 = (f32[128,64,64]{0,2,1:T(8,128)S(1)}, f32[128,64,64]{0,2,1:T(8,128)}, u32[]{:S(2)}) copy-start(f32[128,64,64]{0,2,1:T(8,128)} %copy.28) | copy-start | bytes 6291460
  66.8 26.1 %copy-start.6 = (f32[128,4096]{0,1:T(8,128)S(1)}, f32[128,4096]{0,1:T(8,128)}, u32[]{:S(2)}) copy-start(f32[128,4096]{0,1:T(8,128)} %bitcast_add_fusion.4) | copy-start | bytes 6291460
  107.5 46.6 %copy-start.7 = (f32[128,4096]{0,1:T(8,128)S(1)}, f32[128,4096]{0,1:T(8,128)}, u32[]{:S(2)}) copy-start(f32[128,4096]{0,1:T(8,128)} %get-tuple-element.47) | copy-start | bytes 6291460
  164.1 7.4 %copy-start.14 = (s32[8,2]{0,1:T(2,128)S(1)}, s32[8,2]{0,1:T(2,128)}, u32[]{:S(2)}) copy-start(s32[8,2]{0,1:T(2,128)} %param.13) | copy-start | bytes 196
  164.1 7.4 %copy-start.13 = (f32[200]{0:T(256)S(1)}, f32[200]{0:T(256)}, u32[]{:S(2)}) copy-start(f32[200]{0:T(256)} %param.14) | copy-start | bytes 2404
  164.1 14.1 %copy-start.12 = (f32[384]{0:T(512)S(1)}, f32[384]{0:T(512)}, u32[]{:S(2)}) copy-start(f32[384]{0:T(512)} %param.15) | copy-start | bytes 4612
  164.2 14.0 %all-to-all-start = ((f32[16,8,384]{2,1,0:T(8,128)}), f32[16,8,384]{2,1,0:T(8,128)S(1)}, u32[]{:S(2)}, u32[]{:S(2)}) async-start(f32[16,8,384]{2,1,0:T(8,128)} %bitcast.32), calls=%async_computation | async-start | bytes 393216 | tf_op jit(solution)/shard_map/all_to_all | solution.py:76
  178.2 0.7 copy-start.10
Sparse Core Ops, SparseCore 0:
  12.0 48.9 all-gather.11
  62.8 44.6 all-gather.7
  109.4 44.6 all-gather.9

commit v3 on v2

--- a/solution.py
+++ b/solution.py
@@ -20,7 +20,7 @@
         amp_tile,
         int_rows,
         (((1,), (1,)), ((), ())),
-        precision=lax.Precision.HIGHEST,
+        precision=lax.Precision.HIGH,
         preferred_element_type=jnp.float32,
     )
 
@@ -36,7 +36,6 @@
     give = jnp.clip((own_count - partner_count) // 2, 0, 1)
     take = jnp.clip((partner_count - own_count) // 2, 0, 1)
     keep = own_count - give
-    work = keep + take
 
     send_at = own_count - 1
     send_amp = symmetric_amps(
@@ -48,28 +47,30 @@
     recv_int = lax.ppermute(send_int, "virt", perm)
     recv_amp = lax.ppermute(send_amp, "virt", perm)
 
-    def work_rows(slot):
-        own_int = integrals[slot]
-        own_amp = symmetric_amps(amplitudes[slot], tile_flags[slot])
-        if slot == 0:
-            return own_int, own_amp
-        mine = slot < keep
-        return jnp.where(mine, own_int, recv_int), jnp.where(mine, own_amp, recv_amp)
+    def own_amps(slot):
+        return symmetric_amps(amplitudes[slot], tile_flags[slot])
 
-    def slot_term(slot):
-        int_rows, amp_rows = work_rows(slot)
-        gathered = lax.all_gather(int_rows, "pair", axis=0, tiled=True)
-        return tile_product(amp_rows, gathered)
+    first_two = lax.all_gather(integrals[0:2], "pair", axis=1, tiled=True)
+    running = tile_product(own_amps(0), first_two[0])
+    second = tile_product(own_amps(1), first_two[1])
+    running = running + jnp.where(keep > 1, second, jnp.zeros_like(second))
 
-    running = None
-    for slot in range(slots - 1):
-        term = slot_term(slot)
-        term = jnp.where(slot < work, term, jnp.zeros_like(term))
-        running = term if running is None else running + term
-    last = slots - 1
-    running = lax.cond(
-        last < work, lambda acc: acc + slot_term(last), lambda acc: acc, running
-    )
+    third_int = jnp.where(take > 0, recv_int, integrals[2])
+    third_amp = jnp.where(take > 0, recv_amp, own_amps(2))
+    third = tile_product(third_amp, lax.all_gather(third_int, "pair", axis=0, tiled=True))
+    third_live = (take > 0) | (keep > 2)
+    running = running + jnp.where(third_live, third, jnp.zeros_like(third))
+
+    def fourth(acc):
+        gathered = lax.all_gather(integrals[3], "pair", axis=0, tiled=True)
+        return acc + tile_product(own_amps(3), gathered)
+
+    all_counts = live_count
+    all_partners = jnp.roll(live_count, half)
+    all_keep = all_counts - jnp.clip((all_counts - all_partners) // 2, 0, 1)
+    any_full = jnp.max(all_keep) > 3
+    with_fourth = lax.cond(any_full, fourth, lambda acc: acc, running)
+    running = jnp.where(keep > 3, with_fourth, running)
 
     ab = running.shape[1]
     blocks = running.reshape(n_virt, pair_rows // n_virt, ab)

time: 187 us -> 166 us (0.89)
  waiting for transfers between devices: 77.2 us -> 65.7 us
  matrix products: 30.5 us -> 21 us
    all_gather x3 -> x2, waiting for transfers between devices: 40.7 us -> 31 us  [the longest x1 31 us: on_device(): lax.all_gather(third_int, 'pair', axis=0, tiled=True)]
    dot_general x3, matrix products: 30.5 us -> 21 us  [tile_product(): lax.dot_general(amp_tile, int_rows, (((1,), (1,)), ((), ())), precision=l...]
    slice x2 -> x4, local copies, waits for them, and re-layouts: 7.76 us -> 10.1 us  [the longest x2 7.83 us: own_amps(): return symmetric_amps(amplitudes[slot], tile_flags[slot])]
    squeeze x1, local copies, waits for them, and re-layouts: 1.93 us -> 0.03 us  [on_device(): send_int = lax.dynamic_index_in_dim(integrals, send_at, 0, keepdims=False)]
    add x2 -> x3, other arithmetic: 4.97 us -> 6.56 us  [symmetric_amps(): return amp_rows + flag.astype(jnp.float32) * swap_in_tile(amp_rows)]
    unnamed x34 -> x30, local copies, waits for them, and re-layouts: 9.86 us -> 9.27 us
  transfers between devices with their start and end apart: 6 -> 5, of which waited for: 5 -> 4; matrix products, arithmetic and copies ran while one was open for 32% -> 33% of each run, Pallas kernels for 0% -> 0%
where the time goes in v3:
time: 166 us; the launch traced here: 164 us
  waiting for transfers between devices  65.7 us (40%)
  local copies, waits for them, and re-layouts  28.8 us (17%)
  between operations  22 us (13%)
  matrix products  21 us (13%)
  other arithmetic  15.1 us (9%)
  starting transfers between devices  11.7 us (7%)
    all_gather x1, waiting for transfers between devices, on_device(): lax.all_gather(third_int, 'pair', axis=0, tiled=True)  31 us
    dot_general x3, matrix products, tile_product(): lax.dot_general(amp_tile, int_rows, (((1,), (1,)), ((), ())), precision=l...  21 us
    ppermute x1, waiting for transfers between devices, on_device(): recv_amp = lax.ppermute(send_amp, 'virt', perm)  19.4 us
    unnamed x30, local copies, waits for them, and re-layouts  9.27 us
    ppermute x1, waiting for transfers between devices, on_device(): recv_int = lax.ppermute(send_int, 'virt', perm)  8.91 us
    mul x4, local copies, waits for them, and re-layouts, symmetric_amps(): return amp_rows + flag.astype(jnp.float32) * swap_in_tile(amp_rows)  8.8 us
    slice x2, local copies, waits for them, and re-layouts, own_amps(): return symmetric_amps(amplitudes[slot], tile_flags[slot])  7.83 us
    all_to_all x1, starting transfers between devices, on_device(): received = lax.all_to_all(blocks, 'virt', 0, 0, tiled=False)  7.27 us
  transfers between devices with their start and end apart: 5, of which 4 were waited for; matrix products, arithmetic and copies ran while one was open for 33% of the time, Pallas kernels for 0%

profile of v3, /device:TPU:2, one launch (start us, length us, event | category | flops | bytes accessed | tf_op | source)
XLA Modules:
  0.0 164.4 jit_solution(11622423658392301078)
XLA Ops:
  7.2 0.0 copy-start.6
  7.2 0.0 copy-start.8
  7.2 0.0 all-gather.7.cloned.1.call-start
  7.2 2.2 %slice.57 = f32[2,24,4096]{2,1,0:T(8,128)} slice(f32[4,24,4096]{2,1,0:T(8,128)} %param.10), slice={[0:2], [0:24], [0:4096]} | slice | bytes 1572864 | tf_op jit(solution)/shard_map/slice | solution.py:53
  9.4 0.0 all-gather.7.cloned.1.call-update
  9.4 0.0 all-gather.9.cloned.1.call-start
  9.5 0.0 copy-done.8
  9.5 0.6 fusion.19
  11.4 0.0 copy-done.6
  11.5 2.2 %collective-permute-start.1 = (f32[24,4096]{1,0:T(8,128)S(1)}, f32[24,4096]{1,0:T(8,128)S(1)}, u32[]{:S(2)}, u32[]{:S(2)}) collective-permute-start(f32[24,4096]{1,0:T(8,128)S(1)} %dynamic-slice_bitcast_fusion), channel_id=1, source_target_pairs={{0,8},{1,9},{2,10},{3,11},{4,12},{5,13},{6,14},{7,15},{8,0},{9,1},... | collective-permute-start | bytes 1179656 | tf_op jit(solution)/shard_map/ppermute | solution.py:47
  15.0 8.9 %collective-permute-done.1 = f32[24,4096]{1,0:T(8,128)S(1)} collective-permute-done((f32[24,4096]{1,0:T(8,128)S(1)}, f32[24,4096]{1,0:T(8,128)S(1)}, u32[]{:S(2)}, u32[]{:S(2)}) %collective-permute-start.1) | collective-permute-done | bytes 393248 | tf_op jit(solution)/shard_map/ppermute | solution.py:47
  23.9 0.8 bitcast_select_fusion
  24.7 0.0 all-gather.9.cloned.1.call-update
  24.7 7.2 %fusion.17 = (f32[1,128,4096]{2,1,0:T(8,128)}, f32[1,128,4096]{2,1,0:T(8,128)}, f32[1,128,4096]{2,1,0:T(8,128)}, f32[1,128,4096]{2,1,0:T(8,128)}) fusion(f32[4,128,4096]{2,1,0:T(8,128)} %param.9, s32[]{:T(128)S(6)} %select_n.87), kind=kLoop, calls=%fused_computation.41 | loop fusion | bytes 16777220 | tf_op jit(solution)/shard_map/slice | solution.py:51
  31.9 0.0 copy-start.9
  31.9 1.9 %copy.36 = f32[1,128,4096]{1,2,0:T(8,128)S(1)} copy(f32[1,128,4096]{2,1,0:T(8,128)} %get-tuple-element.29) | data formatting | bytes 4194304
  33.8 0.0 copy-done.9
  33.8 0.7 fusion.18
  35.1 0.1 broadcast_multiply_fusion.1
  35.3 1.2 copy.30
  36.5 1.6 bitcast_add_fusion.2
  38.1 2.1 %collective-permute-start = (f32[128,4096]{0,1:T(8,128)}, f32[128,4096]{0,1:T(8,128)}, u32[]{:S(2)}, u32[]{:S(2)}) collective-permute-start(f32[128,4096]{0,1:T(8,128)} %bitcast_add_fusion.2), channel_id=1, source_target_pairs={{0,8},{1,9},{2,10},{3,11},{4,12},{5,13},{6,14},{7,15},{8,0},{9,1},... | collective-permute-start | bytes 6291464 | tf_op jit(solution)/shard_map/ppermute | solution.py:48
  42.2 1.9 %copy.37 = f32[1,128,4096]{1,2,0:T(8,128)S(1)} copy(f32[1,128,4096]{2,1,0:T(8,128)} %get-tuple-element.28) | data formatting | bytes 4194304
  44.2 0.0 copy-start.1
  44.8 0.1 broadcast_multiply_fusion
  45.0 0.5 copy-done.1
  45.5 2.5 %copy.32 = f32[128,64,64]{0,2,1:T(8,128)} copy(f32[128,64,64]{0,1,2:T(8,128)S(1)} %bitcast.79) | data formatting | bytes 4194304 | tf_op jit(solution)/shard_map/mul | solution.py:15
  48.0 1.9 %copy.34 = f32[1,128,4096]{1,2,0:T(8,128)S(1)} copy(f32[1,128,4096]{2,1,0:T(8,128)} %get-tuple-element.31) | data formatting | bytes 4194304
  50.6 0.1 broadcast_multiply_fusion.3
  50.7 2.5 %copy.26 = f32[128,64,64]{0,2,1:T(8,128)} copy(f32[128,64,64]{0,1,2:T(8,128)S(1)} %bitcast.80) | data formatting | bytes 4194304 | tf_op jit(solution)/shard_map/mul | solution.py:15
  53.2 2.9 %copy.35 = f32[1,128,4096]{1,2,0:T(8,128)} copy(f32[1,128,4096]{2,1,0:T(8,128)} %get-tuple-element.30) | data formatting | bytes 4194304
  56.7 1.7 %broadcast_multiply_fusion.2 = f32[1,128,4096]{1,2,0:T(8,128)S(1)} fusion(f32[1,128,4096]{1,2,0:T(8,128)} %copy.35, f32[]{:T(128)} %bitcast.14), kind=kLoop, calls=%fused_computation.22 | loop fusion | flops 524288 | bytes 4194308 | tf_op jit(solution)/shard_map/mul | solution.py:15
  58.5 2.5 %copy.28 = f32[128,64,64]{0,2,1:T(8,128)} copy(f32[128,64,64]{0,1,2:T(8,128)S(1)} %bitcast.81) | data formatting | bytes 4194304 | tf_op jit(solution)/shard_map/mul | solution.py:15
  61.0 0.1 fusion.20
  61.1 0.7 subtract_reduce_fusion
  62.4 0.0 copy-start
  62.4 0.0 copy-start.3
  62.5 3.3 %bitcast_add_fusion.4 = f32[1,128,4096]{1,2,0:T(8,128)} fusion(f32[1,128,4096]{1,2,0:T(8,128)S(1)} %copy.34, f32[128,64,64]{0,2,1:T(8,128)} %copy.26), kind=kLoop, calls=%fused_computation.15 | loop fusion | flops 524288 | bytes 6291456 | tf_op jit(solution)/shard_map/add | solution.py:15
  65.8 0.0 copy-done
  65.8 0.0 copy-done.3
  65.8 0.0 copy-start.2
  65.8 1.6 bitcast_add_fusion.3
  67.4 19.4 %collective-permute-done = f32[128,4096]{0,1:T(8,128)} collective-permute-done((f32[128,4096]{0,1:T(8,128)}, f32[128,4096]{0,1:T(8,128)}, u32[]{:S(2)}, u32[]{:S(2)}) %collective-permute-start) | collective-permute-done | bytes 2097184 | tf_op jit(solution)/shard_map/ppermute | solution.py:48
  86.8 0.0 copy-done.2
  86.8 0.0 copy-done.5
  86.8 3.3 %fusion.7 = f32[128,4096]{0,1:T(8,128)} fusion(f32[128,4096]{0,1:T(8,128)} %collective-permute-done, f32[128,64,64]{0,2,1:T(8,128)S(1)} %copy-done.5, f32[1,128,4096]{1,2,0:T(8,128)S(1)} %copy-done.2, pred[]{:T(512)S(6)} %gt.20), kind=kLoop, calls=%fused_computation.10 | loop fusion | flops 1048576 | bytes 8388609 | tf_op jit(solution)/shard_map/jit(_where)/select_n | solution.py:59
  90.1 7.2 %fusion.13 = f32[128,384]{1,0:T(8,128)S(1)} fusion(f32[2,384,4096]{2,1,0:T(8,128)} %all-gather.7.cloned.1.call-done, f32[1,128,4096]{1,2,0:T(8,128)} %bitcast_add_fusion.3, pred[]{:T(512)S(6)} %gt.19), kind=kOutput, calls=%fused_computation.17 | convolution fusion | flops 1208008704 | bytes 8585217 | tf_op jit(solution)/shard_map/dot_general | solution.py:19
  97.3 0.0 copy-done.4
  97.3 6.5 %fusion.10 = f32[128,384]{1,0:T(8,128)S(1)} fusion(f32[128,384]{1,0:T(8,128)S(1)} %fusion.13, f32[2,384,4096]{2,1,0:T(8,128)} %all-gather.7.cloned.1.call-done, f32[1,128,4096]{1,2,0:T(8,128)S(1)} %copy-done.4), kind=kOutput, calls=%fused_computation.16 | convolution fusion | flops 1208008704 | bytes 8781824 | tf_op jit(solution)/shard_map/dot_general | solution.py:19
  103.9 31.0 %all-gather.9.cloned.1.call-done = f32[384,4096]{1,0:T(8,128)} async-done(((f32[24,4096]{1,0:T(8,128)}), f32[384,4096]{1,0:T(8,128)}) %all-gather.9.cloned.1.call-update) | async-done | bytes 6291472 | tf_op jit(solution)/shard_map/all_gather | solution.py:60
  134.9 7.3 %fusion.16 = f32[128,384]{1,0:T(8,128)S(1)} fusion(f32[128,384]{1,0:T(8,128)S(1)} %fusion.10, f32[128,4096]{0,1:T(8,128)} %fusion.7, f32[384,4096]{1,0:T(8,128)} %all-gather.9.cloned.1.call-done, pred[]{:T(512)S(6)} %or.3), kind=kOutput, calls=%fused_computation.19 | convolution fusion | flops 1208057856 | bytes 8781825 | tf_op jit(solution)/shard_map/dot_general | solution.py:19
  142.1 0.0 copy-start.12
  142.2 0.0 copy-start.11
  142.2 0.0 copy-start.10
  142.2 0.7 select_bitcast_fusion
  142.9 7.3 %all-to-all-start = ((f32[16,8,384]{2,1,0:T(8,128)}), f32[16,8,384]{2,1,0:T(8,128)S(1)}, u32[]{:S(2)}, u32[]{:S(2)}) async-start(f32[16,8,384]{2,1,0:T(8,128)} %select_bitcast_fusion), calls=%async_computation | async-start | bytes 393216 | tf_op jit(solution)/shard_map/all_to_all | solution.py:77
  150.2 0.0 copy-done.12
  150.2 0.0 copy-done.11
  150.2 0.2 select_reduce_fusion.1
  150.4 6.4 %all-to-all-done = f32[16,8,384]{2,1,0:T(8,128)S(1)} async-done(((f32[16,8,384]{2,1,0:T(8,128)}), f32[16,8,384]{2,1,0:T(8,128)S(1)}, u32[]{:S(2)}, u32[]{:S(2)}) %all-to-all-start) | async-done | bytes 196640 | tf_op jit(solution)/shard_map/all_to_all | solution.py:77
  156.8 0.0 copy-start.7
  156.9 0.0 copy-done.10
  156.9 0.7 subtract_divide_fusion
  157.5 0.0 copy-done.7
  (8 shorter events, 0.1 us)
Async XLA Ops:
  7.2 4.2 %copy-start.6 = (f32[4,24,4096]{2,1,0:T(8,128)S(1)}, f32[4,24,4096]{2,1,0:T(8,128)}, u32[]{:S(2)}) copy-start(f32[4,24,4096]{2,1,0:T(8,128)} %param.10) | copy-start | bytes 4718596
  7.2 2.3 %copy-start.8 = (s32[16]{0:T(128)S(1)}, s32[16]{0:T(128)}, u32[]{:S(2)}) copy-start(s32[16]{0:T(128)} %param.12) | copy-start | bytes 196
  7.2 82.9 %all-gather.7.cloned.1.call-start = ((), (), s32[]{:S(2)}) async-start(), calls=%async_computation.2 | async-start | bytes 13369344 | tf_op jit(solution)/shard_map/all_gather | solution.py:53
  9.4 125.4 %all-gather.9.cloned.1.call-start = ((), (), s32[]{:S(2)}) async-start(), calls=%async_computation.3 | async-start | bytes 6684672 | tf_op jit(solution)/shard_map/all_gather | solution.py:60
  11.5 12.4 %collective-permute-start.1 = (f32[24,4096]{1,0:T(8,128)S(1)}, f32[24,4096]{1,0:T(8,128)S(1)}, u32[]{:S(2)}, u32[]{:S(2)}) collective-permute-start(f32[24,4096]{1,0:T(8,128)S(1)} %dynamic-slice_bitcast_fusion), channel_id=1, source_target_pairs={{0,8},{1,9},{2,10},{3,11},{4,12},{5,13},{6,14},{7,15},{8,0},{9,1},... | collective-permute-start | bytes 1179656 | tf_op jit(solution)/shard_map/ppermute | solution.py:47
  31.9 1.9 %copy-start.9 = (s32[4]{0:T(128)S(1)}, s32[4]{0:T(128)}, u32[]{:S(2)}) copy-start(s32[4]{0:T(128)} %param.11) | copy-start | bytes 52
  38.1 48.7 %collective-permute-start = (f32[128,4096]{0,1:T(8,128)}, f32[128,4096]{0,1:T(8,128)}, u32[]{:S(2)}, u32[]{:S(2)}) collective-permute-start(f32[128,4096]{0,1:T(8,128)} %bitcast_add_fusion.2), channel_id=1, source_target_pairs={{0,8},{1,9},{2,10},{3,11},{4,12},{5,13},{6,14},{7,15},{8,0},{9,1},... | collective-permute-start | bytes 6291464 | tf_op jit(solution)/shard_map/ppermute | solution.py:48
  44.2 1.3 copy-start.1
  62.4 3.4 %copy-start = (f32[1,128,4096]{1,2,0:T(8,128)S(1)}, f32[1,128,4096]{1,2,0:T(8,128)}, u32[]{:S(2)}) copy-start(f32[1,128,4096]{1,2,0:T(8,128)} %copy.35) | copy-start | bytes 6291460
  62.4 3.3 %copy-start.3 = (f32[128,64,64]{0,2,1:T(8,128)S(1)}, f32[128,64,64]{0,2,1:T(8,128)}, u32[]{:S(2)}) copy-start(f32[128,64,64]{0,2,1:T(8,128)} %copy.28) | copy-start | bytes 6291460
  65.8 21.0 %copy-start.2 = (f32[1,128,4096]{1,2,0:T(8,128)S(1)}, f32[1,128,4096]{1,2,0:T(8,128)}, u32[]{:S(2)}) copy-start(f32[1,128,4096]{1,2,0:T(8,128)} %copy-done.1) | copy-start | bytes 6291460
  65.8 21.0 %copy-start.5 = (f32[128,64,64]{0,2,1:T(8,128)S(1)}, f32[128,64,64]{0,2,1:T(8,128)}, u32[]{:S(2)}) copy-start(f32[128,64,64]{0,2,1:T(8,128)} %copy.32) | copy-start | bytes 6291460
  90.1 7.2 %copy-start.4 = (f32[1,128,4096]{1,2,0:T(8,128)S(1)}, f32[1,128,4096]{1,2,0:T(8,128)}, u32[]{:S(2)}) copy-start(f32[1,128,4096]{1,2,0:T(8,128)} %bitcast_add_fusion.4) | copy-start | bytes 6291460
  142.1 8.1 %copy-start.12 = (s32[8,2]{0,1:T(2,128)S(1)}, s32[8,2]{0,1:T(2,128)}, u32[]{:S(2)}) copy-start(s32[8,2]{0,1:T(2,128)} %param.13) | copy-start | bytes 196
  142.2 8.1 %copy-start.11 = (f32[200]{0:T(256)S(1)}, f32[200]{0:T(256)}, u32[]{:S(2)}) copy-start(f32[200]{0:T(256)} %param.14) | copy-start | bytes 2404
  142.2 14.7 %copy-start.10 = (f32[384]{0:T(512)S(1)}, f32[384]{0:T(512)}, u32[]{:S(2)}) copy-start(f32[384]{0:T(512)} %param.15) | copy-start | bytes 4612
  142.9 13.9 %all-to-all-start = ((f32[16,8,384]{2,1,0:T(8,128)}), f32[16,8,384]{2,1,0:T(8,128)S(1)}, u32[]{:S(2)}, u32[]{:S(2)}) async-start(f32[16,8,384]{2,1,0:T(8,128)} %select_bitcast_fusion), calls=%async_computation | async-start | bytes 393216 | tf_op jit(solution)/shard_map/all_to_all | solution.py:77
  156.8 0.7 copy-start.7
Sparse Core Ops, SparseCore 0:
  9.8 78.5 all-gather.6
  90.2 44.5 all-gather.8

commit v4 on v3

--- a/solution.py
+++ b/solution.py
@@ -15,12 +15,12 @@
     return amp_rows + flag.astype(jnp.float32) * swap_in_tile(amp_rows)
 
 
-def tile_product(amp_tile, int_rows):
+def tile_product(amp_tile, int_rows, precision=lax.Precision.HIGH):
     return lax.dot_general(
         amp_tile,
         int_rows,
         (((1,), (1,)), ((), ())),
-        precision=lax.Precision.HIGH,
+        precision=precision,
         preferred_element_type=jnp.float32,
     )
 
@@ -51,8 +51,8 @@
         return symmetric_amps(amplitudes[slot], tile_flags[slot])
 
     first_two = lax.all_gather(integrals[0:2], "pair", axis=1, tiled=True)
-    running = tile_product(own_amps(0), first_two[0])
-    second = tile_product(own_amps(1), first_two[1])
+    running = tile_product(own_amps(0), first_two[0], lax.Precision.HIGHEST)
+    second = tile_product(own_amps(1), first_two[1], lax.Precision.HIGHEST)
     running = running + jnp.where(keep > 1, second, jnp.zeros_like(second))
 
     third_int = jnp.where(take > 0, recv_int, integrals[2])
@@ -63,14 +63,14 @@
 
     def fourth(acc):
         gathered = lax.all_gather(integrals[3], "pair", axis=0, tiled=True)
-        return acc + tile_product(own_amps(3), gathered)
+        term = tile_product(own_amps(3), gathered)
+        return acc + jnp.where(keep > 3, term, jnp.zeros_like(term))
 
     all_counts = live_count
     all_partners = jnp.roll(live_count, half)
     all_keep = all_counts - jnp.clip((all_counts - all_partners) // 2, 0, 1)
     any_full = jnp.max(all_keep) > 3
-    with_fourth = lax.cond(any_full, fourth, lambda acc: acc, running)
-    running = jnp.where(keep > 3, with_fourth, running)
+    running = lax.cond(any_full, fourth, lambda acc: acc, running)
 
     ab = running.shape[1]
     blocks = running.reshape(n_virt, pair_rows // n_virt, ab)

time: 166 us -> 166 us (level)
  matrix products: 21 us -> 28.2 us
  waiting for transfers between devices: 65.7 us -> 58.9 us
    dot_general x3, matrix products: 21 us -> 28.2 us  [tile_product(): lax.dot_general(amp_tile, int_rows, (((1,), (1,)), ((), ())), precision=p...]
    all_gather x1, waiting for transfers between devices: 31 us -> 24.3 us  [on_device(): lax.all_gather(third_int, 'pair', axis=0, tiled=True)]
  transfers between devices with their start and end apart: 5 -> 5, of which waited for: 4 -> 4; matrix products, arithmetic and copies ran while one was open for 33% -> 37% of each run, Pallas kernels for 0% -> 0%
where the time goes in v4:
time: 166 us; the launch traced here: 164 us
  waiting for transfers between devices  58.9 us (35%)
  local copies, waits for them, and re-layouts  28.9 us (17%)
  matrix products  28.2 us (17%)
  between operations  22 us (13%)
  other arithmetic  14.4 us (9%)
  starting transfers between devices  11.8 us (7%)
    dot_general x3, matrix products, tile_product(): lax.dot_general(amp_tile, int_rows, (((1,), (1,)), ((), ())), precision=p...  28.2 us
    all_gather x1, waiting for transfers between devices, on_device(): lax.all_gather(third_int, 'pair', axis=0, tiled=True)  24.3 us
    ppermute x1, waiting for transfers between devices, on_device(): recv_amp = lax.ppermute(send_amp, 'virt', perm)  19.3 us
    unnamed x30, local copies, waits for them, and re-layouts  9.35 us
    ppermute x1, waiting for transfers between devices, on_device(): recv_int = lax.ppermute(send_int, 'virt', perm)  8.91 us
    mul x4, local copies, waits for them, and re-layouts, symmetric_amps(): return amp_rows + flag.astype(jnp.float32) * swap_in_tile(amp_rows)  8.8 us
    slice x2, local copies, waits for them, and re-layouts, own_amps(): return symmetric_amps(amplitudes[slot], tile_flags[slot])  7.83 us
    all_to_all x1, starting transfers between devices, on_device(): received = lax.all_to_all(blocks, 'virt', 0, 0, tiled=False)  7.41 us
  transfers between devices with their start and end apart: 5, of which 4 were waited for; matrix products, arithmetic and copies ran while one was open for 37% of the time, Pallas kernels for 0%

profile of v4, /device:TPU:2, one launch (start us, length us, event | category | flops | bytes accessed | tf_op | source)
XLA Modules:
  0.0 164.2 jit_solution(13498925303174141118)
XLA Ops:
  7.2 0.0 copy-start.6
  7.2 0.0 copy-start.8
  7.2 0.0 all-gather.7.cloned.1.call-start
  7.2 2.2 %slice.57 = f32[2,24,4096]{2,1,0:T(8,128)} slice(f32[4,24,4096]{2,1,0:T(8,128)} %param.10), slice={[0:2], [0:24], [0:4096]} | slice | bytes 1572864 | tf_op jit(solution)/shard_map/slice | solution.py:53
  9.4 0.0 all-gather.7.cloned.1.call-update
  9.4 0.0 all-gather.9.cloned.1.call-start
  9.5 0.0 copy-done.8
  9.5 0.6 fusion.22
  11.4 0.0 copy-done.6
  11.5 2.2 %collective-permute-start.1 = (f32[24,4096]{1,0:T(8,128)S(1)}, f32[24,4096]{1,0:T(8,128)S(1)}, u32[]{:S(2)}, u32[]{:S(2)}) collective-permute-start(f32[24,4096]{1,0:T(8,128)S(1)} %dynamic-slice_bitcast_fusion), channel_id=1, source_target_pairs={{0,8},{1,9},{2,10},{3,11},{4,12},{5,13},{6,14},{7,15},{8,0},{9,1},... | collective-permute-start | bytes 1179656 | tf_op jit(solution)/shard_map/ppermute | solution.py:47
  15.0 8.9 %collective-permute-done.1 = f32[24,4096]{1,0:T(8,128)S(1)} collective-permute-done((f32[24,4096]{1,0:T(8,128)S(1)}, f32[24,4096]{1,0:T(8,128)S(1)}, u32[]{:S(2)}, u32[]{:S(2)}) %collective-permute-start.1) | collective-permute-done | bytes 393248 | tf_op jit(solution)/shard_map/ppermute | solution.py:47
  23.9 0.8 bitcast_select_fusion
  24.7 0.0 all-gather.9.cloned.1.call-update
  24.7 7.2 %fusion.20 = (f32[1,128,4096]{2,1,0:T(8,128)}, f32[1,128,4096]{2,1,0:T(8,128)}, f32[1,128,4096]{2,1,0:T(8,128)}, f32[1,128,4096]{2,1,0:T(8,128)}) fusion(f32[4,128,4096]{2,1,0:T(8,128)} %param.9, s32[]{:T(128)S(6)} %select_n.86), kind=kLoop, calls=%fused_computation.41 | loop fusion | bytes 16777220 | tf_op jit(solution)/shard_map/slice | solution.py:51
  31.9 0.0 copy-start.9
  31.9 1.9 %copy.36 = f32[1,128,4096]{1,2,0:T(8,128)S(1)} copy(f32[1,128,4096]{2,1,0:T(8,128)} %get-tuple-element.34) | data formatting | bytes 4194304
  33.8 0.0 copy-done.9
  33.8 0.7 fusion.21
  35.1 0.1 broadcast_multiply_fusion.1
  35.3 1.2 copy.30
  36.5 1.6 bitcast_add_fusion.2
  38.1 2.1 %collective-permute-start = (f32[128,4096]{0,1:T(8,128)}, f32[128,4096]{0,1:T(8,128)}, u32[]{:S(2)}, u32[]{:S(2)}) collective-permute-start(f32[128,4096]{0,1:T(8,128)} %bitcast_add_fusion.2), channel_id=1, source_target_pairs={{0,8},{1,9},{2,10},{3,11},{4,12},{5,13},{6,14},{7,15},{8,0},{9,1},... | collective-permute-start | bytes 6291464 | tf_op jit(solution)/shard_map/ppermute | solution.py:48
  41.6 1.9 %copy.37 = f32[1,128,4096]{1,2,0:T(8,128)S(1)} copy(f32[1,128,4096]{2,1,0:T(8,128)} %get-tuple-element.33) | data formatting | bytes 4194304
  43.5 0.0 copy-start.1
  44.2 0.1 broadcast_multiply_fusion
  44.3 0.5 copy-done.1
  44.8 2.5 %copy.32 = f32[128,64,64]{0,2,1:T(8,128)} copy(f32[128,64,64]{0,1,2:T(8,128)S(1)} %bitcast.80) | data formatting | bytes 4194304 | tf_op jit(solution)/shard_map/mul | solution.py:15
  47.4 2.0 %copy.34 = f32[1,128,4096]{1,2,0:T(8,128)S(1)} copy(f32[1,128,4096]{2,1,0:T(8,128)} %get-tuple-element.36) | data formatting | bytes 4194304
  50.0 0.1 broadcast_multiply_fusion.3
  50.1 2.5 %copy.26 = f32[128,64,64]{0,2,1:T(8,128)} copy(f32[128,64,64]{0,1,2:T(8,128)S(1)} %bitcast.81) | data formatting | bytes 4194304 | tf_op jit(solution)/shard_map/mul | solution.py:15
  52.7 3.0 %copy.35 = f32[1,128,4096]{1,2,0:T(8,128)} copy(f32[1,128,4096]{2,1,0:T(8,128)} %get-tuple-element.35) | data formatting | bytes 4194304
  56.2 1.8 %broadcast_multiply_fusion.2 = f32[1,128,4096]{1,2,0:T(8,128)S(1)} fusion(f32[1,128,4096]{1,2,0:T(8,128)} %copy.35, f32[]{:T(128)} %bitcast.14), kind=kLoop, calls=%fused_computation.23 | loop fusion | flops 524288 | bytes 4194308 | tf_op jit(solution)/shard_map/mul | solution.py:15
  57.9 2.5 %copy.28 = f32[128,64,64]{0,2,1:T(8,128)} copy(f32[128,64,64]{0,1,2:T(8,128)S(1)} %bitcast.82) | data formatting | bytes 4194304 | tf_op jit(solution)/shard_map/mul | solution.py:15
  61.1 0.1 fusion.23
  61.2 0.7 subtract_reduce_fusion
  62.6 0.0 copy-start
  62.6 0.0 copy-start.3
  62.6 3.3 %bitcast_add_fusion.4 = f32[1,128,4096]{1,2,0:T(8,128)} fusion(f32[1,128,4096]{1,2,0:T(8,128)S(1)} %copy.34, f32[128,64,64]{0,2,1:T(8,128)} %copy.26), kind=kLoop, calls=%fused_computation.16 | loop fusion | flops 524288 | bytes 6291456 | tf_op jit(solution)/shard_map/add | solution.py:15
  65.9 0.0 copy-done
  65.9 0.0 copy-done.3
  65.9 0.0 copy-start.5
  65.9 1.6 bitcast_add_fusion.3
  67.5 19.3 %collective-permute-done = f32[128,4096]{0,1:T(8,128)} collective-permute-done((f32[128,4096]{0,1:T(8,128)}, f32[128,4096]{0,1:T(8,128)}, u32[]{:S(2)}, u32[]{:S(2)}) %collective-permute-start) | collective-permute-done | bytes 2097184 | tf_op jit(solution)/shard_map/ppermute | solution.py:48
  86.8 0.0 copy-done.2
  86.8 0.0 copy-done.5
  86.8 3.3 %fusion.10 = f32[128,4096]{0,1:T(8,128)} fusion(f32[128,4096]{0,1:T(8,128)} %collective-permute-done, f32[128,64,64]{0,2,1:T(8,128)S(1)} %copy-done.5, f32[1,128,4096]{1,2,0:T(8,128)S(1)} %copy-done.2, pred[]{:T(512)S(6)} %gt.19), kind=kLoop, calls=%fused_computation.11 | loop fusion | flops 1048576 | bytes 8388609 | tf_op jit(solution)/shard_map/jit(_where)/select_n | solution.py:59
  90.1 0.0 copy-start.4
  90.1 0.0 all-gather.7.cloned.1.call-done
  90.1 10.8 %fusion.16 = f32[128,384]{1,0:T(8,128)S(1)} fusion(f32[2,384,4096]{2,1,0:T(8,128)} %all-gather.7.cloned.1.call-done, f32[1,128,4096]{1,2,0:T(8,128)} %bitcast_add_fusion.3, pred[]{:T(512)S(6)} %gt.18), kind=kOutput, calls=%fused_computation.18 | convolution fusion | flops 2415968256 | bytes 8585217 | tf_op jit(solution)/shard_map/dot_general | solution.py:19
  101.0 0.0 copy-done.4
  101.0 9.6 %fusion.13 = f32[128,384]{1,0:T(8,128)S(1)} fusion(f32[128,384]{1,0:T(8,128)S(1)} %fusion.16, f32[2,384,4096]{2,1,0:T(8,128)} %all-gather.7.cloned.1.call-done, f32[1,128,4096]{1,2,0:T(8,128)S(1)} %copy-done.4), kind=kOutput, calls=%fused_computation.17 | convolution fusion | flops 2415968256 | bytes 8781824 | tf_op jit(solution)/shard_map/dot_general | solution.py:19
  110.6 24.3 %all-gather.9.cloned.1.call-done = f32[384,4096]{1,0:T(8,128)} async-done(((f32[24,4096]{1,0:T(8,128)}), f32[384,4096]{1,0:T(8,128)}) %all-gather.9.cloned.1.call-update) | async-done | bytes 6291472 | tf_op jit(solution)/shard_map/all_gather | solution.py:60
  134.9 7.7 %fusion.19 = f32[128,384]{1,0:T(8,128)} fusion(f32[128,384]{1,0:T(8,128)S(1)} %fusion.13, f32[128,4096]{0,1:T(8,128)} %fusion.10, f32[384,4096]{1,0:T(8,128)} %all-gather.9.cloned.1.call-done, pred[]{:T(512)S(6)} %or.3), kind=kOutput, calls=%fused_computation.20 | convolution fusion | flops 1208057856 | bytes 8781825 | tf_op jit(solution)/shard_map/dot_general | solution.py:19
  142.6 0.0 copy-start.12
  142.6 0.0 copy-start.11
  142.6 7.4 %all-to-all-start = ((f32[16,8,384]{2,1,0:T(8,128)}), f32[16,8,384]{2,1,0:T(8,128)S(1)}, u32[]{:S(2)}, u32[]{:S(2)}) async-start(f32[16,8,384]{2,1,0:T(8,128)} %bitcast.32), calls=%async_computation | async-start | bytes 393216 | tf_op jit(solution)/shard_map/all_to_all | solution.py:77
  150.0 0.0 copy-done.12
  150.0 0.0 copy-done.11
  150.1 0.2 select_reduce_fusion.1
  150.3 6.4 %all-to-all-done = f32[16,8,384]{2,1,0:T(8,128)S(1)} async-done(((f32[16,8,384]{2,1,0:T(8,128)}), f32[16,8,384]{2,1,0:T(8,128)S(1)}, u32[]{:S(2)}, u32[]{:S(2)}) %all-to-all-start) | async-done | bytes 196640 | tf_op jit(solution)/shard_map/all_to_all | solution.py:77
  156.7 0.0 copy-start.7
  156.7 0.0 copy-done.10
  156.7 0.7 subtract_divide_fusion
  157.4 0.0 copy-done.7
  (6 shorter events, 0.1 us)
Async XLA Ops:
  7.2 4.2 %copy-start.6 = (f32[4,24,4096]{2,1,0:T(8,128)S(1)}, f32[4,24,4096]{2,1,0:T(8,128)}, u32[]{:S(2)}) copy-start(f32[4,24,4096]{2,1,0:T(8,128)} %param.10) | copy-start | bytes 4718596
  7.2 2.3 %copy-start.8 = (s32[16]{0:T(128)S(1)}, s32[16]{0:T(128)}, u32[]{:S(2)}) copy-start(s32[16]{0:T(128)} %param.12) | copy-start | bytes 196
  7.2 82.9 %all-gather.7.cloned.1.call-start = ((), (), s32[]{:S(2)}) async-start(), calls=%async_computation.2 | async-start | bytes 13369344 | tf_op jit(solution)/shard_map/all_gather | solution.py:53
  9.4 125.4 %all-gather.9.cloned.1.call-start = ((), (), s32[]{:S(2)}) async-start(), calls=%async_computation.3 | async-start | bytes 6684672 | tf_op jit(solution)/shard_map/all_gather | solution.py:60
  11.5 12.4 %collective-permute-start.1 = (f32[24,4096]{1,0:T(8,128)S(1)}, f32[24,4096]{1,0:T(8,128)S(1)}, u32[]{:S(2)}, u32[]{:S(2)}) collective-permute-start(f32[24,4096]{1,0:T(8,128)S(1)} %dynamic-slice_bitcast_fusion), channel_id=1, source_target_pairs={{0,8},{1,9},{2,10},{3,11},{4,12},{5,13},{6,14},{7,15},{8,0},{9,1},... | collective-permute-start | bytes 1179656 | tf_op jit(solution)/shard_map/ppermute | solution.py:47
  31.9 1.9 %copy-start.9 = (s32[4]{0:T(128)S(1)}, s32[4]{0:T(128)}, u32[]{:S(2)}) copy-start(s32[4]{0:T(128)} %param.11) | copy-start | bytes 52
  38.1 48.7 %collective-permute-start = (f32[128,4096]{0,1:T(8,128)}, f32[128,4096]{0,1:T(8,128)}, u32[]{:S(2)}, u32[]{:S(2)}) collective-permute-start(f32[128,4096]{0,1:T(8,128)} %bitcast_add_fusion.2), channel_id=1, source_target_pairs={{0,8},{1,9},{2,10},{3,11},{4,12},{5,13},{6,14},{7,15},{8,0},{9,1},... | collective-permute-start | bytes 6291464 | tf_op jit(solution)/shard_map/ppermute | solution.py:48
  43.5 1.3 copy-start.1
  62.6 3.3 %copy-start = (f32[1,128,4096]{1,2,0:T(8,128)S(1)}, f32[1,128,4096]{1,2,0:T(8,128)}, u32[]{:S(2)}) copy-start(f32[1,128,4096]{1,2,0:T(8,128)} %copy.35) | copy-start | bytes 6291460
  62.6 3.3 %copy-start.3 = (f32[128,64,64]{0,2,1:T(8,128)S(1)}, f32[128,64,64]{0,2,1:T(8,128)}, u32[]{:S(2)}) copy-start(f32[128,64,64]{0,2,1:T(8,128)} %copy.28) | copy-start | bytes 6291460
  65.9 20.9 %copy-start.2 = (f32[1,128,4096]{1,2,0:T(8,128)S(1)}, f32[1,128,4096]{1,2,0:T(8,128)}, u32[]{:S(2)}) copy-start(f32[1,128,4096]{1,2,0:T(8,128)} %copy-done.1) | copy-start | bytes 6291460
  65.9 20.9 %copy-start.5 = (f32[128,64,64]{0,2,1:T(8,128)S(1)}, f32[128,64,64]{0,2,1:T(8,128)}, u32[]{:S(2)}) copy-start(f32[128,64,64]{0,2,1:T(8,128)} %copy.32) | copy-start | bytes 6291460
  90.1 10.9 %copy-start.4 = (f32[1,128,4096]{1,2,0:T(8,128)S(1)}, f32[1,128,4096]{1,2,0:T(8,128)}, u32[]{:S(2)}) copy-start(f32[1,128,4096]{1,2,0:T(8,128)} %bitcast_add_fusion.4) | copy-start | bytes 6291460
  142.6 7.4 %copy-start.12 = (s32[8,2]{0,1:T(2,128)S(1)}, s32[8,2]{0,1:T(2,128)}, u32[]{:S(2)}) copy-start(s32[8,2]{0,1:T(2,128)} %param.13) | copy-start | bytes 196
  142.6 7.4 %copy-start.11 = (f32[200]{0:T(256)S(1)}, f32[200]{0:T(256)}, u32[]{:S(2)}) copy-start(f32[200]{0:T(256)} %param.14) | copy-start | bytes 2404
  142.6 14.1 %copy-start.10 = (f32[384]{0:T(512)S(1)}, f32[384]{0:T(512)}, u32[]{:S(2)}) copy-start(f32[384]{0:T(512)} %param.15) | copy-start | bytes 4612
  142.6 14.0 %all-to-all-start = ((f32[16,8,384]{2,1,0:T(8,128)}), f32[16,8,384]{2,1,0:T(8,128)S(1)}, u32[]{:S(2)}, u32[]{:S(2)}) async-start(f32[16,8,384]{2,1,0:T(8,128)} %bitcast.32), calls=%async_computation | async-start | bytes 393216 | tf_op jit(solution)/shard_map/all_to_all | solution.py:77
  156.7 0.7 copy-start.7
Sparse Core Ops, SparseCore 0:
  9.8 78.5 all-gather.6
  90.2 44.5 all-gather.8

commit v5 on v4

--- a/solution.py
+++ b/solution.py
@@ -31,11 +31,21 @@
     half = n_virt // 2
     virt_index = lax.axis_index("virt")
     partner = (virt_index + half) % n_virt
+    columns = jnp.arange(n_virt, dtype=jnp.int32)
+    neighbour = columns ^ 1
+    across = jnp.roll(live_count, half)
+    give_one = jnp.clip((live_count - across) // 2, 0, 1)
+    take_one = jnp.clip((across - live_count) // 2, 0, 1)
+    keep_one = live_count - give_one
+    give_two = (
+        (keep_one == 4) & (take_one[neighbour] == 0) & (keep_one[neighbour] <= 2)
+    ).astype(jnp.int32)
+    take_two = give_two[neighbour]
+    keep_all = keep_one - give_two
     own_count = live_count[virt_index]
-    partner_count = live_count[partner]
-    give = jnp.clip((own_count - partner_count) // 2, 0, 1)
-    take = jnp.clip((partner_count - own_count) // 2, 0, 1)
-    keep = own_count - give
+    take = take_one[virt_index]
+    take_y = take_two[virt_index]
+    keep = keep_all[virt_index]
 
     send_at = own_count - 1
     send_amp = symmetric_amps(
@@ -46,6 +56,9 @@
     perm = [(v, (v + half) % n_virt) for v in range(n_virt)]
     recv_int = lax.ppermute(send_int, "virt", perm)
     recv_amp = lax.ppermute(send_amp, "virt", perm)
+    perm_y = [(v, v ^ 1) for v in range(n_virt)]
+    recv_int_y = lax.ppermute(integrals[3], "virt", perm_y)
+    recv_amp_y = lax.ppermute(symmetric_amps(amplitudes[3], tile_flags[3]), "virt", perm_y)
 
     def own_amps(slot):
         return symmetric_amps(amplitudes[slot], tile_flags[slot])
@@ -55,10 +68,10 @@
     second = tile_product(own_amps(1), first_two[1], lax.Precision.HIGHEST)
     running = running + jnp.where(keep > 1, second, jnp.zeros_like(second))
 
-    third_int = jnp.where(take > 0, recv_int, integrals[2])
-    third_amp = jnp.where(take > 0, recv_amp, own_amps(2))
+    third_int = jnp.where(take > 0, recv_int, jnp.where(take_y > 0, recv_int_y, integrals[2]))
+    third_amp = jnp.where(take > 0, recv_amp, jnp.where(take_y > 0, recv_amp_y, own_amps(2)))
     third = tile_product(third_amp, lax.all_gather(third_int, "pair", axis=0, tiled=True))
-    third_live = (take > 0) | (keep > 2)
+    third_live = (take > 0) | (take_y > 0) | (keep > 2)
     running = running + jnp.where(third_live, third, jnp.zeros_like(third))
 
     def fourth(acc):
@@ -66,10 +79,7 @@
         term = tile_product(own_amps(3), gathered)
         return acc + jnp.where(keep > 3, term, jnp.zeros_like(term))
 
-    all_counts = live_count
-    all_partners = jnp.roll(live_count, half)
-    all_keep = all_counts - jnp.clip((all_counts - all_partners) // 2, 0, 1)
-    any_full = jnp.max(all_keep) > 3
+    any_full = jnp.max(keep_all) > 3
     running = lax.cond(any_full, fourth, lambda acc: acc, running)
 
     ab = running.shape[1]

time: 166 us -> 165 us (level)
  waiting for transfers between devices: 58.9 us -> 48.2 us
  local copies, waits for them, and re-layouts: 28.9 us -> 36.9 us
  starting transfers between devices: 11.8 us -> 14.6 us
  matrix products: 28.2 us -> 26.4 us
    ppermute x1, waiting for transfers between devices: 19.3 us -> 13 us  [on_device(): recv_amp = lax.ppermute(send_amp, 'virt', perm)]
    ppermute x0 -> x2, waiting for transfers between devices: none -> 6.19 us  [the longest x1 5.84 us: on_device(): lax.ppermute(symmetric_amps(amplitudes[3], tile_flags[3]), 'virt', perm_y)]
    ppermute x1, waiting for transfers between devices: 8.91 us -> 3.25 us  [on_device(): recv_int = lax.ppermute(send_int, 'virt', perm)]
    all_gather x1, waiting for transfers between devices: 24.3 us -> 19.4 us  [on_device(): lax.all_gather(third_int, 'pair', axis=0, tiled=True)]
    ppermute x0 -> x2, starting transfers between devices: none -> 3.15 us  [the longest x1 1.58 us: on_device(): lax.ppermute(symmetric_amps(amplitudes[3], tile_flags[3]), 'virt', perm_y)]
    gather x0 -> x3, local copies, waits for them, and re-layouts: none -> 1.98 us  [the longest x1 0.67 us: on_device(): keep_one[neighbour] <= 2]
    unnamed x30 -> x35, local copies, waits for them, and re-layouts: 9.35 us -> 11.2 us
    dynamic_slice x1 -> x4, local copies, waits for them, and re-layouts: 0.59 us -> 2.43 us  [the longest x1 0.67 us: on_device(): take = take_one[virt_index]]
  transfers between devices with their start and end apart: 5 -> 7, of which waited for: 4 -> 6; matrix products, arithmetic and copies ran while one was open for 37% -> 42% of each run, Pallas kernels for 0% -> 0%
where the time goes in v5:
time: 165 us; the launch traced here: 164 us
  waiting for transfers between devices  48.2 us (29%)
  local copies, waits for them, and re-layouts  36.9 us (22%)
  matrix products  26.4 us (16%)
  between operations  22 us (13%)
  other arithmetic  15.4 us (9%)
  starting transfers between devices  14.6 us (9%)
    dot_general x3, matrix products, tile_product(): lax.dot_general(amp_tile, int_rows, (((1,), (1,)), ((), ())), precision=p...  26.4 us
    all_gather x1, waiting for transfers between devices, on_device(): lax.all_gather(third_int, 'pair', axis=0, tiled=True)  19.4 us
    ppermute x1, waiting for transfers between devices, on_device(): recv_amp = lax.ppermute(send_amp, 'virt', perm)  13 us
    unnamed x35, local copies, waits for them, and re-layouts  11.2 us
    mul x5, local copies, waits for them, and re-layouts, symmetric_amps(): return amp_rows + flag.astype(jnp.float32) * swap_in_tile(amp_rows)  10 us
    slice x2, local copies, waits for them, and re-layouts, own_amps(): return symmetric_amps(amplitudes[slot], tile_flags[slot])  8.97 us
    add x4, other arithmetic, symmetric_amps(): return amp_rows + flag.astype(jnp.float32) * swap_in_tile(amp_rows)  8.23 us
    all_to_all x1, starting transfers between devices, on_device(): received = lax.all_to_all(blocks, 'virt', 0, 0, tiled=False)  7.41 us
  transfers between devices with their start and end apart: 7, of which 6 were waited for; matrix products, arithmetic and copies ran while one was open for 42% of the time, Pallas kernels for 0%

profile of v5, /device:TPU:2, one launch (start us, length us, event | category | flops | bytes accessed | tf_op | source)
XLA Modules:
  0.0 163.6 jit_solution(631864503196057487)
XLA Ops:
  7.2 0.0 copy-start.8
  7.2 0.0 copy-start.11
  7.2 0.0 all-gather.7.cloned.1.call-start
  7.2 2.2 %slice.66 = f32[2,24,4096]{2,1,0:T(8,128)} slice(f32[4,24,4096]{2,1,0:T(8,128)} %param.10), slice={[0:2], [0:24], [0:4096]} | slice | bytes 1572864 | tf_op jit(solution)/shard_map/slice | solution.py:66
  9.4 0.0 all-gather.7.cloned.1.call-update
  9.4 0.0 all-gather.9.cloned.1.call-start
  9.5 0.0 copy-done.11
  9.5 0.6 dynamic_slice.27
  11.4 0.0 copy-done.8
  11.4 0.1 slice_bitcast_fusion.8
  11.5 2.2 %collective-permute-start.2 = (f32[24,4096]{1,0:T(8,128)S(1)}, f32[24,4096]{1,0:T(8,128)S(1)}, u32[]{:S(2)}, u32[]{:S(2)}) collective-permute-start(f32[24,4096]{1,0:T(8,128)S(1)} %get-tuple-element.42), channel_id=1, source_target_pairs={{0,8},{1,9},{2,10},{3,11},{4,12},{5,13},{6,14},{7,15},{8,0},{9,1},... | collective-permute-start | bytes 1179656 | tf_op jit(solution)/shard_map/ppermute | solution.py:57
  13.7 1.6 collective-permute-start.3
  15.2 0.1 fusion.27
  15.3 0.1 fusion.23
  15.4 0.7 dynamic_slice.25
  16.1 0.7 gather_fusion
  16.7 0.7 gather_fusion.1
  17.4 0.6 fusion.24
  18.1 0.7 gather_fusion.2
  18.7 0.6 dynamic_slice.26
  20.7 3.3 %collective-permute-done.2 = f32[24,4096]{1,0:T(8,128)S(1)} collective-permute-done((f32[24,4096]{1,0:T(8,128)S(1)}, f32[24,4096]{1,0:T(8,128)S(1)}, u32[]{:S(2)}, u32[]{:S(2)}) %collective-permute-start.2) | collective-permute-done | bytes 393248 | tf_op jit(solution)/shard_map/ppermute | solution.py:57
  23.9 0.3 collective-permute-done.3
  24.2 0.8 fusion.21
  25.1 0.0 all-gather.9.cloned.1.call-update
  25.1 8.3 %fusion.25 = (f32[1,128,4096]{2,1,0:T(8,128)}, f32[1,128,4096]{2,1,0:T(8,128)}, f32[1,128,4096]{2,1,0:T(8,128)}, f32[1,128,4096]{2,1,0:T(8,128)}, f32[1,128,4096]{2,1,0:T(8,128)}) fusion(f32[4,128,4096]{2,1,0:T(8,128)} %param.9, s32[]{:T(128)S(6)} %select_n.101), kind=kLoop, calls=%fused_computation.59 | loop fusion | bytes 20971524 | tf_op jit(solution)/shard_map/slice | solution.py:64
  33.4 1.9 %copy.41 = f32[1,128,4096]{1,2,0:T(8,128)S(1)} copy(f32[1,128,4096]{2,1,0:T(8,128)} %get-tuple-element.38) | data formatting | bytes 4194304
  35.3 0.0 copy-done.10
  35.4 0.7 fusion.26
  36.7 0.1 broadcast_multiply_fusion.2
  36.8 1.2 copy.33
  38.0 1.7 %bitcast_add_fusion.3 = f32[128,4096]{0,1:T(8,128)} fusion(f32[128,64,64]{0,2,1:T(8,128)S(1)} %copy.33, f32[1,128,4096]{1,2,0:T(8,128)S(1)} %copy.41), kind=kLoop, calls=%fused_computation.17 | loop fusion | flops 524288 | bytes 6291456 | tf_op jit(solution)/shard_map/add | solution.py:15
  39.7 1.8 %collective-permute-start = (f32[128,4096]{0,1:T(8,128)}, f32[128,4096]{0,1:T(8,128)}, u32[]{:S(2)}, u32[]{:S(2)}) collective-permute-start(f32[128,4096]{0,1:T(8,128)} %bitcast_add_fusion.3), channel_id=1, source_target_pairs={{0,8},{1,9},{2,10},{3,11},{4,12},{5,13},{6,14},{7,15},{8,0},{9,1},... | collective-permute-start | bytes 6291464 | tf_op jit(solution)/shard_map/ppermute | solution.py:58
  41.5 1.9 %copy.42 = f32[1,128,4096]{1,2,0:T(8,128)S(1)} copy(f32[1,128,4096]{2,1,0:T(8,128)} %get-tuple-element.37) | data formatting | bytes 4194304
  44.1 0.1 broadcast_multiply_fusion.1
  44.2 1.2 copy.35
  45.4 1.6 bitcast_add_fusion.2
  47.0 1.6 collective-permute-start.1
  48.6 1.9 %copy.43 = f32[1,128,4096]{1,2,0:T(8,128)S(1)} copy(f32[1,128,4096]{2,1,0:T(8,128)} %get-tuple-element.36) | data formatting | bytes 4194304
  50.5 0.0 copy-start.1
  51.1 0.1 broadcast_multiply_fusion
  51.3 0.5 copy-done.1
  51.8 2.5 %copy.37 = f32[128,64,64]{0,2,1:T(8,128)} copy(f32[128,64,64]{0,1,2:T(8,128)S(1)} %bitcast.100) | data formatting | bytes 4194304 | tf_op jit(solution)/shard_map/mul | solution.py:15
  54.3 1.9 %copy.40 = f32[1,128,4096]{1,2,0:T(8,128)S(1)} copy(f32[1,128,4096]{2,1,0:T(8,128)} %get-tuple-element.39) | data formatting | bytes 4194304
  56.9 0.1 broadcast_multiply_fusion.3
  57.1 2.6 %copy.31 = f32[128,64,64]{0,2,1:T(8,128)} copy(f32[128,64,64]{0,1,2:T(8,128)S(1)} %bitcast.101) | data formatting | bytes 4194304 | tf_op jit(solution)/shard_map/mul | solution.py:15
  59.7 0.6 dynamic_slice.24
  60.2 2.9 %copy.39 = f32[1,128,4096]{1,2,0:T(8,128)} copy(f32[1,128,4096]{2,1,0:T(8,128)} %get-tuple-element.40) | data formatting | bytes 4194304
  63.7 1.8 %broadcast_multiply_fusion.4 = f32[1,128,4096]{1,2,0:T(8,128)S(1)} fusion(f32[1,128,4096]{1,2,0:T(8,128)} %copy.39, f32[]{:T(128)} %bitcast.7), kind=kLoop, calls=%fused_computation.30 | loop fusion | flops 524288 | bytes 4194308 | tf_op jit(solution)/shard_map/mul | solution.py:15
  65.5 2.5 %copy.29 = f32[128,64,64]{0,2,1:T(8,128)} copy(f32[128,64,64]{0,1,2:T(8,128)S(1)} %bitcast.102) | data formatting | bytes 4194304 | tf_op jit(solution)/shard_map/mul | solution.py:15
  70.0 3.4 %bitcast_add_fusion.4 = f32[1,128,4096]{1,2,0:T(8,128)} fusion(f32[1,128,4096]{1,2,0:T(8,128)S(1)} %copy.40, f32[128,64,64]{0,2,1:T(8,128)} %copy.31), kind=kLoop, calls=%fused_computation.19 | loop fusion | flops 524288 | bytes 6291456 | tf_op jit(solution)/shard_map/add | solution.py:15
  73.5 1.6 bitcast_add_fusion.5
  75.0 13.0 %collective-permute-done = f32[128,4096]{0,1:T(8,128)} collective-permute-done((f32[128,4096]{0,1:T(8,128)}, f32[128,4096]{0,1:T(8,128)}, u32[]{:S(2)}, u32[]{:S(2)}) %collective-permute-start) | collective-permute-done | bytes 2097184 | tf_op jit(solution)/shard_map/ppermute | solution.py:58
  88.0 5.8 %collective-permute-done.1 = f32[128,4096]{0,1:T(8,128)} collective-permute-done((f32[128,4096]{0,1:T(8,128)}, f32[128,4096]{0,1:T(8,128)}, u32[]{:S(2)}, u32[]{:S(2)}) %collective-permute-start.1) | collective-permute-done | bytes 2097184 | tf_op jit(solution)/shard_map/ppermute | solution.py:61
  93.9 2.3 %fusion.11 = f32[128,4096]{0,1:T(8,128)} fusion(f32[128,4096]{0,1:T(8,128)} %collective-permute-done, f32[128,4096]{0,1:T(8,128)} %collective-permute-done.1, f32[128,64,64]{0,2,1:T(8,128)S(1)} %copy-done.7, f32[1,128,4096]{1,2,0:T(8,128)S(1)} %copy-done.2, pred[]{:T(512)} %bitcast.21, pred[]{:T(512)} %bitcast.20), kind=kLoop, calls=%fused_computation.15 | loop fusion | flops 1572864 | bytes 10485762 | tf_op jit(solution)/shard_map/jit(_where)/select_n | solution.py:72
  96.2 9.5 %fusion.17 = f32[128,384]{1,0:T(8,128)S(1)} fusion(f32[2,384,4096]{2,1,0:T(8,128)} %all-gather.7.cloned.1.call-done, f32[1,128,4096]{1,2,0:T(8,128)S(1)} %copy-done.4, pred[]{:T(512)S(6)} %gt.29), kind=kOutput, calls=%fused_computation.23 | convolution fusion | flops 2415968256 | bytes 8585217 | tf_op jit(solution)/shard_map/dot_general | solution.py:19
  105.7 9.8 %fusion.14 = f32[128,384]{1,0:T(8,128)S(1)} fusion(f32[128,384]{1,0:T(8,128)S(1)} %fusion.17, f32[2,384,4096]{2,1,0:T(8,128)} %all-gather.7.cloned.1.call-done, f32[1,128,4096]{1,2,0:T(8,128)S(1)} %copy-done.5), kind=kOutput, calls=%fused_computation.22 | convolution fusion | flops 2415968256 | bytes 8781824 | tf_op jit(solution)/shard_map/dot_general | solution.py:19
  115.5 19.4 %all-gather.9.cloned.1.call-done = f32[384,4096]{1,0:T(8,128)} async-done(((f32[24,4096]{1,0:T(8,128)}), f32[384,4096]{1,0:T(8,128)}) %all-gather.9.cloned.1.call-update) | async-done | bytes 6291472 | tf_op jit(solution)/shard_map/all_gather | solution.py:73
  134.9 7.1 %fusion.20 = f32[128,384]{1,0:T(8,128)} fusion(f32[128,384]{1,0:T(8,128)S(1)} %fusion.14, f32[128,4096]{0,1:T(8,128)S(1)} %copy-done.6, f32[384,4096]{1,0:T(8,128)} %all-gather.9.cloned.1.call-done, pred[]{:T(512)S(6)} %or.7), kind=kOutput, calls=%fused_computation.25 | convolution fusion | flops 1208057856 | bytes 8781825 | tf_op jit(solution)/shard_map/dot_general | solution.py:19
  142.0 7.4 %all-to-all-start = ((f32[16,8,384]{2,1,0:T(8,128)}), f32[16,8,384]{2,1,0:T(8,128)S(1)}, u32[]{:S(2)}, u32[]{:S(2)}) async-start(f32[16,8,384]{2,1,0:T(8,128)} %bitcast.42), calls=%async_computation | async-start | bytes 393216 | tf_op jit(solution)/shard_map/all_to_all | solution.py:87
  149.4 0.0 copy-done.14
  149.4 0.2 select_reduce_fusion.1
  149.6 6.4 %all-to-all-done = f32[16,8,384]{2,1,0:T(8,128)S(1)} async-done(((f32[16,8,384]{2,1,0:T(8,128)}), f32[16,8,384]{2,1,0:T(8,128)S(1)}, u32[]{:S(2)}, u32[]{:S(2)}) %all-to-all-start) | async-done | bytes 196640 | tf_op jit(solution)/shard_map/all_to_all | solution.py:87
  156.0 0.0 copy-start.9
  156.1 0.7 subtract_divide_fusion
  (27 shorter events, 0.1 us)
Async XLA Ops:
  7.2 4.2 %copy-start.8 = (f32[4,24,4096]{2,1,0:T(8,128)S(1)}, f32[4,24,4096]{2,1,0:T(8,128)}, u32[]{:S(2)}) copy-start(f32[4,24,4096]{2,1,0:T(8,128)} %param.10) | copy-start | bytes 4718596
  7.2 2.3 %copy-start.11 = (s32[16]{0:T(128)S(1)}, s32[16]{0:T(128)}, u32[]{:S(2)}) copy-start(s32[16]{0:T(128)} %param.12) | copy-start | bytes 196
  7.2 89.0 %all-gather.7.cloned.1.call-start = ((), (), s32[]{:S(2)}) async-start(), calls=%async_computation.2 | async-start | bytes 13369344 | tf_op jit(solution)/shard_map/all_gather | solution.py:66
  9.4 125.4 %all-gather.9.cloned.1.call-start = ((), (), s32[]{:S(2)}) async-start(), calls=%async_computation.3 | async-start | bytes 6684672 | tf_op jit(solution)/shard_map/all_gather | solution.py:73
  11.5 12.4 %collective-permute-start.2 = (f32[24,4096]{1,0:T(8,128)S(1)}, f32[24,4096]{1,0:T(8,128)S(1)}, u32[]{:S(2)}, u32[]{:S(2)}) collective-permute-start(f32[24,4096]{1,0:T(8,128)S(1)} %get-tuple-element.42), channel_id=1, source_target_pairs={{0,8},{1,9},{2,10},{3,11},{4,12},{5,13},{6,14},{7,15},{8,0},{9,1},... | collective-permute-start | bytes 1179656 | tf_op jit(solution)/shard_map/ppermute | solution.py:57
  13.7 10.6 %collective-permute-start.3 = (f32[24,4096]{1,0:T(8,128)S(1)}, f32[24,4096]{1,0:T(8,128)S(1)}, u32[]{:S(2)}, u32[]{:S(2)}) collective-permute-start(f32[24,4096]{1,0:T(8,128)S(1)} %get-tuple-element.41), channel_id=1, source_target_pairs={{0,1},{1,0},{2,3},{3,2},{4,5},{5,4},{6,7},{7,6},{8,9},{9,8},{10,11... | collective-permute-start | bytes 1179656 | tf_op jit(solution)/shard_map/ppermute | solution.py:60
  33.4 2.0 %copy-start.10 = (s32[4]{0:T(128)S(1)}, s32[4]{0:T(128)}, u32[]{:S(2)}) copy-start(s32[4]{0:T(128)} %param.11) | copy-start | bytes 52
  39.7 48.3 %collective-permute-start = (f32[128,4096]{0,1:T(8,128)}, f32[128,4096]{0,1:T(8,128)}, u32[]{:S(2)}, u32[]{:S(2)}) collective-permute-start(f32[128,4096]{0,1:T(8,128)} %bitcast_add_fusion.3), channel_id=1, source_target_pairs={{0,8},{1,9},{2,10},{3,11},{4,12},{5,13},{6,14},{7,15},{8,0},{9,1},... | collective-permute-start | bytes 6291464 | tf_op jit(solution)/shard_map/ppermute | solution.py:58
  47.0 46.9 %collective-permute-start.1 = (f32[128,4096]{0,1:T(8,128)}, f32[128,4096]{0,1:T(8,128)}, u32[]{:S(2)}, u32[]{:S(2)}) collective-permute-start(f32[128,4096]{0,1:T(8,128)} %bitcast_add_fusion.2), channel_id=1, source_target_pairs={{0,1},{1,0},{2,3},{3,2},{4,5},{5,4},{6,7},{7,6},{8,9},{9,8},{10,11... | collective-permute-start | bytes 6291464 | tf_op jit(solution)/shard_map/ppermute | solution.py:61
  50.5 1.3 copy-start.1
  70.0 3.5 %copy-start = (f32[1,128,4096]{1,2,0:T(8,128)S(1)}, f32[1,128,4096]{1,2,0:T(8,128)}, u32[]{:S(2)}) copy-start(f32[1,128,4096]{1,2,0:T(8,128)} %copy.39) | copy-start | bytes 6291460
  70.0 3.4 %copy-start.3 = (f32[128,64,64]{0,2,1:T(8,128)S(1)}, f32[128,64,64]{0,2,1:T(8,128)}, u32[]{:S(2)}) copy-start(f32[128,64,64]{0,2,1:T(8,128)} %copy.29) | copy-start | bytes 6291460
  73.5 20.4 %copy-start.2 = (f32[1,128,4096]{1,2,0:T(8,128)S(1)}, f32[1,128,4096]{1,2,0:T(8,128)}, u32[]{:S(2)}) copy-start(f32[1,128,4096]{1,2,0:T(8,128)} %copy-done.1) | copy-start | bytes 6291460
  73.5 20.4 %copy-start.7 = (f32[128,64,64]{0,2,1:T(8,128)S(1)}, f32[128,64,64]{0,2,1:T(8,128)}, u32[]{:S(2)}) copy-start(f32[128,64,64]{0,2,1:T(8,128)} %copy.37) | copy-start | bytes 6291460
  75.0 21.1 %copy-start.4 = (f32[1,128,4096]{1,2,0:T(8,128)S(1)}, f32[1,128,4096]{1,2,0:T(8,128)}, u32[]{:S(2)}) copy-start(f32[1,128,4096]{1,2,0:T(8,128)} %bitcast_add_fusion.4) | copy-start | bytes 6291460
  96.2 9.5 %copy-start.5 = (f32[1,128,4096]{1,2,0:T(8,128)S(1)}, f32[1,128,4096]{1,2,0:T(8,128)}, u32[]{:S(2)}) copy-start(f32[1,128,4096]{1,2,0:T(8,128)} %bitcast_add_fusion.5) | copy-start | bytes 6291460
  105.7 29.2 %copy-start.6 = (f32[128,4096]{0,1:T(8,128)S(1)}, f32[128,4096]{0,1:T(8,128)}, u32[]{:S(2)}) copy-start(f32[128,4096]{0,1:T(8,128)} %fusion.11) | copy-start | bytes 6291460
  142.0 7.4 %copy-start.14 = (s32[8,2]{0,1:T(2,128)S(1)}, s32[8,2]{0,1:T(2,128)}, u32[]{:S(2)}) copy-start(s32[8,2]{0,1:T(2,128)} %param.13) | copy-start | bytes 196
  142.0 7.4 %copy-start.13 = (f32[200]{0:T(256)S(1)}, f32[200]{0:T(256)}, u32[]{:S(2)}) copy-start(f32[200]{0:T(256)} %param.14) | copy-start | bytes 2404
  142.0 14.1 %copy-start.12 = (f32[384]{0:T(512)S(1)}, f32[384]{0:T(512)}, u32[]{:S(2)}) copy-start(f32[384]{0:T(512)} %param.15) | copy-start | bytes 4612
  142.0 14.0 %all-to-all-start = ((f32[16,8,384]{2,1,0:T(8,128)}), f32[16,8,384]{2,1,0:T(8,128)S(1)}, u32[]{:S(2)}, u32[]{:S(2)}) async-start(f32[16,8,384]{2,1,0:T(8,128)} %bitcast.42), calls=%async_computation | async-start | bytes 393216 | tf_op jit(solution)/shard_map/all_to_all | solution.py:87
  156.0 0.7 copy-start.9
Sparse Core Ops, SparseCore 0:
  9.8 78.5 all-gather.6
  90.2 44.5 all-gather.8

commit v6 on v5

--- a/solution.py
+++ b/solution.py
@@ -83,9 +83,13 @@
     running = lax.cond(any_full, fourth, lambda acc: acc, running)
 
     ab = running.shape[1]
-    blocks = running.reshape(n_virt, pair_rows // n_virt, ab)
-    received = lax.all_to_all(blocks, "virt", 0, 0, tiled=False)
-    ladder = jnp.sum(received, axis=0)
+    side = 4
+    along_x = [[y + side * x for x in range(n_virt // side)] for y in range(side)]
+    along_y = [[side * x + y for y in range(side)] for x in range(n_virt // side)]
+    first = running.reshape(n_virt // side, pair_rows // (n_virt // side), ab)
+    first = jnp.sum(lax.all_to_all(first, "virt", 0, 0, axis_index_groups=along_x), axis=0)
+    second = first.reshape(side, first.shape[0] // side, ab)
+    ladder = jnp.sum(lax.all_to_all(second, "virt", 0, 0, axis_index_groups=along_y), axis=0)
 
     occ_range = jnp.arange(occ_energy.shape[0], dtype=jnp.int32)
     first_energy = jnp.sum(

time: 165 us -> 170 us (1.030)
  waiting for transfers between devices: 48.2 us -> 52.2 us
  starting transfers between devices: 14.6 us -> 16.4 us
    all_to_all x1 -> x2, waiting for transfers between devices: 6.39 us -> 10.2 us  [the longest x1 5.32 us: on_device(): lax.all_to_all(second, 'virt', 0, 0, axis_index_groups=along_y)]
    all_to_all x1 -> x2, starting transfers between devices: 7.41 us -> 9.18 us  [the longest x1 4.9 us: on_device(): lax.all_to_all(first, 'virt', 0, 0, axis_index_groups=along_x)]
  transfers between devices with their start and end apart: 7 -> 8, of which waited for: 6 -> 7; matrix products, arithmetic and copies ran while one was open for 42% -> 40% of each run, Pallas kernels for 0% -> 0%
where the time goes in v6:
time: 170 us
  waiting for transfers between devices  52.2 us (31%)
  local copies, waits for them, and re-layouts  37 us (22%)
  matrix products  26.4 us (16%)
  between operations  21.9 us (13%)
  starting transfers between devices  16.4 us (10%)
  other arithmetic  15.9 us (9%)
    dot_general x3, matrix products, tile_product(): lax.dot_general(amp_tile, int_rows, (((1,), (1,)), ((), ())), precision=p...  26.4 us
    all_gather x1, waiting for transfers between devices, on_device(): lax.all_gather(third_int, 'pair', axis=0, tiled=True)  19.4 us
    ppermute x1, waiting for transfers between devices, on_device(): recv_amp = lax.ppermute(send_amp, 'virt', perm)  13 us
    unnamed x35, local copies, waits for them, and re-layouts  11.3 us
    mul x5, local copies, waits for them, and re-layouts, symmetric_amps(): return amp_rows + flag.astype(jnp.float32) * swap_in_tile(amp_rows)  10 us
    slice x2, local copies, waits for them, and re-layouts, own_amps(): return symmetric_amps(amplitudes[slot], tile_flags[slot])  8.96 us
    add x4, other arithmetic, symmetric_amps(): return amp_rows + flag.astype(jnp.float32) * swap_in_tile(amp_rows)  8.21 us
    ppermute x1, waiting for transfers between devices, on_device(): lax.ppermute(symmetric_amps(amplitudes[3], tile_flags[3]), 'virt', perm_y)  5.91 us
  transfers between devices with their start and end apart: 8, of which 7 were waited for; matrix products, arithmetic and copies ran while one was open for 40% of the time, Pallas kernels for 0%

profile of v6, /device:TPU:2, one launch (start us, length us, event | category | flops | bytes accessed | tf_op | source)
XLA Modules:
  0.0 169.8 jit_solution(17591229181481691487)
XLA Ops:
  7.2 0.0 copy-start.8
  7.2 0.0 copy-start.11
  7.2 0.0 all-gather.7.cloned.1.call-start
  7.2 2.2 %slice.66 = f32[2,24,4096]{2,1,0:T(8,128)} slice(f32[4,24,4096]{2,1,0:T(8,128)} %param.10), slice={[0:2], [0:24], [0:4096]} | slice | bytes 1572864 | tf_op jit(solution)/shard_map/slice | solution.py:66
  9.4 0.0 all-gather.7.cloned.1.call-update
  9.4 0.0 all-gather.9.cloned.1.call-start
  9.5 0.6 dynamic_slice.27
  11.4 0.1 slice_bitcast_fusion.8
  11.4 2.2 %collective-permute-start.2 = (f32[24,4096]{1,0:T(8,128)S(1)}, f32[24,4096]{1,0:T(8,128)S(1)}, u32[]{:S(2)}, u32[]{:S(2)}) collective-permute-start(f32[24,4096]{1,0:T(8,128)S(1)} %get-tuple-element.42), channel_id=1, source_target_pairs={{0,8},{1,9},{2,10},{3,11},{4,12},{5,13},{6,14},{7,15},{8,0},{9,1},... | collective-permute-start | bytes 1179656 | tf_op jit(solution)/shard_map/ppermute | solution.py:57
  13.7 1.6 collective-permute-start.3
  15.2 0.1 fusion.27
  15.3 0.1 fusion.23
  15.4 0.7 dynamic_slice.25
  16.1 0.7 gather_fusion
  16.7 0.7 gather_fusion.1
  17.4 0.6 fusion.24
  18.0 0.7 gather_fusion.2
  18.7 0.6 dynamic_slice.26
  20.6 3.3 %collective-permute-done.2 = f32[24,4096]{1,0:T(8,128)S(1)} collective-permute-done((f32[24,4096]{1,0:T(8,128)S(1)}, f32[24,4096]{1,0:T(8,128)S(1)}, u32[]{:S(2)}, u32[]{:S(2)}) %collective-permute-start.2) | collective-permute-done | bytes 393248 | tf_op jit(solution)/shard_map/ppermute | solution.py:57
  23.9 0.3 collective-permute-done.3
  24.2 0.8 fusion.21
  25.0 0.0 all-gather.9.cloned.1.call-update
  25.1 8.3 %fusion.25 = (f32[1,128,4096]{2,1,0:T(8,128)}, f32[1,128,4096]{2,1,0:T(8,128)}, f32[1,128,4096]{2,1,0:T(8,128)}, f32[1,128,4096]{2,1,0:T(8,128)}, f32[1,128,4096]{2,1,0:T(8,128)}) fusion(f32[4,128,4096]{2,1,0:T(8,128)} %param.9, s32[]{:T(128)S(6)} %select_n.101), kind=kLoop, calls=%fused_computation.59 | loop fusion | bytes 20971524 | tf_op jit(solution)/shard_map/slice | solution.py:64
  33.4 1.9 %copy.41 = f32[1,128,4096]{1,2,0:T(8,128)S(1)} copy(f32[1,128,4096]{2,1,0:T(8,128)} %get-tuple-element.38) | data formatting | bytes 4194304
  35.3 0.7 fusion.26
  36.6 0.1 broadcast_multiply_fusion.2
  36.8 1.2 copy.33
  38.0 1.7 bitcast_add_fusion.3
  39.7 1.8 %collective-permute-start = (f32[128,4096]{0,1:T(8,128)}, f32[128,4096]{0,1:T(8,128)}, u32[]{:S(2)}, u32[]{:S(2)}) collective-permute-start(f32[128,4096]{0,1:T(8,128)} %bitcast_add_fusion.3), channel_id=1, source_target_pairs={{0,8},{1,9},{2,10},{3,11},{4,12},{5,13},{6,14},{7,15},{8,0},{9,1},... | collective-permute-start | bytes 6291464 | tf_op jit(solution)/shard_map/ppermute | solution.py:58
  41.4 1.9 %copy.42 = f32[1,128,4096]{1,2,0:T(8,128)S(1)} copy(f32[1,128,4096]{2,1,0:T(8,128)} %get-tuple-element.37) | data formatting | bytes 4194304
  44.1 0.1 broadcast_multiply_fusion.1
  44.2 1.2 copy.35
  45.4 1.6 bitcast_add_fusion.2
  47.0 1.6 collective-permute-start.1
  48.6 1.9 %copy.43 = f32[1,128,4096]{1,2,0:T(8,128)S(1)} copy(f32[1,128,4096]{2,1,0:T(8,128)} %get-tuple-element.36) | data formatting | bytes 4194304
  50.5 0.0 copy-start.1
  51.2 0.1 broadcast_multiply_fusion
  51.3 0.5 copy-done.1
  51.8 2.5 %copy.37 = f32[128,64,64]{0,2,1:T(8,128)} copy(f32[128,64,64]{0,1,2:T(8,128)S(1)} %bitcast.101) | data formatting | bytes 4194304 | tf_op jit(solution)/shard_map/mul | solution.py:15
  54.3 1.9 %copy.40 = f32[1,128,4096]{1,2,0:T(8,128)S(1)} copy(f32[1,128,4096]{2,1,0:T(8,128)} %get-tuple-element.39) | data formatting | bytes 4194304
  56.8 0.1 broadcast_multiply_fusion.3
  57.0 2.6 %copy.31 = f32[128,64,64]{0,2,1:T(8,128)} copy(f32[128,64,64]{0,1,2:T(8,128)S(1)} %bitcast.102) | data formatting | bytes 4194304 | tf_op jit(solution)/shard_map/mul | solution.py:15
  59.5 0.6 dynamic_slice.24
  60.1 3.0 %copy.39 = f32[1,128,4096]{1,2,0:T(8,128)} copy(f32[1,128,4096]{2,1,0:T(8,128)} %get-tuple-element.40) | data formatting | bytes 4194304
  63.7 1.8 %broadcast_multiply_fusion.4 = f32[1,128,4096]{1,2,0:T(8,128)S(1)} fusion(f32[1,128,4096]{1,2,0:T(8,128)} %copy.39, f32[]{:T(128)} %bitcast.7), kind=kLoop, calls=%fused_computation.30 | loop fusion | flops 524288 | bytes 4194308 | tf_op jit(solution)/shard_map/mul | solution.py:15
  65.5 2.5 %copy.29 = f32[128,64,64]{0,2,1:T(8,128)} copy(f32[128,64,64]{0,1,2:T(8,128)S(1)} %bitcast.103) | data formatting | bytes 4194304 | tf_op jit(solution)/shard_map/mul | solution.py:15
  70.0 3.4 %bitcast_add_fusion.4 = f32[1,128,4096]{1,2,0:T(8,128)} fusion(f32[1,128,4096]{1,2,0:T(8,128)S(1)} %copy.40, f32[128,64,64]{0,2,1:T(8,128)} %copy.31), kind=kLoop, calls=%fused_computation.19 | loop fusion | flops 524288 | bytes 6291456 | tf_op jit(solution)/shard_map/add | solution.py:15
  73.4 0.0 copy-done.3
  73.4 1.5 bitcast_add_fusion.5
  75.0 13.0 %collective-permute-done = f32[128,4096]{0,1:T(8,128)} collective-permute-done((f32[128,4096]{0,1:T(8,128)}, f32[128,4096]{0,1:T(8,128)}, u32[]{:S(2)}, u32[]{:S(2)}) %collective-permute-start) | collective-permute-done | bytes 2097184 | tf_op jit(solution)/shard_map/ppermute | solution.py:58
  88.0 5.9 %collective-permute-done.1 = f32[128,4096]{0,1:T(8,128)} collective-permute-done((f32[128,4096]{0,1:T(8,128)}, f32[128,4096]{0,1:T(8,128)}, u32[]{:S(2)}, u32[]{:S(2)}) %collective-permute-start.1) | collective-permute-done | bytes 2097184 | tf_op jit(solution)/shard_map/ppermute | solution.py:61
  93.9 0.0 copy-done.7
  93.9 2.3 %fusion.11 = f32[128,4096]{0,1:T(8,128)} fusion(f32[128,4096]{0,1:T(8,128)} %collective-permute-done, f32[128,4096]{0,1:T(8,128)} %collective-permute-done.1, f32[128,64,64]{0,2,1:T(8,128)S(1)} %copy-done.7, f32[1,128,4096]{1,2,0:T(8,128)S(1)} %copy-done.2, pred[]{:T(512)} %bitcast.21, pred[]{:T(512)} %bitcast.20), kind=kLoop, calls=%fused_computation.15 | loop fusion | flops 1572864 | bytes 10485762 | tf_op jit(solution)/shard_map/jit(_where)/select_n | solution.py:72
  96.2 9.5 %fusion.17 = f32[128,384]{1,0:T(8,128)S(1)} fusion(f32[2,384,4096]{2,1,0:T(8,128)} %all-gather.7.cloned.1.call-done, f32[1,128,4096]{1,2,0:T(8,128)S(1)} %copy-done.4, pred[]{:T(512)S(6)} %gt.29), kind=kOutput, calls=%fused_computation.23 | convolution fusion | flops 2415968256 | bytes 8585217 | tf_op jit(solution)/shard_map/dot_general | solution.py:19
  105.7 9.8 %fusion.14 = f32[128,384]{1,0:T(8,128)S(1)} fusion(f32[128,384]{1,0:T(8,128)S(1)} %fusion.17, f32[2,384,4096]{2,1,0:T(8,128)} %all-gather.7.cloned.1.call-done, f32[1,128,4096]{1,2,0:T(8,128)S(1)} %copy-done.5), kind=kOutput, calls=%fused_computation.22 | convolution fusion | flops 2415968256 | bytes 8781824 | tf_op jit(solution)/shard_map/dot_general | solution.py:19
  115.5 19.4 %all-gather.9.cloned.1.call-done = f32[384,4096]{1,0:T(8,128)} async-done(((f32[24,4096]{1,0:T(8,128)}), f32[384,4096]{1,0:T(8,128)}) %all-gather.9.cloned.1.call-update) | async-done | bytes 6291472 | tf_op jit(solution)/shard_map/all_gather | solution.py:73
  134.9 7.1 %fusion.20 = f32[128,384]{1,0:T(8,128)} fusion(f32[128,384]{1,0:T(8,128)S(1)} %fusion.14, f32[128,4096]{0,1:T(8,128)S(1)} %copy-done.6, f32[384,4096]{1,0:T(8,128)} %all-gather.9.cloned.1.call-done, pred[]{:T(512)S(6)} %or.7), kind=kOutput, calls=%fused_computation.25 | convolution fusion | flops 1208057856 | bytes 8781825 | tf_op jit(solution)/shard_map/dot_general | solution.py:19
  142.0 4.9 %all-to-all-start = ((f32[4,32,384]{2,1,0:T(8,128)}), f32[4,32,384]{2,1,0:T(8,128)S(1)}, u32[]{:S(2)}, u32[]{:S(2)}) async-start(f32[4,32,384]{2,1,0:T(8,128)} %bitcast.42), calls=%async_computation | async-start | bytes 393216 | tf_op jit(solution)/shard_map/all_to_all | solution.py:90
  146.9 4.9 %all-to-all-done = f32[4,32,384]{2,1,0:T(8,128)S(1)} async-done(((f32[4,32,384]{2,1,0:T(8,128)}), f32[4,32,384]{2,1,0:T(8,128)S(1)}, u32[]{:S(2)}, u32[]{:S(2)}) %all-to-all-start) | async-done | bytes 196640 | tf_op jit(solution)/shard_map/all_to_all | solution.py:90
  151.8 0.6 reduce_sum.36
  152.5 4.3 %all-to-all-start.1 = ((f32[4,8,384]{2,1,0:T(8,128)}), f32[4,8,384]{2,1,0:T(8,128)S(1)}, u32[]{:S(2)}, u32[]{:S(2)}) async-start(f32[4,8,384]{2,1,0:T(8,128)} %bitcast.43), calls=%async_computation.1 | async-start | bytes 98304 | tf_op jit(solution)/shard_map/all_to_all | solution.py:92
  156.7 0.2 select_reduce_fusion.1
  156.9 5.3 %all-to-all-done.1 = f32[4,8,384]{2,1,0:T(8,128)S(1)} async-done(((f32[4,8,384]{2,1,0:T(8,128)}), f32[4,8,384]{2,1,0:T(8,128)S(1)}, u32[]{:S(2)}, u32[]{:S(2)}) %all-to-all-start.1) | async-done | bytes 49184 | tf_op jit(solution)/shard_map/all_to_all | solution.py:92
  162.3 0.7 subtract_divide_fusion
  (30 shorter events, 0.1 us)
Async XLA Ops:
  7.2 4.2 %copy-start.8 = (f32[4,24,4096]{2,1,0:T(8,128)S(1)}, f32[4,24,4096]{2,1,0:T(8,128)}, u32[]{:S(2)}) copy-start(f32[4,24,4096]{2,1,0:T(8,128)} %param.10) | copy-start | bytes 4718596
  7.2 2.3 %copy-start.11 = (s32[16]{0:T(128)S(1)}, s32[16]{0:T(128)}, u32[]{:S(2)}) copy-start(s32[16]{0:T(128)} %param.12) | copy-start | bytes 196
  7.2 89.0 %all-gather.7.cloned.1.call-start = ((), (), s32[]{:S(2)}) async-start(), calls=%async_computation.3 | async-start | bytes 13369344 | tf_op jit(solution)/shard_map/all_gather | solution.py:66
  9.4 125.5 %all-gather.9.cloned.1.call-start = ((), (), s32[]{:S(2)}) async-start(), calls=%async_computation.4 | async-start | bytes 6684672 | tf_op jit(solution)/shard_map/all_gather | solution.py:73
  11.4 12.4 %collective-permute-start.2 = (f32[24,4096]{1,0:T(8,128)S(1)}, f32[24,4096]{1,0:T(8,128)S(1)}, u32[]{:S(2)}, u32[]{:S(2)}) collective-permute-start(f32[24,4096]{1,0:T(8,128)S(1)} %get-tuple-element.42), channel_id=1, source_target_pairs={{0,8},{1,9},{2,10},{3,11},{4,12},{5,13},{6,14},{7,15},{8,0},{9,1},... | collective-permute-start | bytes 1179656 | tf_op jit(solution)/shard_map/ppermute | solution.py:57
  13.7 10.6 %collective-permute-start.3 = (f32[24,4096]{1,0:T(8,128)S(1)}, f32[24,4096]{1,0:T(8,128)S(1)}, u32[]{:S(2)}, u32[]{:S(2)}) collective-permute-start(f32[24,4096]{1,0:T(8,128)S(1)} %get-tuple-element.41), channel_id=1, source_target_pairs={{0,1},{1,0},{2,3},{3,2},{4,5},{5,4},{6,7},{7,6},{8,9},{9,8},{10,11... | collective-permute-start | bytes 1179656 | tf_op jit(solution)/shard_map/ppermute | solution.py:60
  33.4 2.0 %copy-start.10 = (s32[4]{0:T(128)S(1)}, s32[4]{0:T(128)}, u32[]{:S(2)}) copy-start(s32[4]{0:T(128)} %param.11) | copy-start | bytes 52
  39.7 48.3 %collective-permute-start = (f32[128,4096]{0,1:T(8,128)}, f32[128,4096]{0,1:T(8,128)}, u32[]{:S(2)}, u32[]{:S(2)}) collective-permute-start(f32[128,4096]{0,1:T(8,128)} %bitcast_add_fusion.3), channel_id=1, source_target_pairs={{0,8},{1,9},{2,10},{3,11},{4,12},{5,13},{6,14},{7,15},{8,0},{9,1},... | collective-permute-start | bytes 6291464 | tf_op jit(solution)/shard_map/ppermute | solution.py:58
  47.0 46.9 %collective-permute-start.1 = (f32[128,4096]{0,1:T(8,128)}, f32[128,4096]{0,1:T(8,128)}, u32[]{:S(2)}, u32[]{:S(2)}) collective-permute-start(f32[128,4096]{0,1:T(8,128)} %bitcast_add_fusion.2), channel_id=1, source_target_pairs={{0,1},{1,0},{2,3},{3,2},{4,5},{5,4},{6,7},{7,6},{8,9},{9,8},{10,11... | collective-permute-start | bytes 6291464 | tf_op jit(solution)/shard_map/ppermute | solution.py:61
  50.5 1.3 copy-start.1
  70.0 3.5 %copy-start = (f32[1,128,4096]{1,2,0:T(8,128)S(1)}, f32[1,128,4096]{1,2,0:T(8,128)}, u32[]{:S(2)}) copy-start(f32[1,128,4096]{1,2,0:T(8,128)} %copy.39) | copy-start | bytes 6291460
  70.0 3.4 %copy-start.3 = (f32[128,64,64]{0,2,1:T(8,128)S(1)}, f32[128,64,64]{0,2,1:T(8,128)}, u32[]{:S(2)}) copy-start(f32[128,64,64]{0,2,1:T(8,128)} %copy.29) | copy-start | bytes 6291460
  73.4 20.5 %copy-start.2 = (f32[1,128,4096]{1,2,0:T(8,128)S(1)}, f32[1,128,4096]{1,2,0:T(8,128)}, u32[]{:S(2)}) copy-start(f32[1,128,4096]{1,2,0:T(8,128)} %copy-done.1) | copy-start | bytes 6291460
  73.4 20.5 %copy-start.7 = (f32[128,64,64]{0,2,1:T(8,128)S(1)}, f32[128,64,64]{0,2,1:T(8,128)}, u32[]{:S(2)}) copy-start(f32[128,64,64]{0,2,1:T(8,128)} %copy.37) | copy-start | bytes 6291460
  75.0 21.2 %copy-start.4 = (f32[1,128,4096]{1,2,0:T(8,128)S(1)}, f32[1,128,4096]{1,2,0:T(8,128)}, u32[]{:S(2)}) copy-start(f32[1,128,4096]{1,2,0:T(8,128)} %bitcast_add_fusion.4) | copy-start | bytes 6291460
  96.2 9.5 %copy-start.5 = (f32[1,128,4096]{1,2,0:T(8,128)S(1)}, f32[1,128,4096]{1,2,0:T(8,128)}, u32[]{:S(2)}) copy-start(f32[1,128,4096]{1,2,0:T(8,128)} %bitcast_add_fusion.5) | copy-start | bytes 6291460
  105.7 29.2 %copy-start.6 = (f32[128,4096]{0,1:T(8,128)S(1)}, f32[128,4096]{0,1:T(8,128)}, u32[]{:S(2)}) copy-start(f32[128,4096]{0,1:T(8,128)} %fusion.11) | copy-start | bytes 6291460
  142.0 4.9 %copy-start.14 = (s32[8,2]{0,1:T(2,128)S(1)}, s32[8,2]{0,1:T(2,128)}, u32[]{:S(2)}) copy-start(s32[8,2]{0,1:T(2,128)} %param.13) | copy-start | bytes 196
  142.0 14.7 %copy-start.13 = (f32[200]{0:T(256)S(1)}, f32[200]{0:T(256)}, u32[]{:S(2)}) copy-start(f32[200]{0:T(256)} %param.14) | copy-start | bytes 2404
  142.0 20.3 %copy-start.12 = (f32[384]{0:T(512)S(1)}, f32[384]{0:T(512)}, u32[]{:S(2)}) copy-start(f32[384]{0:T(512)} %param.15) | copy-start | bytes 4612
  142.0 9.8 %all-to-all-start = ((f32[4,32,384]{2,1,0:T(8,128)}), f32[4,32,384]{2,1,0:T(8,128)S(1)}, u32[]{:S(2)}, u32[]{:S(2)}) async-start(f32[4,32,384]{2,1,0:T(8,128)} %bitcast.42), calls=%async_computation | async-start | bytes 393216 | tf_op jit(solution)/shard_map/all_to_all | solution.py:90
  152.5 9.8 %all-to-all-start.1 = ((f32[4,8,384]{2,1,0:T(8,128)}), f32[4,8,384]{2,1,0:T(8,128)S(1)}, u32[]{:S(2)}, u32[]{:S(2)}) async-start(f32[4,8,384]{2,1,0:T(8,128)} %bitcast.43), calls=%async_computation.1 | async-start | bytes 98304 | tf_op jit(solution)/shard_map/all_to_all | solution.py:92
  162.3 0.7 copy-start.9
Sparse Core Ops, SparseCore 0:
  9.8 78.5 all-gather.6
  90.2 44.6 all-gather.8

commit v7 on v5

--- a/solution.py
+++ b/solution.py
@@ -1,9 +1,63 @@
 import jax
 import jax.numpy as jnp
 from jax import lax
+from jax.experimental import pallas as pl
+from jax.experimental.pallas import tpu as pltpu
 from jax.sharding import PartitionSpec as P
 
 TILE = 64
+CHUNK = 1024
+
+
+def _split(x):
+    hi = x.astype(jnp.bfloat16)
+    lo = (x - hi.astype(jnp.float32)).astype(jnp.bfloat16)
+    return hi, lo
+
+
+def _three_pass_kernel(init_ref, a_ref, g_ref, o_ref, acc_ref):
+    step = pl.program_id(0)
+
+    @pl.when(step == 0)
+    def _():
+        acc_ref[...] = init_ref[...]
+
+    a_hi, a_lo = _split(a_ref[...])
+    g_hi, g_lo = _split(g_ref[...])
+    dims = (((1,), (1,)), ((), ()))
+
+    def dot(x, y):
+        return lax.dot_general(x, y, dims, preferred_element_type=jnp.float32)
+
+    acc_ref[...] += dot(a_hi, g_hi) + (dot(a_hi, g_lo) + dot(a_lo, g_hi))
+
+    @pl.when(step == pl.num_programs(0) - 1)
+    def _():
+        o_ref[...] = acc_ref[...]
+
+
+def three_pass_product(init, amp_tile, int_rows):
+    rows, depth = amp_tile.shape
+    cols = int_rows.shape[0]
+    steps = depth // CHUNK
+    return pl.pallas_call(
+        _three_pass_kernel,
+        grid=(steps,),
+        in_specs=[
+            pl.BlockSpec((rows, cols), lambda k: (0, 0)),
+            pl.BlockSpec((rows, CHUNK), lambda k: (0, k)),
+            pl.BlockSpec((cols, CHUNK), lambda k: (0, k)),
+        ],
+        out_specs=pl.BlockSpec((rows, cols), lambda k: (0, 0)),
+        out_shape=jax.ShapeDtypeStruct((rows, cols), jnp.float32),
+        scratch_shapes=[pltpu.VMEM((rows, cols), jnp.float32)],
+        compiler_params=pltpu.CompilerParams(dimension_semantics=("arbitrary",)),
+        cost_estimate=pl.CostEstimate(
+            flops=6 * rows * cols * depth,
+            bytes_accessed=4 * (rows * depth + cols * depth + 2 * rows * cols),
+            transcendentals=0,
+        ),
+    )(init, amp_tile, int_rows)
 
 
 def swap_in_tile(rows):
@@ -70,9 +124,11 @@
 
     third_int = jnp.where(take > 0, recv_int, jnp.where(take_y > 0, recv_int_y, integrals[2]))
     third_amp = jnp.where(take > 0, recv_amp, jnp.where(take_y > 0, recv_amp_y, own_amps(2)))
-    third = tile_product(third_amp, lax.all_gather(third_int, "pair", axis=0, tiled=True))
     third_live = (take > 0) | (take_y > 0) | (keep > 2)
-    running = running + jnp.where(third_live, third, jnp.zeros_like(third))
+    third_amp = jnp.where(third_live, third_amp, jnp.zeros_like(third_amp))
+    running = three_pass_product(
+        running, third_amp, lax.all_gather(third_int, "pair", axis=0, tiled=True)
+    )
 
     def fourth(acc):
         gathered = lax.all_gather(integrals[3], "pair", axis=0, tiled=True)

time: 165 us -> 165 us (level)
  waiting for transfers between devices: 48.2 us -> 30.1 us
  other arithmetic: 15.4 us -> 29.8 us
  Pallas kernels: 0 us -> 6.54 us
  matrix products: 26.4 us -> 21.4 us
  local copies, waits for them, and re-layouts: 36.9 us -> 38.7 us
    all_gather x1, waiting for transfers between devices: 19.4 us -> 1.91 us  [on_device(): lax.all_gather(third_int, 'pair', axis=0, tiled=True)]
    mul x5 -> x10, local copies, waits for them, and re-layouts: 10 us -> 24.6 us  [symmetric_amps(): return amp_rows + flag.astype(jnp.float32) * swap_in_tile(amp_rows)]
    mul x5 -> x4, other arithmetic: 2.36 us -> 11.6 us  [symmetric_amps(): return amp_rows + flag.astype(jnp.float32) * swap_in_tile(amp_rows)]
    slice x2 -> x1, local copies, waits for them, and re-layouts: 8.97 us -> 0.67 us  [own_amps(): return symmetric_amps(amplitudes[slot], tile_flags[slot])]
    ppermute x1, waiting for transfers between devices: 13 us -> 5.94 us  [on_device(): recv_amp = lax.ppermute(send_amp, 'virt', perm)]
    pallas_call x0 -> x1, Pallas kernels: none -> 6.54 us  [three_pass_product(): pl.pallas_call(_three_pass_kernel, grid=(steps,), in_specs=[pl.BlockSpec(...]
    ppermute x1, waiting for transfers between devices: 5.84 us -> 12 us  [on_device(): lax.ppermute(symmetric_amps(amplitudes[3], tile_flags[3]), 'virt', perm_y)]
    dot_general x3 -> x2, matrix products: 26.4 us -> 21.4 us  [tile_product(): lax.dot_general(amp_tile, int_rows, (((1,), (1,)), ((), ())), precision=p...]
  transfers between devices with their start and end apart: 7 -> 7, of which waited for: 6 -> 6; matrix products, arithmetic and copies ran while one was open for 42% -> 53% of each run, Pallas kernels for 0% -> 0%
where the time goes in v7:
time: 165 us; the launch traced here: 163 us
  local copies, waits for them, and re-layouts  38.7 us (23%)
  waiting for transfers between devices  30.1 us (18%)
  other arithmetic  29.8 us (18%)
  between operations  21.9 us (13%)
  matrix products  21.4 us (13%)
  starting transfers between devices  14.6 us (9%)
  Pallas kernels  6.54 us (4%)
    mul x10, local copies, waits for them, and re-layouts, symmetric_amps(): return amp_rows + flag.astype(jnp.float32) * swap_in_tile(amp_rows)  24.6 us
    dot_general x2, matrix products, tile_product(): lax.dot_general(amp_tile, int_rows, (((1,), (1,)), ((), ())), precision=p...  21.4 us
    add x4, other arithmetic, symmetric_amps(): return amp_rows + flag.astype(jnp.float32) * swap_in_tile(amp_rows)  12.1 us
    ppermute x1, waiting for transfers between devices, on_device(): lax.ppermute(symmetric_amps(amplitudes[3], tile_flags[3]), 'virt', perm_y)  12 us
    mul x4, other arithmetic, symmetric_amps(): return amp_rows + flag.astype(jnp.float32) * swap_in_tile(amp_rows)  11.6 us
    all_to_all x1, starting transfers between devices, on_device(): received = lax.all_to_all(blocks, 'virt', 0, 0, tiled=False)  7.41 us
    unnamed x27, local copies, waits for them, and re-layouts  6.76 us
    pallas_call x1, Pallas kernels, three_pass_product(): pl.pallas_call(_three_pass_kernel, grid=(steps,), in_specs=[pl.BlockSpec(...  6.54 us
  transfers between devices with their start and end apart: 7, of which 6 were waited for; matrix products, arithmetic and copies ran while one was open for 53% of the time, Pallas kernels for 0%

profile of v7, /device:TPU:2, one launch (start us, length us, event | category | flops | bytes accessed | tf_op | source)
XLA Modules:
  0.0 163.0 jit_solution(17202847038643999364)
XLA Ops:
  7.2 0.0 copy-start.5
  7.2 0.0 copy-start.8
  7.2 0.0 all-gather.7.cloned.1.call-start
  7.2 2.2 %slice.66 = f32[2,24,4096]{2,1,0:T(8,128)} slice(f32[4,24,4096]{2,1,0:T(8,128)} %param.10), slice={[0:2], [0:24], [0:4096]} | slice | bytes 1572864 | tf_op jit(solution)/shard_map/slice | solution.py:120
  9.4 0.0 all-gather.7.cloned.1.call-update
  9.5 0.0 all-gather.9.cloned.1.call-start
  9.5 0.0 copy-done.8
  9.5 0.6 dynamic_slice.27
  11.4 0.0 copy-done.5
  11.4 0.1 slice_bitcast_fusion.8
  11.5 0.0 copy-start.7
  11.5 2.2 %collective-permute-start.2 = (f32[24,4096]{1,0:T(8,128)S(1)}, f32[24,4096]{1,0:T(8,128)S(1)}, u32[]{:S(2)}, u32[]{:S(2)}) collective-permute-start(f32[24,4096]{1,0:T(8,128)S(1)} %get-tuple-element.42), channel_id=1, source_target_pairs={{0,8},{1,9},{2,10},{3,11},{4,12},{5,13},{6,14},{7,15},{8,0},{9,1},... | collective-permute-start | bytes 1179656 | tf_op jit(solution)/shard_map/ppermute | solution.py:111
  13.7 1.6 collective-permute-start.3
  15.3 0.1 fusion.26
  15.4 0.1 fusion.23
  15.4 0.6 dynamic_slice.25
  16.0 0.7 gather_fusion
  16.7 0.7 gather_fusion.1
  17.4 0.6 fusion.24
  18.0 0.7 gather_fusion.2
  18.7 0.6 dynamic_slice.26
  20.5 3.5 %collective-permute-done.2 = f32[24,4096]{1,0:T(8,128)S(1)} collective-permute-done((f32[24,4096]{1,0:T(8,128)S(1)}, f32[24,4096]{1,0:T(8,128)S(1)}, u32[]{:S(2)}, u32[]{:S(2)}) %collective-permute-start.2) | collective-permute-done | bytes 393248 | tf_op jit(solution)/shard_map/ppermute | solution.py:111
  23.9 0.3 collective-permute-done.3
  24.3 0.8 fusion.21
  25.1 0.0 all-gather.9.cloned.1.call-update
  25.1 0.0 copy-done.7
  25.1 0.7 fusion.25
  27.1 7.9 %slice_multiply_fusion.1 = (f32[1,128,4096]{2,1,0:T(8,128)}, f32[1,128,4096]{2,1,0:T(8,128)}, f32[1,128,4096]{2,1,0:T(8,128)}, f32[1,128,4096]{2,1,0:T(8,128)}, f32[1,128,4096]{2,1,0:T(8,128)S(1)}) fusion(f32[4,128,4096]{2,1,0:T(8,128)} %param.9, f32[]{:T(128)} %bitcast.35, f32[]{:T(128)} %bitcast.30, s32[]{:T(128)S(6)} %select_n.101), kind=kLoop, calls=%fused_computation.23 | loop fusion | flops 1048576 | bytes 20971532 | tf_op jit(solution)/shard_map/mul | solution.py:69
  35.0 1.8 %copy.49 = f32[1,128,4096]{1,2,0:T(8,128)} copy(f32[1,128,4096]{2,1,0:T(8,128)S(1)} %get-tuple-element.40) | data formatting | bytes 4194304
  37.4 1.8 %broadcast_multiply_fusion = f32[1,128,4096]{1,2,0:T(8,128)S(1)} fusion(f32[1,128,4096]{1,2,0:T(8,128)} %copy.49, f32[]{:T(128)} %bitcast.25), kind=kLoop, calls=%fused_computation.27 | loop fusion | flops 524288 | bytes 4194308 | tf_op jit(solution)/shard_map/mul | solution.py:69
  39.2 2.5 %copy.38 = f32[128,64,64]{0,2,1:T(8,128)} copy(f32[128,64,64]{0,1,2:T(8,128)S(1)} %bitcast.95) | data formatting | bytes 4194304 | tf_op jit(solution)/shard_map/mul | solution.py:69
  41.7 2.9 %copy.39 = f32[128,4096]{1,0:T(8,128)} copy(f32[128,4096]{0,1:T(8,128)} %bitcast.96) | data formatting | bytes 4194304 | tf_op jit(solution)/shard_map/mul | solution.py:69
  44.6 3.1 %bitcast_add_fusion.3 = f32[128,4096]{1,0:T(8,128)} fusion(f32[128,4096]{1,0:T(8,128)} %copy.39, f32[1,128,4096]{2,1,0:T(8,128)S(1)} %get-tuple-element.40), kind=kLoop, calls=%fused_computation.18 | loop fusion | flops 524288 | bytes 6291456 | tf_op jit(solution)/shard_map/add | solution.py:69
  47.7 1.8 %collective-permute-start = (f32[128,4096]{1,0:T(8,128)}, f32[128,4096]{1,0:T(8,128)}, u32[]{:S(2)}, u32[]{:S(2)}) collective-permute-start(f32[128,4096]{1,0:T(8,128)} %bitcast_add_fusion.3), channel_id=1, source_target_pairs={{0,8},{1,9},{2,10},{3,11},{4,12},{5,13},{6,14},{7,15},{8,0},{9,1},... | collective-permute-start | bytes 6291464 | tf_op jit(solution)/shard_map/ppermute | solution.py:112
  49.5 2.0 %copy.40 = f32[1,128,4096]{1,2,0:T(8,128)S(1)} copy(f32[1,128,4096]{2,1,0:T(8,128)} %get-tuple-element.37) | data formatting | bytes 4194304 | tf_op jit(solution)/shard_map/mul | solution.py:69
  51.5 2.6 %copy.41 = f32[128,64,64]{0,2,1:T(8,128)} copy(f32[128,64,64]{0,1,2:T(8,128)S(1)} %bitcast.97) | data formatting | bytes 4194304 | tf_op jit(solution)/shard_map/mul | solution.py:69
  54.1 3.0 %copy.42 = f32[128,4096]{1,0:T(8,128)} copy(f32[128,4096]{0,1:T(8,128)} %bitcast.98) | data formatting | bytes 4194304 | tf_op jit(solution)/shard_map/mul | solution.py:69
  57.1 4.1 %bitcast_add_fusion.2 = f32[128,4096]{1,0:T(8,128)} fusion(f32[128,4096]{1,0:T(8,128)} %copy.42, f32[4,128,4096]{2,1,0:T(8,128)} %param.9), kind=kLoop, calls=%fused_computation.17 | loop fusion | flops 524288 | bytes 6291456 | tf_op jit(solution)/shard_map/add | solution.py:69
  61.2 1.5 collective-permute-start.1
  62.8 1.8 %copy.43 = f32[1,128,4096]{1,2,0:T(8,128)} copy(f32[1,128,4096]{2,1,0:T(8,128)S(1)} %copy-done.1) | data formatting | bytes 4194304 | tf_op jit(solution)/shard_map/mul | solution.py:69
  64.6 2.8 %copy.44 = f32[128,64,64]{0,2,1:T(8,128)S(1)} copy(f32[128,64,64]{0,1,2:T(8,128)} %bitcast.99) | data formatting | bytes 4194304 | tf_op jit(solution)/shard_map/mul | solution.py:69
  67.5 1.8 %copy.45 = f32[128,4096]{1,0:T(8,128)} copy(f32[128,4096]{0,1:T(8,128)S(1)} %bitcast.100) | data formatting | bytes 4194304 | tf_op jit(solution)/shard_map/mul | solution.py:69
  69.3 0.6 dynamic_slice.24
  69.9 1.9 %copy.47 = f32[1,128,4096]{1,2,0:T(8,128)S(1)} copy(f32[1,128,4096]{2,1,0:T(8,128)} %get-tuple-element.39) | data formatting | bytes 4194304
  72.4 0.1 broadcast_multiply_fusion.2
  72.6 2.5 %copy.33 = f32[128,64,64]{0,2,1:T(8,128)} copy(f32[128,64,64]{0,1,2:T(8,128)S(1)} %bitcast.101) | data formatting | bytes 4194304 | tf_op jit(solution)/shard_map/mul | solution.py:69
  75.1 3.0 %copy.48 = f32[1,128,4096]{1,2,0:T(8,128)} copy(f32[1,128,4096]{2,1,0:T(8,128)} %get-tuple-element.38) | data formatting | bytes 4194304
  78.7 1.8 %broadcast_multiply_fusion.1 = f32[1,128,4096]{1,2,0:T(8,128)S(1)} fusion(f32[1,128,4096]{1,2,0:T(8,128)} %copy.48, f32[]{:T(128)} %bitcast.14), kind=kLoop, calls=%fused_computation.28 | loop fusion | flops 524288 | bytes 4194308 | tf_op jit(solution)/shard_map/mul | solution.py:69
  80.6 2.5 %copy.35 = f32[128,64,64]{0,2,1:T(8,128)} copy(f32[128,64,64]{0,1,2:T(8,128)S(1)} %bitcast.102) | data formatting | bytes 4194304 | tf_op jit(solution)/shard_map/mul | solution.py:69
  85.1 3.4 %bitcast_add_fusion.5 = f32[1,128,4096]{1,2,0:T(8,128)} fusion(f32[1,128,4096]{1,2,0:T(8,128)S(1)} %copy.47, f32[128,64,64]{0,2,1:T(8,128)} %copy.33), kind=kLoop, calls=%fused_computation.22 | loop fusion | flops 524288 | bytes 6291456 | tf_op jit(solution)/shard_map/add | solution.py:69
  88.4 0.0 copy-done
  88.4 1.5 bitcast_add_fusion.4
  89.9 5.9 %collective-permute-done = f32[128,4096]{1,0:T(8,128)} collective-permute-done((f32[128,4096]{1,0:T(8,128)}, f32[128,4096]{1,0:T(8,128)}, u32[]{:S(2)}, u32[]{:S(2)}) %collective-permute-start) | collective-permute-done | bytes 2097184 | tf_op jit(solution)/shard_map/ppermute | solution.py:112
  95.9 12.0 %collective-permute-done.1 = f32[128,4096]{1,0:T(8,128)} collective-permute-done((f32[128,4096]{1,0:T(8,128)}, f32[128,4096]{1,0:T(8,128)}, u32[]{:S(2)}, u32[]{:S(2)}) %collective-permute-start.1) | collective-permute-done | bytes 2097184 | tf_op jit(solution)/shard_map/ppermute | solution.py:115
  107.9 3.6 %fusion.12.a_ref = f32[128,4096]{1,0:T(8,128)} fusion(f32[128,4096]{1,0:T(8,128)} %collective-permute-done, f32[128,4096]{1,0:T(8,128)} %collective-permute-done.1, f32[128,4096]{1,0:T(8,128)S(1)} %copy-done.4, f32[4,128,4096]{2,1,0:T(8,128)} %param.9, pred[]{:T(512)} %bitcast.21, pred[]{:T(512)} %bitcast.20, pred[]{:T(512)S(6)} %or.7), kind=kLoop, calls=%fused_computation.16 | loop fusion | flops 2097152 | bytes 10485763 | tf_op jit(solution)/shard_map/jit(_where)/select_n | solution.py:128
  111.6 11.0 %fusion.18 = f32[128,384]{1,0:T(8,128)S(1)} fusion(f32[2,384,4096]{2,1,0:T(8,128)} %all-gather.7.cloned.1.call-done, f32[1,128,4096]{1,2,0:T(8,128)} %bitcast_add_fusion.4, pred[]{:T(512)S(6)} %gt.29), kind=kOutput, calls=%fused_computation.26 | convolution fusion | flops 2415968256 | bytes 8585217 | tf_op jit(solution)/shard_map/dot_general | solution.py:73
  122.6 10.3 %fusion.15.init_ref = f32[128,384]{1,0:T(8,128)} fusion(f32[128,384]{1,0:T(8,128)S(1)} %fusion.18, f32[2,384,4096]{2,1,0:T(8,128)} %all-gather.7.cloned.1.call-done, f32[1,128,4096]{1,2,0:T(8,128)S(1)} %copy-done.3), kind=kOutput, calls=%fused_computation.25 | convolution fusion | flops 2415968256 | bytes 8781824 | tf_op jit(solution)/shard_map/dot_general | solution.py:73
  133.0 1.9 %all-gather.9.cloned.1.call-done.g_ref = f32[384,4096]{1,0:T(8,128)} async-done(((f32[24,4096]{1,0:T(8,128)}), f32[384,4096]{1,0:T(8,128)}) %all-gather.9.cloned.1.call-update) | async-done | bytes 6291472 | tf_op jit(solution)/shard_map/all_gather | solution.py:130
  134.9 6.5 %shard_map.86 = f32[128,384]{1,0:T(8,128)} custom-call(f32[128,384]{1,0:T(8,128)} %fusion.15.init_ref, f32[128,4096]{1,0:T(8,128)} %fusion.12.a_ref, f32[384,4096]{1,0:T(8,128)} %all-gather.9.cloned.1.call-done.g_ref), custom_call_target="tpu_custom_call" | custom-call | flops 1207959552 | bytes 8781824 | tf_op jit(solution)/shard_map/pallas_call | solution.py:43
  141.4 7.4 %all-to-all-start = ((f32[16,8,384]{2,1,0:T(8,128)}), f32[16,8,384]{2,1,0:T(8,128)S(1)}, u32[]{:S(2)}, u32[]{:S(2)}) async-start(f32[16,8,384]{2,1,0:T(8,128)} %bitcast.42), calls=%async_computation | async-start | bytes 393216 | tf_op jit(solution)/shard_map/all_to_all | solution.py:143
  148.9 0.2 select_reduce_fusion.1
  149.1 6.4 %all-to-all-done = f32[16,8,384]{2,1,0:T(8,128)S(1)} async-done(((f32[16,8,384]{2,1,0:T(8,128)}), f32[16,8,384]{2,1,0:T(8,128)S(1)}, u32[]{:S(2)}, u32[]{:S(2)}) %all-to-all-start) | async-done | bytes 196640 | tf_op jit(solution)/shard_map/all_to_all | solution.py:143
  155.5 0.0 copy-start.6
  155.5 0.7 subtract_divide_fusion
  (22 shorter events, 0.1 us)
Async XLA Ops:
  7.2 4.2 %copy-start.5 = (f32[4,24,4096]{2,1,0:T(8,128)S(1)}, f32[4,24,4096]{2,1,0:T(8,128)}, u32[]{:S(2)}) copy-start(f32[4,24,4096]{2,1,0:T(8,128)} %param.10) | copy-start | bytes 4718596
  7.2 2.3 %copy-start.8 = (s32[16]{0:T(128)S(1)}, s32[16]{0:T(128)}, u32[]{:S(2)}) copy-start(s32[16]{0:T(128)} %param.12) | copy-start | bytes 196
  7.2 104.4 %all-gather.7.cloned.1.call-start = ((), (), s32[]{:S(2)}) async-start(), calls=%async_computation.2 | async-start | bytes 13369344 | tf_op jit(solution)/shard_map/all_gather | solution.py:120
  9.5 125.4 %all-gather.9.cloned.1.call-start = ((), (), s32[]{:S(2)}) async-start(), calls=%async_computation.3 | async-start | bytes 6684672 | tf_op jit(solution)/shard_map/all_gather | solution.py:130
  11.5 13.6 %copy-start.7 = (s32[4]{0:T(128)S(1)}, s32[4]{0:T(128)}, u32[]{:S(2)}) copy-start(s32[4]{0:T(128)} %param.11) | copy-start | bytes 52
  11.5 12.4 %collective-permute-start.2 = (f32[24,4096]{1,0:T(8,128)S(1)}, f32[24,4096]{1,0:T(8,128)S(1)}, u32[]{:S(2)}, u32[]{:S(2)}) collective-permute-start(f32[24,4096]{1,0:T(8,128)S(1)} %get-tuple-element.42), channel_id=1, source_target_pairs={{0,8},{1,9},{2,10},{3,11},{4,12},{5,13},{6,14},{7,15},{8,0},{9,1},... | collective-permute-start | bytes 1179656 | tf_op jit(solution)/shard_map/ppermute | solution.py:111
  13.7 10.6 %collective-permute-start.3 = (f32[24,4096]{1,0:T(8,128)S(1)}, f32[24,4096]{1,0:T(8,128)S(1)}, u32[]{:S(2)}, u32[]{:S(2)}) collective-permute-start(f32[24,4096]{1,0:T(8,128)S(1)} %get-tuple-element.41), channel_id=1, source_target_pairs={{0,1},{1,0},{2,3},{3,2},{4,5},{5,4},{6,7},{7,6},{8,9},{9,8},{10,11... | collective-permute-start | bytes 1179656 | tf_op jit(solution)/shard_map/ppermute | solution.py:114
  47.7 48.2 %collective-permute-start = (f32[128,4096]{1,0:T(8,128)}, f32[128,4096]{1,0:T(8,128)}, u32[]{:S(2)}, u32[]{:S(2)}) collective-permute-start(f32[128,4096]{1,0:T(8,128)} %bitcast_add_fusion.3), channel_id=1, source_target_pairs={{0,8},{1,9},{2,10},{3,11},{4,12},{5,13},{6,14},{7,15},{8,0},{9,1},... | collective-permute-start | bytes 6291464 | tf_op jit(solution)/shard_map/ppermute | solution.py:112
  57.1 5.7 %copy-start.1 = (f32[1,128,4096]{2,1,0:T(8,128)S(1)}, f32[1,128,4096]{2,1,0:T(8,128)}, u32[]{:S(2)}) copy-start(f32[1,128,4096]{2,1,0:T(8,128)} %get-tuple-element.36) | copy-start | bytes 6291460
  61.2 46.7 %collective-permute-start.1 = (f32[128,4096]{1,0:T(8,128)}, f32[128,4096]{1,0:T(8,128)}, u32[]{:S(2)}, u32[]{:S(2)}) collective-permute-start(f32[128,4096]{1,0:T(8,128)} %bitcast_add_fusion.2), channel_id=1, source_target_pairs={{0,1},{1,0},{2,3},{3,2},{4,5},{5,4},{6,7},{7,6},{8,9},{9,8},{10,11... | collective-permute-start | bytes 6291464 | tf_op jit(solution)/shard_map/ppermute | solution.py:115
  85.0 3.4 %copy-start = (f32[1,128,4096]{1,2,0:T(8,128)S(1)}, f32[1,128,4096]{1,2,0:T(8,128)}, u32[]{:S(2)}) copy-start(f32[1,128,4096]{1,2,0:T(8,128)} %copy.48) | copy-start | bytes 6291460
  85.0 3.4 %copy-start.2 = (f32[128,64,64]{0,2,1:T(8,128)S(1)}, f32[128,64,64]{0,2,1:T(8,128)}, u32[]{:S(2)}) copy-start(f32[128,64,64]{0,2,1:T(8,128)} %copy.35) | copy-start | bytes 6291460
  88.4 19.5 %copy-start.4 = (f32[128,4096]{1,0:T(8,128)S(1)}, f32[128,4096]{1,0:T(8,128)}, u32[]{:S(2)}) copy-start(f32[128,4096]{1,0:T(8,128)} %copy.45) | copy-start | bytes 6291460
  111.6 11.0 %copy-start.3 = (f32[1,128,4096]{1,2,0:T(8,128)S(1)}, f32[1,128,4096]{1,2,0:T(8,128)}, u32[]{:S(2)}) copy-start(f32[1,128,4096]{1,2,0:T(8,128)} %bitcast_add_fusion.5) | copy-start | bytes 6291460
  141.4 7.4 %copy-start.11 = (s32[8,2]{0,1:T(2,128)S(1)}, s32[8,2]{0,1:T(2,128)}, u32[]{:S(2)}) copy-start(s32[8,2]{0,1:T(2,128)} %param.13) | copy-start | bytes 196
  141.4 7.5 %copy-start.10 = (f32[200]{0:T(256)S(1)}, f32[200]{0:T(256)}, u32[]{:S(2)}) copy-start(f32[200]{0:T(256)} %param.14) | copy-start | bytes 2404
  141.4 14.1 %copy-start.9 = (f32[384]{0:T(512)S(1)}, f32[384]{0:T(512)}, u32[]{:S(2)}) copy-start(f32[384]{0:T(512)} %param.15) | copy-start | bytes 4612
  141.4 14.0 %all-to-all-start = ((f32[16,8,384]{2,1,0:T(8,128)}), f32[16,8,384]{2,1,0:T(8,128)S(1)}, u32[]{:S(2)}, u32[]{:S(2)}) async-start(f32[16,8,384]{2,1,0:T(8,128)} %bitcast.42), calls=%async_computation | async-start | bytes 393216 | tf_op jit(solution)/shard_map/all_to_all | solution.py:143
  155.5 0.7 copy-start.6
Sparse Core Ops, SparseCore 0:
  9.8 78.5 all-gather.6
  90.2 44.5 all-gather.8

commit v8 on v7

--- a/solution.py
+++ b/solution.py
@@ -118,9 +118,12 @@
         return symmetric_amps(amplitudes[slot], tile_flags[slot])
 
     first_two = lax.all_gather(integrals[0:2], "pair", axis=1, tiled=True)
-    running = tile_product(own_amps(0), first_two[0], lax.Precision.HIGHEST)
-    second = tile_product(own_amps(1), first_two[1], lax.Precision.HIGHEST)
-    running = running + jnp.where(keep > 1, second, jnp.zeros_like(second))
+    second_amp = own_amps(1)
+    second_amp = jnp.where(keep > 1, second_amp, jnp.zeros_like(second_amp))
+    running = three_pass_product(
+        jnp.zeros((pair_rows, first_two.shape[1]), jnp.float32), own_amps(0), first_two[0]
+    )
+    running = three_pass_product(running, second_amp, first_two[1])
 
     third_int = jnp.where(take > 0, recv_int, jnp.where(take_y > 0, recv_int_y, integrals[2]))
     third_amp = jnp.where(take > 0, recv_amp, jnp.where(take_y > 0, recv_amp_y, own_amps(2)))

time: 165 us -> 172 us (1.042)
  local copies, waits for them, and re-layouts: 38.7 us -> 61.6 us
  matrix products: 21.4 us -> 0 us
  Pallas kernels: 6.54 us -> 19.7 us
  waiting for transfers between devices: 30.1 us -> 24.7 us
  other arithmetic: 29.8 us -> 27.3 us
    dot_general x2 -> x0, matrix products: 21.4 us -> none  [tile_product(): lax.dot_general(amp_tile, int_rows, (((1,), (1,)), ((), ())), precision=p...]
    mul x10 -> x14, local copies, waits for them, and re-layouts: 24.6 us -> 40.5 us  [symmetric_amps(): return amp_rows + flag.astype(jnp.float32) * swap_in_tile(amp_rows)]
    pallas_call x1 -> x3, Pallas kernels: 6.54 us -> 19.7 us  [three_pass_product(): pl.pallas_call(_three_pass_kernel, grid=(steps,), in_specs=[pl.BlockSpec(...]
    squeeze x0 -> x1, local copies, waits for them, and re-layouts: none -> 11.2 us  [on_device(): running = three_pass_product(running, second_amp, first_two[1])]
    add x4 -> x2, other arithmetic: 12.1 us -> 7.12 us  [symmetric_amps(): return amp_rows + flag.astype(jnp.float32) * swap_in_tile(amp_rows)]
    unnamed x27 -> x23, local copies, waits for them, and re-layouts: 6.76 us -> 1.85 us
    select_n x1, other arithmetic: 3.64 us -> 7.8 us  [on_device(): third_amp = jnp.where(third_live, third_amp, jnp.zeros_like(third_amp))]
    ppermute x1, waiting for transfers between devices: 5.94 us -> 2.93 us  [on_device(): recv_amp = lax.ppermute(send_amp, 'virt', perm)]
  transfers between devices with their start and end apart: 7 -> 7, of which waited for: 6 -> 5; matrix products, arithmetic and copies ran while one was open for 53% -> 51% of each run, Pallas kernels for 0% -> 8%
where the time goes in v8:
time: 172 us; the launch traced here: 170 us
  local copies, waits for them, and re-layouts  61.6 us (36%)
  other arithmetic  27.3 us (16%)
  waiting for transfers between devices  24.7 us (14%)
  between operations  21.9 us (13%)
  Pallas kernels  19.7 us (11%)
  starting transfers between devices  14.9 us (9%)
    mul x14, local copies, waits for them, and re-layouts, symmetric_amps(): return amp_rows + flag.astype(jnp.float32) * swap_in_tile(amp_rows)  40.5 us
    pallas_call x3, Pallas kernels, three_pass_product(): pl.pallas_call(_three_pass_kernel, grid=(steps,), in_specs=[pl.BlockSpec(...  19.7 us
    ppermute x1, waiting for transfers between devices, on_device(): lax.ppermute(symmetric_amps(amplitudes[3], tile_flags[3]), 'virt', perm_y)  11.8 us
    squeeze x1, local copies, waits for them, and re-layouts, on_device(): running = three_pass_product(running, second_amp, first_two[1])  11.2 us
    mul x2, other arithmetic, symmetric_amps(): return amp_rows + flag.astype(jnp.float32) * swap_in_tile(amp_rows)  9.89 us
    select_n x1, other arithmetic, on_device(): third_amp = jnp.where(third_live, third_amp, jnp.zeros_like(third_amp))  7.8 us
    all_to_all x1, starting transfers between devices, on_device(): received = lax.all_to_all(blocks, 'virt', 0, 0, tiled=False)  7.6 us
    add x2, other arithmetic, symmetric_amps(): return amp_rows + flag.astype(jnp.float32) * swap_in_tile(amp_rows)  7.12 us
  transfers between devices with their start and end apart: 7, of which 5 were waited for; matrix products, arithmetic and copies ran while one was open for 51% of the time, Pallas kernels for 8%

profile of v8, /device:TPU:2, one launch (start us, length us, event | category | flops | bytes accessed | tf_op | source)
XLA Modules:
  0.0 170.2 jit_solution(16117168727991317312)
XLA Ops:
  7.2 0.0 copy-start.4
  7.2 0.0 copy-start.7
  7.2 0.0 all-gather.7.cloned.1.call-start
  7.2 2.2 %slice.66 = f32[2,24,4096]{2,1,0:T(8,128)} slice(f32[4,24,4096]{2,1,0:T(8,128)} %param.10), slice={[0:2], [0:24], [0:4096]} | slice | bytes 1572864 | tf_op jit(solution)/shard_map/slice | solution.py:120
  9.4 0.0 all-gather.7.cloned.1.call-update
  9.4 0.0 all-gather.9.cloned.1.call-start
  9.5 0.6 dynamic_slice.27
  11.4 0.1 slice_bitcast_fusion.2
  11.5 0.0 copy-start.6
  11.5 2.2 %collective-permute-start.2 = (f32[24,4096]{1,0:T(8,128)S(1)}, f32[24,4096]{1,0:T(8,128)S(1)}, u32[]{:S(2)}, u32[]{:S(2)}) collective-permute-start(f32[24,4096]{1,0:T(8,128)S(1)} %get-tuple-element.47), channel_id=1, source_target_pairs={{0,8},{1,9},{2,10},{3,11},{4,12},{5,13},{6,14},{7,15},{8,0},{9,1},... | collective-permute-start | bytes 1179656 | tf_op jit(solution)/shard_map/ppermute | solution.py:111
  13.7 1.6 collective-permute-start.3
  15.3 0.1 fusion.17
  15.3 0.1 fusion.14
  15.4 0.7 dynamic_slice.25
  16.1 0.7 gather_fusion
  16.8 0.7 gather_fusion.1
  17.4 0.6 fusion.15
  18.1 0.7 gather_fusion.2
  18.7 0.6 dynamic_slice.26
  20.7 3.3 %collective-permute-done.2 = f32[24,4096]{1,0:T(8,128)S(1)} collective-permute-done((f32[24,4096]{1,0:T(8,128)S(1)}, f32[24,4096]{1,0:T(8,128)S(1)}, u32[]{:S(2)}, u32[]{:S(2)}) %collective-permute-start.2) | collective-permute-done | bytes 393248 | tf_op jit(solution)/shard_map/ppermute | solution.py:111
  23.9 0.3 collective-permute-done.3
  24.3 0.8 fusion.12
  25.1 0.0 all-gather.9.cloned.1.call-update
  25.1 0.0 copy-done.6
  25.1 0.7 fusion.16
  28.3 8.1 %slice_multiply_fusion.1 = (f32[1,128,4096]{2,1,0:T(8,128)}, f32[1,128,4096]{2,1,0:T(8,128)}, f32[1,128,4096]{2,1,0:T(8,128)}, f32[1,128,4096]{2,1,0:T(8,128)}, f32[1,128,4096]{2,1,0:T(8,128)S(1)}) fusion(f32[4,128,4096]{2,1,0:T(8,128)} %param.9, f32[]{:T(128)} %bitcast.35, f32[]{:T(128)} %bitcast.8, f32[]{:T(128)} %bitcast.15, f32[]{:T(128)} %bitcast.30, ...), kind=kLoop, calls=%fused_computation.20 | loop fusion | flops 2097152 | bytes 20971540 | tf_op jit(solution)/shard_map/mul | solution.py:69
  36.4 1.8 %copy.51 = f32[1,128,4096]{1,2,0:T(8,128)} copy(f32[1,128,4096]{2,1,0:T(8,128)S(1)} %get-tuple-element.45) | data formatting | bytes 4194304
  38.8 1.8 %broadcast_multiply_fusion = f32[1,128,4096]{1,2,0:T(8,128)S(1)} fusion(f32[1,128,4096]{1,2,0:T(8,128)} %copy.51, f32[]{:T(128)} %bitcast.25), kind=kLoop, calls=%fused_computation.24 | loop fusion | flops 524288 | bytes 4194308 | tf_op jit(solution)/shard_map/mul | solution.py:69
  40.6 2.5 %copy.42 = f32[128,64,64]{0,2,1:T(8,128)} copy(f32[128,64,64]{0,1,2:T(8,128)S(1)} %bitcast.83) | data formatting | bytes 4194304 | tf_op jit(solution)/shard_map/mul | solution.py:69
  43.1 3.0 %copy.43 = f32[128,4096]{1,0:T(8,128)} copy(f32[128,4096]{0,1:T(8,128)} %bitcast.84) | data formatting | bytes 4194304 | tf_op jit(solution)/shard_map/mul | solution.py:69
  46.1 3.2 %bitcast_add_fusion.3 = f32[128,4096]{1,0:T(8,128)} fusion(f32[128,4096]{1,0:T(8,128)} %copy.43, f32[1,128,4096]{2,1,0:T(8,128)S(1)} %get-tuple-element.45), kind=kLoop, calls=%fused_computation.16 | loop fusion | flops 524288 | bytes 6291456 | tf_op jit(solution)/shard_map/add | solution.py:69
  49.3 1.7 %collective-permute-start = (f32[128,4096]{1,0:T(8,128)}, f32[128,4096]{1,0:T(8,128)}, u32[]{:S(2)}, u32[]{:S(2)}) collective-permute-start(f32[128,4096]{1,0:T(8,128)} %bitcast_add_fusion.3), channel_id=1, source_target_pairs={{0,8},{1,9},{2,10},{3,11},{4,12},{5,13},{6,14},{7,15},{8,0},{9,1},... | collective-permute-start | bytes 6291464 | tf_op jit(solution)/shard_map/ppermute | solution.py:112
  51.0 1.9 %copy.44 = f32[1,128,4096]{1,2,0:T(8,128)S(1)} copy(f32[1,128,4096]{2,1,0:T(8,128)} %get-tuple-element.44) | data formatting | bytes 4194304 | tf_op jit(solution)/shard_map/mul | solution.py:69
  52.9 2.6 %copy.45 = f32[128,64,64]{0,2,1:T(8,128)} copy(f32[128,64,64]{0,1,2:T(8,128)S(1)} %bitcast.85) | data formatting | bytes 4194304 | tf_op jit(solution)/shard_map/mul | solution.py:69
  55.6 3.0 %copy.46 = f32[128,4096]{1,0:T(8,128)} copy(f32[128,4096]{0,1:T(8,128)} %bitcast.86) | data formatting | bytes 4194304 | tf_op jit(solution)/shard_map/mul | solution.py:69
  58.5 4.0 %bitcast_add_fusion.2 = f32[128,4096]{1,0:T(8,128)} fusion(f32[128,4096]{1,0:T(8,128)} %copy.46, f32[4,128,4096]{2,1,0:T(8,128)} %param.9), kind=kLoop, calls=%fused_computation.15 | loop fusion | flops 524288 | bytes 6291456 | tf_op jit(solution)/shard_map/add | solution.py:69
  62.5 1.7 %collective-permute-start.1 = (f32[128,4096]{1,0:T(8,128)}, f32[128,4096]{1,0:T(8,128)}, u32[]{:S(2)}, u32[]{:S(2)}) collective-permute-start(f32[128,4096]{1,0:T(8,128)} %bitcast_add_fusion.2), channel_id=1, source_target_pairs={{0,1},{1,0},{2,3},{3,2},{4,5},{5,4},{6,7},{7,6},{8,9},{9,8},{10,11... | collective-permute-start | bytes 6291464 | tf_op jit(solution)/shard_map/ppermute | solution.py:115
  64.2 0.0 copy-done.3
  64.2 1.8 %copy.34 = f32[1,128,4096]{1,2,0:T(8,128)} copy(f32[1,128,4096]{2,1,0:T(8,128)S(1)} %copy-done.3) | data formatting | bytes 4194304 | tf_op jit(solution)/shard_map/mul | solution.py:69
  66.1 4.2 %copy.35 = f32[128,64,64]{0,2,1:T(8,128)} copy(f32[128,64,64]{0,1,2:T(8,128)} %bitcast.87) | data formatting | bytes 4194304 | tf_op jit(solution)/shard_map/mul | solution.py:69
  70.3 3.1 %copy.36 = f32[128,4096]{1,0:T(8,128)} copy(f32[128,4096]{0,1:T(8,128)} %bitcast.88) | data formatting | bytes 4194304 | tf_op jit(solution)/shard_map/mul | solution.py:69
  73.4 0.0 copy-done.2
  73.4 1.8 %copy.37 = f32[1,128,4096]{1,2,0:T(8,128)} copy(f32[1,128,4096]{2,1,0:T(8,128)S(1)} %copy-done.2) | data formatting | bytes 4194304 | tf_op jit(solution)/shard_map/mul | solution.py:69
  75.2 4.2 %copy.38 = f32[128,64,64]{0,2,1:T(8,128)} copy(f32[128,64,64]{0,1,2:T(8,128)} %bitcast.89) | data formatting | bytes 4194304 | tf_op jit(solution)/shard_map/mul | solution.py:69
  79.5 3.1 %copy.39 = f32[128,4096]{1,0:T(8,128)} copy(f32[128,4096]{0,1:T(8,128)} %bitcast.90) | data formatting | bytes 4194304 | tf_op jit(solution)/shard_map/mul | solution.py:69
  82.6 1.9 %copy.47 = f32[1,128,4096]{1,2,0:T(8,128)} copy(f32[1,128,4096]{2,1,0:T(8,128)S(1)} %copy-done) | data formatting | bytes 4194304 | tf_op jit(solution)/shard_map/mul | solution.py:69
  84.5 4.2 %copy.48 = f32[128,64,64]{0,2,1:T(8,128)} copy(f32[128,64,64]{0,1,2:T(8,128)} %bitcast.91) | data formatting | bytes 4194304 | tf_op jit(solution)/shard_map/mul | solution.py:69
  88.6 3.1 %copy.49 = f32[128,4096]{1,0:T(8,128)} copy(f32[128,4096]{0,1:T(8,128)} %bitcast.92) | data formatting | bytes 4194304 | tf_op jit(solution)/shard_map/mul | solution.py:69
  91.7 0.6 dynamic_slice.24
  94.3 2.9 %collective-permute-done = f32[128,4096]{1,0:T(8,128)} collective-permute-done((f32[128,4096]{1,0:T(8,128)}, f32[128,4096]{1,0:T(8,128)}, u32[]{:S(2)}, u32[]{:S(2)}) %collective-permute-start) | collective-permute-done | bytes 2097184 | tf_op jit(solution)/shard_map/ppermute | solution.py:112
  97.2 11.8 %collective-permute-done.1 = f32[128,4096]{1,0:T(8,128)} collective-permute-done((f32[128,4096]{1,0:T(8,128)}, f32[128,4096]{1,0:T(8,128)}, u32[]{:S(2)}, u32[]{:S(2)}) %collective-permute-start.1) | collective-permute-done | bytes 2097184 | tf_op jit(solution)/shard_map/ppermute | solution.py:115
  109.0 0.0 copy-done.1
  109.0 7.8 %fusion.10 = (f32[128,4096]{1,0:T(8,128)}, f32[128,4096]{1,0:T(8,128)}, f32[128,4096]{1,0:T(8,128)}) fusion(f32[128,4096]{1,0:T(8,128)} %collective-permute-done, f32[128,4096]{1,0:T(8,128)} %collective-permute-done.1, f32[128,4096]{1,0:T(8,128)} %copy.49, f32[4,128,4096]{2,1,0:T(8,128)} %param.9, pred[]{:T(512)} %bitcast.21, pred[]{:T(512)} %bitcast.20, ...), kind=kLoop, calls=%fused_computation.14 | loop fusion | flops 3670016 | bytes 23068676 | tf_op jit(solution)/shard_map/jit(_where)/select_n | solution.py:131
  116.8 11.2 %slice_bitcast_fusion = (f32[384,4096]{1,0:T(8,128)}, f32[384,4096]{1,0:T(8,128)}) fusion(f32[2,384,4096]{2,1,0:T(8,128)} %all-gather.7.cloned.1.call-done), kind=kLoop, calls=%fused_computation.9 | loop fusion | bytes 25165824 | tf_op jit(solution)/shard_map/squeeze | solution.py:126
  128.0 0.7 broadcast_13_init_ref.2.init_ref
  128.7 6.6 %shard_map.86.init_ref = f32[128,384]{1,0:T(8,128)} custom-call(f32[128,384]{1,0:T(8,128)} %broadcast_13_init_ref.2.init_ref, f32[128,4096]{1,0:T(8,128)} %get-tuple-element.40.a_ref, f32[384,4096]{1,0:T(8,128)} %get-tuple-element.37.g_ref), custom_call_target="tpu_custom_call" | custom-call | flops 1207959552 | bytes 8781824 | tf_op jit(solution)/shard_map/pallas_call | solution.py:43
  135.3 6.5 %shard_map.87.init_ref = f32[128,384]{1,0:T(8,128)} custom-call(f32[128,384]{1,0:T(8,128)} %shard_map.86.init_ref, f32[128,4096]{1,0:T(8,128)} %get-tuple-element.39.a_ref, f32[384,4096]{1,0:T(8,128)} %get-tuple-element.36.g_ref), custom_call_target="tpu_custom_call" | custom-call | flops 1207959552 | bytes 8781824 | tf_op jit(solution)/shard_map/pallas_call | solution.py:43
  141.9 6.6 %shard_map.88 = f32[128,384]{1,0:T(8,128)} custom-call(f32[128,384]{1,0:T(8,128)} %shard_map.87.init_ref, f32[128,4096]{1,0:T(8,128)} %get-tuple-element.38.a_ref, f32[384,4096]{1,0:T(8,128)} %all-gather.9.cloned.1.call-done.g_ref), custom_call_target="tpu_custom_call" | custom-call | flops 1207959552 | bytes 8781824 | tf_op jit(solution)/shard_map/pallas_call | solution.py:43
  148.5 7.6 %all-to-all-start = ((f32[16,8,384]{2,1,0:T(8,128)}), f32[16,8,384]{2,1,0:T(8,128)S(1)}, u32[]{:S(2)}, u32[]{:S(2)}) async-start(f32[16,8,384]{2,1,0:T(8,128)} %bitcast.42), calls=%async_computation | async-start | bytes 393216 | tf_op jit(solution)/shard_map/all_to_all | solution.py:146
  156.1 0.0 copy-done.9
  156.1 0.2 select_reduce_fusion.1
  156.3 6.3 %all-to-all-done = f32[16,8,384]{2,1,0:T(8,128)S(1)} async-done(((f32[16,8,384]{2,1,0:T(8,128)}), f32[16,8,384]{2,1,0:T(8,128)S(1)}, u32[]{:S(2)}, u32[]{:S(2)}) %all-to-all-start) | async-done | bytes 196640 | tf_op jit(solution)/shard_map/all_to_all | solution.py:146
  162.7 0.0 copy-start.5
  162.7 0.7 subtract_divide_fusion
  (20 shorter events, 0.1 us)
Async XLA Ops:
  7.2 4.2 %copy-start.4 = (f32[4,24,4096]{2,1,0:T(8,128)S(1)}, f32[4,24,4096]{2,1,0:T(8,128)}, u32[]{:S(2)}) copy-start(f32[4,24,4096]{2,1,0:T(8,128)} %param.10) | copy-start | bytes 4718596
  7.2 2.3 %copy-start.7 = (s32[16]{0:T(128)S(1)}, s32[16]{0:T(128)}, u32[]{:S(2)}) copy-start(s32[16]{0:T(128)} %param.12) | copy-start | bytes 196
  7.2 109.6 %all-gather.7.cloned.1.call-start = ((), (), s32[]{:S(2)}) async-start(), calls=%async_computation.2 | async-start | bytes 13369344 | tf_op jit(solution)/shard_map/all_gather | solution.py:120
  9.4 132.4 %all-gather.9.cloned.1.call-start = ((), (), s32[]{:S(2)}) async-start(), calls=%async_computation.3 | async-start | bytes 6684672 | tf_op jit(solution)/shard_map/all_gather | solution.py:133
  11.5 13.6 %copy-start.6 = (s32[4]{0:T(128)S(1)}, s32[4]{0:T(128)}, u32[]{:S(2)}) copy-start(s32[4]{0:T(128)} %param.11) | copy-start | bytes 52
  11.5 12.4 %collective-permute-start.2 = (f32[24,4096]{1,0:T(8,128)S(1)}, f32[24,4096]{1,0:T(8,128)S(1)}, u32[]{:S(2)}, u32[]{:S(2)}) collective-permute-start(f32[24,4096]{1,0:T(8,128)S(1)} %get-tuple-element.47), channel_id=1, source_target_pairs={{0,8},{1,9},{2,10},{3,11},{4,12},{5,13},{6,14},{7,15},{8,0},{9,1},... | collective-permute-start | bytes 1179656 | tf_op jit(solution)/shard_map/ppermute | solution.py:111
  13.7 10.6 %collective-permute-start.3 = (f32[24,4096]{1,0:T(8,128)S(1)}, f32[24,4096]{1,0:T(8,128)S(1)}, u32[]{:S(2)}, u32[]{:S(2)}) collective-permute-start(f32[24,4096]{1,0:T(8,128)S(1)} %get-tuple-element.46), channel_id=1, source_target_pairs={{0,1},{1,0},{2,3},{3,2},{4,5},{5,4},{6,7},{7,6},{8,9},{9,8},{10,11... | collective-permute-start | bytes 1179656 | tf_op jit(solution)/shard_map/ppermute | solution.py:114
  49.3 47.9 %collective-permute-start = (f32[128,4096]{1,0:T(8,128)}, f32[128,4096]{1,0:T(8,128)}, u32[]{:S(2)}, u32[]{:S(2)}) collective-permute-start(f32[128,4096]{1,0:T(8,128)} %bitcast_add_fusion.3), channel_id=1, source_target_pairs={{0,8},{1,9},{2,10},{3,11},{4,12},{5,13},{6,14},{7,15},{8,0},{9,1},... | collective-permute-start | bytes 6291464 | tf_op jit(solution)/shard_map/ppermute | solution.py:112
  58.5 5.7 %copy-start.3 = (f32[1,128,4096]{2,1,0:T(8,128)S(1)}, f32[1,128,4096]{2,1,0:T(8,128)}, u32[]{:S(2)}) copy-start(f32[1,128,4096]{2,1,0:T(8,128)} %get-tuple-element.42) | copy-start | bytes 6291460
  62.5 46.5 %collective-permute-start.1 = (f32[128,4096]{1,0:T(8,128)}, f32[128,4096]{1,0:T(8,128)}, u32[]{:S(2)}, u32[]{:S(2)}) collective-permute-start(f32[128,4096]{1,0:T(8,128)} %bitcast_add_fusion.2), channel_id=1, source_target_pairs={{0,1},{1,0},{2,3},{3,2},{4,5},{5,4},{6,7},{7,6},{8,9},{9,8},{10,11... | collective-permute-start | bytes 6291464 | tf_op jit(solution)/shard_map/ppermute | solution.py:115
  70.3 3.1 %copy-start.2 = (f32[1,128,4096]{2,1,0:T(8,128)S(1)}, f32[1,128,4096]{2,1,0:T(8,128)}, u32[]{:S(2)}) copy-start(f32[1,128,4096]{2,1,0:T(8,128)} %get-tuple-element.43) | copy-start | bytes 6291460
  79.5 3.1 %copy-start = (f32[1,128,4096]{2,1,0:T(8,128)S(1)}, f32[1,128,4096]{2,1,0:T(8,128)}, u32[]{:S(2)}) copy-start(f32[1,128,4096]{2,1,0:T(8,128)} %get-tuple-element.41) | copy-start | bytes 6291460
  88.6 20.4 %copy-start.1 = (f32[128,4096]{1,0:T(8,128)S(1)}, f32[128,4096]{1,0:T(8,128)}, u32[]{:S(2)}) copy-start(f32[128,4096]{1,0:T(8,128)} %copy.36) | copy-start | bytes 6291460
  148.4 7.6 %copy-start.10 = (s32[8,2]{0,1:T(2,128)S(1)}, s32[8,2]{0,1:T(2,128)}, u32[]{:S(2)}) copy-start(s32[8,2]{0,1:T(2,128)} %param.13) | copy-start | bytes 196
  148.4 7.6 %copy-start.9 = (f32[200]{0:T(256)S(1)}, f32[200]{0:T(256)}, u32[]{:S(2)}) copy-start(f32[200]{0:T(256)} %param.14) | copy-start | bytes 2404
  148.4 14.2 %copy-start.8 = (f32[384]{0:T(512)S(1)}, f32[384]{0:T(512)}, u32[]{:S(2)}) copy-start(f32[384]{0:T(512)} %param.15) | copy-start | bytes 4612
  148.5 14.2 %all-to-all-start = ((f32[16,8,384]{2,1,0:T(8,128)}), f32[16,8,384]{2,1,0:T(8,128)S(1)}, u32[]{:S(2)}, u32[]{:S(2)}) async-start(f32[16,8,384]{2,1,0:T(8,128)} %bitcast.42), calls=%async_computation | async-start | bytes 393216 | tf_op jit(solution)/shard_map/all_to_all | solution.py:146
  162.7 0.7 copy-start.5
Sparse Core Ops, SparseCore 0:
  9.8 78.5 all-gather.6
  90.2 44.5 all-gather.8

commit v9 on v7

--- a/solution.py
+++ b/solution.py
@@ -15,21 +15,44 @@
     return hi, lo
 
 
-def _three_pass_kernel(init_ref, a_ref, g_ref, o_ref, acc_ref):
+def _split_kernel(a_ref, hi_ref, lo_ref):
+    hi, lo = _split(a_ref[...])
+    hi_ref[...] = hi
+    lo_ref[...] = lo
+
+
+def split_amps(amp_tile):
+    rows, depth = amp_tile.shape
+    block = pl.BlockSpec((rows, CHUNK), lambda k: (0, k))
+    half_type = jax.ShapeDtypeStruct((rows, depth), jnp.bfloat16)
+    return pl.pallas_call(
+        _split_kernel,
+        grid=(depth // CHUNK,),
+        in_specs=[block],
+        out_specs=[block, block],
+        out_shape=[half_type, half_type],
+        compiler_params=pltpu.CompilerParams(dimension_semantics=("arbitrary",)),
+        cost_estimate=pl.CostEstimate(
+            flops=3 * rows * depth, bytes_accessed=8 * rows * depth, transcendentals=0
+        ),
+    )(amp_tile)
+
+
+def _three_pass_kernel(init_ref, a_hi_ref, a_lo_ref, g_ref, o_ref, acc_ref):
     step = pl.program_id(0)
 
     @pl.when(step == 0)
     def _():
         acc_ref[...] = init_ref[...]
 
-    a_hi, a_lo = _split(a_ref[...])
+    a_hi = a_hi_ref[...]
     g_hi, g_lo = _split(g_ref[...])
     dims = (((1,), (1,)), ((), ()))
 
     def dot(x, y):
         return lax.dot_general(x, y, dims, preferred_element_type=jnp.float32)
 
-    acc_ref[...] += dot(a_hi, g_hi) + (dot(a_hi, g_lo) + dot(a_lo, g_hi))
+    acc_ref[...] += dot(a_hi, g_hi) + (dot(a_hi, g_lo) + dot(a_lo_ref[...], g_hi))
 
     @pl.when(step == pl.num_programs(0) - 1)
     def _():
@@ -39,13 +62,15 @@
 def three_pass_product(init, amp_tile, int_rows):
     rows, depth = amp_tile.shape
     cols = int_rows.shape[0]
-    steps = depth // CHUNK
+    a_hi, a_lo = split_amps(amp_tile)
+    amp_block = pl.BlockSpec((rows, CHUNK), lambda k: (0, k))
     return pl.pallas_call(
         _three_pass_kernel,
-        grid=(steps,),
+        grid=(depth // CHUNK,),
         in_specs=[
             pl.BlockSpec((rows, cols), lambda k: (0, 0)),
-            pl.BlockSpec((rows, CHUNK), lambda k: (0, k)),
+            amp_block,
+            amp_block,
             pl.BlockSpec((cols, CHUNK), lambda k: (0, k)),
         ],
         out_specs=pl.BlockSpec((rows, cols), lambda k: (0, 0)),
@@ -57,7 +82,7 @@
             bytes_accessed=4 * (rows * depth + cols * depth + 2 * rows * cols),
             transcendentals=0,
         ),
-    )(init, amp_tile, int_rows)
+    )(init, a_hi, a_lo, int_rows)
 
 
 def swap_in_tile(rows):

time: 165 us -> 166 us (level)
  Pallas kernels: 6.54 us -> 10.5 us
  waiting for transfers between devices: 30.1 us -> 27.7 us
    pallas_call x1 -> x2, Pallas kernels: 6.54 us -> 10.5 us  [the longest x1 6.61 us: three_pass_product(): pl.pallas_call(_three_pass_kernel, grid=(depth // CHUNK,), in_specs=[pl.B...]
    all_gather x1, waiting for transfers between devices: 1.91 us -> 0.01 us  [on_device(): lax.all_gather(third_int, 'pair', axis=0, tiled=True)]
  transfers between devices with their start and end apart: 7 -> 7, of which waited for: 6 -> 5; matrix products, arithmetic and copies ran while one was open for 53% -> 53% of each run, Pallas kernels for 0% -> 2%
where the time goes in v9:
time: 166 us; the launch traced here: 164 us
  local copies, waits for them, and re-layouts  38.8 us (23%)
  other arithmetic  30.6 us (18%)
  waiting for transfers between devices  27.7 us (17%)
  between operations  21.8 us (13%)
  matrix products  21.1 us (13%)
  starting transfers between devices  13.9 us (8%)
  Pallas kernels  10.5 us (6%)
    mul x10, local copies, waits for them, and re-layouts, symmetric_amps(): return amp_rows + flag.astype(jnp.float32) * swap_in_tile(amp_rows)  24.6 us
    dot_general x2, matrix products, tile_product(): lax.dot_general(amp_tile, int_rows, (((1,), (1,)), ((), ())), precision=p...  21.1 us
    add x4, other arithmetic, symmetric_amps(): return amp_rows + flag.astype(jnp.float32) * swap_in_tile(amp_rows)  12.2 us
    ppermute x1, waiting for transfers between devices, on_device(): lax.ppermute(symmetric_amps(amplitudes[3], tile_flags[3]), 'virt', perm_y)  11.8 us
    mul x4, other arithmetic, symmetric_amps(): return amp_rows + flag.astype(jnp.float32) * swap_in_tile(amp_rows)  11.6 us
    unnamed x27, local copies, waits for them, and re-layouts  6.77 us
    all_to_all x1, starting transfers between devices, on_device(): received = lax.all_to_all(blocks, 'virt', 0, 0, tiled=False)  6.63 us
    pallas_call x1, Pallas kernels, three_pass_product(): pl.pallas_call(_three_pass_kernel, grid=(depth // CHUNK,), in_specs=[pl.B...  6.61 us
  transfers between devices with their start and end apart: 7, of which 5 were waited for; matrix products, arithmetic and copies ran while one was open for 53% of the time, Pallas kernels for 2%

profile of v9, /device:TPU:2, one launch (start us, length us, event | category | flops | bytes accessed | tf_op | source)
XLA Modules:
  0.0 164.3 jit_solution(11638844514821611438)
XLA Ops:
  7.2 0.0 copy-start.5
  7.2 0.0 copy-start.8
  7.2 0.0 all-gather.7.cloned.1.call-start
  7.2 2.2 %slice.66 = f32[2,24,4096]{2,1,0:T(8,128)} slice(f32[4,24,4096]{2,1,0:T(8,128)} %param.10), slice={[0:2], [0:24], [0:4096]} | slice | bytes 1572864 | tf_op jit(solution)/shard_map/slice | solution.py:145
  9.4 0.0 all-gather.7.cloned.1.call-update
  9.5 0.0 all-gather.9.cloned.1.call-start
  9.5 0.0 copy-done.8
  9.5 0.6 dynamic_slice.27
  11.4 0.0 copy-done.5
  11.4 0.1 slice_bitcast_fusion.8
  11.5 0.0 copy-start.7
  11.5 2.2 %collective-permute-start.2 = (f32[24,4096]{1,0:T(8,128)S(1)}, f32[24,4096]{1,0:T(8,128)S(1)}, u32[]{:S(2)}, u32[]{:S(2)}) collective-permute-start(f32[24,4096]{1,0:T(8,128)S(1)} %get-tuple-element.46), channel_id=1, source_target_pairs={{0,8},{1,9},{2,10},{3,11},{4,12},{5,13},{6,14},{7,15},{8,0},{9,1},... | collective-permute-start | bytes 1179656 | tf_op jit(solution)/shard_map/ppermute | solution.py:136
  13.7 1.6 collective-permute-start.3
  15.3 0.1 fusion.26
  15.3 0.1 fusion.23
  15.4 0.6 dynamic_slice.25
  16.0 0.7 gather_fusion
  16.7 0.7 gather_fusion.1
  17.4 0.6 fusion.24
  18.0 0.7 gather_fusion.2
  18.7 0.6 dynamic_slice.26
  20.5 3.4 %collective-permute-done.2 = f32[24,4096]{1,0:T(8,128)S(1)} collective-permute-done((f32[24,4096]{1,0:T(8,128)S(1)}, f32[24,4096]{1,0:T(8,128)S(1)}, u32[]{:S(2)}, u32[]{:S(2)}) %collective-permute-start.2) | collective-permute-done | bytes 393248 | tf_op jit(solution)/shard_map/ppermute | solution.py:136
  23.9 0.3 collective-permute-done.3
  24.3 0.8 fusion.21
  25.1 0.0 all-gather.9.cloned.1.call-update
  25.1 0.6 fusion.25
  27.0 7.8 %slice_multiply_fusion.1 = (f32[1,128,4096]{2,1,0:T(8,128)}, f32[1,128,4096]{2,1,0:T(8,128)}, f32[1,128,4096]{2,1,0:T(8,128)}, f32[1,128,4096]{2,1,0:T(8,128)}, f32[1,128,4096]{2,1,0:T(8,128)S(1)}) fusion(f32[4,128,4096]{2,1,0:T(8,128)} %param.9, f32[]{:T(128)} %bitcast.35, f32[]{:T(128)} %bitcast.30, s32[]{:T(128)S(6)} %select_n.101), kind=kLoop, calls=%fused_computation.23 | loop fusion | flops 1048576 | bytes 20971532 | tf_op jit(solution)/shard_map/mul | solution.py:94
  34.8 1.8 %copy.49 = f32[1,128,4096]{1,2,0:T(8,128)} copy(f32[1,128,4096]{2,1,0:T(8,128)S(1)} %get-tuple-element.44) | data formatting | bytes 4194304
  37.2 1.8 %broadcast_multiply_fusion = f32[1,128,4096]{1,2,0:T(8,128)S(1)} fusion(f32[1,128,4096]{1,2,0:T(8,128)} %copy.49, f32[]{:T(128)} %bitcast.25), kind=kLoop, calls=%fused_computation.27 | loop fusion | flops 524288 | bytes 4194308 | tf_op jit(solution)/shard_map/mul | solution.py:94
  39.0 2.5 %copy.38 = f32[128,64,64]{0,2,1:T(8,128)} copy(f32[128,64,64]{0,1,2:T(8,128)S(1)} %bitcast.95) | data formatting | bytes 4194304 | tf_op jit(solution)/shard_map/mul | solution.py:94
  41.5 2.9 %copy.39 = f32[128,4096]{1,0:T(8,128)} copy(f32[128,4096]{0,1:T(8,128)} %bitcast.96) | data formatting | bytes 4194304 | tf_op jit(solution)/shard_map/mul | solution.py:94
  44.4 3.1 %bitcast_add_fusion.3 = f32[128,4096]{1,0:T(8,128)} fusion(f32[128,4096]{1,0:T(8,128)} %copy.39, f32[1,128,4096]{2,1,0:T(8,128)S(1)} %get-tuple-element.44), kind=kLoop, calls=%fused_computation.18 | loop fusion | flops 524288 | bytes 6291456 | tf_op jit(solution)/shard_map/add | solution.py:94
  47.5 1.8 %collective-permute-start = (f32[128,4096]{1,0:T(8,128)}, f32[128,4096]{1,0:T(8,128)}, u32[]{:S(2)}, u32[]{:S(2)}) collective-permute-start(f32[128,4096]{1,0:T(8,128)} %bitcast_add_fusion.3), channel_id=1, source_target_pairs={{0,8},{1,9},{2,10},{3,11},{4,12},{5,13},{6,14},{7,15},{8,0},{9,1},... | collective-permute-start | bytes 6291464 | tf_op jit(solution)/shard_map/ppermute | solution.py:137
  49.4 2.0 %copy.40 = f32[1,128,4096]{1,2,0:T(8,128)S(1)} copy(f32[1,128,4096]{2,1,0:T(8,128)} %get-tuple-element.41) | data formatting | bytes 4194304 | tf_op jit(solution)/shard_map/mul | solution.py:94
  51.4 2.6 %copy.41 = f32[128,64,64]{0,2,1:T(8,128)} copy(f32[128,64,64]{0,1,2:T(8,128)S(1)} %bitcast.97) | data formatting | bytes 4194304 | tf_op jit(solution)/shard_map/mul | solution.py:94
  54.0 3.0 %copy.42 = f32[128,4096]{1,0:T(8,128)} copy(f32[128,4096]{0,1:T(8,128)} %bitcast.98) | data formatting | bytes 4194304 | tf_op jit(solution)/shard_map/mul | solution.py:94
  57.0 4.1 %bitcast_add_fusion.2 = f32[128,4096]{1,0:T(8,128)} fusion(f32[128,4096]{1,0:T(8,128)} %copy.42, f32[4,128,4096]{2,1,0:T(8,128)} %param.9), kind=kLoop, calls=%fused_computation.17 | loop fusion | flops 524288 | bytes 6291456 | tf_op jit(solution)/shard_map/add | solution.py:94
  61.1 1.5 collective-permute-start.1
  62.6 0.0 copy-done.1
  62.6 1.8 %copy.43 = f32[1,128,4096]{1,2,0:T(8,128)} copy(f32[1,128,4096]{2,1,0:T(8,128)S(1)} %copy-done.1) | data formatting | bytes 4194304 | tf_op jit(solution)/shard_map/mul | solution.py:94
  64.4 2.9 %copy.44 = f32[128,64,64]{0,2,1:T(8,128)S(1)} copy(f32[128,64,64]{0,1,2:T(8,128)} %bitcast.99) | data formatting | bytes 4194304 | tf_op jit(solution)/shard_map/mul | solution.py:94
  67.3 1.8 %copy.45 = f32[128,4096]{1,0:T(8,128)} copy(f32[128,4096]{0,1:T(8,128)S(1)} %bitcast.100) | data formatting | bytes 4194304 | tf_op jit(solution)/shard_map/mul | solution.py:94
  69.1 0.6 dynamic_slice.24
  69.8 1.9 %copy.47 = f32[1,128,4096]{1,2,0:T(8,128)S(1)} copy(f32[1,128,4096]{2,1,0:T(8,128)} %get-tuple-element.43) | data formatting | bytes 4194304
  72.3 0.1 broadcast_multiply_fusion.2
  72.5 2.5 %copy.33 = f32[128,64,64]{0,2,1:T(8,128)} copy(f32[128,64,64]{0,1,2:T(8,128)S(1)} %bitcast.101) | data formatting | bytes 4194304 | tf_op jit(solution)/shard_map/mul | solution.py:94
  75.0 3.0 %copy.48 = f32[1,128,4096]{1,2,0:T(8,128)} copy(f32[1,128,4096]{2,1,0:T(8,128)} %get-tuple-element.42) | data formatting | bytes 4194304
  78.6 1.8 %broadcast_multiply_fusion.1 = f32[1,128,4096]{1,2,0:T(8,128)S(1)} fusion(f32[1,128,4096]{1,2,0:T(8,128)} %copy.48, f32[]{:T(128)} %bitcast.14), kind=kLoop, calls=%fused_computation.28 | loop fusion | flops 524288 | bytes 4194308 | tf_op jit(solution)/shard_map/mul | solution.py:94
  80.4 2.5 %copy.35 = f32[128,64,64]{0,2,1:T(8,128)} copy(f32[128,64,64]{0,1,2:T(8,128)S(1)} %bitcast.102) | data formatting | bytes 4194304 | tf_op jit(solution)/shard_map/mul | solution.py:94
  85.0 3.4 %bitcast_add_fusion.5 = f32[1,128,4096]{1,2,0:T(8,128)} fusion(f32[1,128,4096]{1,2,0:T(8,128)S(1)} %copy.47, f32[128,64,64]{0,2,1:T(8,128)} %copy.33), kind=kLoop, calls=%fused_computation.22 | loop fusion | flops 524288 | bytes 6291456 | tf_op jit(solution)/shard_map/add | solution.py:94
  88.3 1.6 bitcast_add_fusion.4
  89.9 5.8 %collective-permute-done = f32[128,4096]{1,0:T(8,128)} collective-permute-done((f32[128,4096]{1,0:T(8,128)}, f32[128,4096]{1,0:T(8,128)}, u32[]{:S(2)}, u32[]{:S(2)}) %collective-permute-start) | collective-permute-done | bytes 2097184 | tf_op jit(solution)/shard_map/ppermute | solution.py:137
  95.7 11.8 %collective-permute-done.1 = f32[128,4096]{1,0:T(8,128)} collective-permute-done((f32[128,4096]{1,0:T(8,128)}, f32[128,4096]{1,0:T(8,128)}, u32[]{:S(2)}, u32[]{:S(2)}) %collective-permute-start.1) | collective-permute-done | bytes 2097184 | tf_op jit(solution)/shard_map/ppermute | solution.py:140
  107.5 4.3 %fusion.12.a_ref = f32[128,4096]{1,0:T(8,128)} fusion(f32[128,4096]{1,0:T(8,128)} %collective-permute-done, f32[128,4096]{1,0:T(8,128)} %collective-permute-done.1, f32[128,4096]{1,0:T(8,128)S(1)} %copy-done.4, f32[4,128,4096]{2,1,0:T(8,128)} %param.9, pred[]{:T(512)} %bitcast.21, pred[]{:T(512)} %bitcast.20, pred[]{:T(512)S(6)} %or.7), kind=kLoop, calls=%fused_computation.16 | loop fusion | flops 2097152 | bytes 10485763 | tf_op jit(solution)/shard_map/jit(_where)/select_n | solution.py:153
  111.9 3.9 %shard_map.86 = (bf16[128,4096]{1,0:T(8,128)(2,1)}, bf16[128,4096]{1,0:T(8,128)(2,1)}) custom-call(f32[128,4096]{1,0:T(8,128)} %fusion.12.a_ref), custom_call_target="tpu_custom_call" | custom-call | flops 1572864 | bytes 4194304 | tf_op jit(solution)/shard_map/pallas_call | solution.py:28
  115.8 11.0 %fusion.18 = f32[128,384]{1,0:T(8,128)S(1)} fusion(f32[2,384,4096]{2,1,0:T(8,128)} %all-gather.7.cloned.1.call-done, f32[1,128,4096]{1,2,0:T(8,128)} %bitcast_add_fusion.4, pred[]{:T(512)S(6)} %gt.29), kind=kOutput, calls=%fused_computation.26 | convolution fusion | flops 2415968256 | bytes 8585217 | tf_op jit(solution)/shard_map/dot_general | solution.py:98
  126.8 0.0 copy-done.3
  126.8 10.1 %fusion.15.init_ref = f32[128,384]{1,0:T(8,128)} fusion(f32[128,384]{1,0:T(8,128)S(1)} %fusion.18, f32[2,384,4096]{2,1,0:T(8,128)} %all-gather.7.cloned.1.call-done, f32[1,128,4096]{1,2,0:T(8,128)S(1)} %copy-done.3), kind=kOutput, calls=%fused_computation.25 | convolution fusion | flops 2415968256 | bytes 8781824 | tf_op jit(solution)/shard_map/dot_general | solution.py:98
  136.9 6.6 %shard_map.87 = f32[128,384]{1,0:T(8,128)} custom-call(f32[128,384]{1,0:T(8,128)} %fusion.15.init_ref, bf16[128,4096]{1,0:T(8,128)(2,1)} %get-tuple-element.23.a_hi_ref, bf16[128,4096]{1,0:T(8,128)(2,1)} %get-tuple-element.24.a_lo_ref, f32[384,4096]{1,0:T(8,128)} %all-gather.9.cloned.1.call-done.g_ref), custom_call_target="tpu_custom_call" | custom-call | flops 1207959552 | bytes 8781824 | tf_op jit(solution)/shard_map/pallas_call | solution.py:67
  143.5 6.6 %all-to-all-start = ((f32[16,8,384]{2,1,0:T(8,128)}), f32[16,8,384]{2,1,0:T(8,128)S(1)}, u32[]{:S(2)}, u32[]{:S(2)}) async-start(f32[16,8,384]{2,1,0:T(8,128)} %bitcast.42), calls=%async_computation | async-start | bytes 393216 | tf_op jit(solution)/shard_map/all_to_all | solution.py:168
  150.2 0.2 select_reduce_fusion.1
  150.4 6.3 %all-to-all-done = f32[16,8,384]{2,1,0:T(8,128)S(1)} async-done(((f32[16,8,384]{2,1,0:T(8,128)}), f32[16,8,384]{2,1,0:T(8,128)S(1)}, u32[]{:S(2)}, u32[]{:S(2)}) %all-to-all-start) | async-done | bytes 196640 | tf_op jit(solution)/shard_map/all_to_all | solution.py:168
  156.8 0.0 copy-start.6
  156.8 0.7 subtract_divide_fusion
  (23 shorter events, 0.1 us)
Async XLA Ops:
  7.2 4.2 %copy-start.5 = (f32[4,24,4096]{2,1,0:T(8,128)S(1)}, f32[4,24,4096]{2,1,0:T(8,128)}, u32[]{:S(2)}) copy-start(f32[4,24,4096]{2,1,0:T(8,128)} %param.10) | copy-start | bytes 4718596
  7.2 2.3 %copy-start.8 = (s32[16]{0:T(128)S(1)}, s32[16]{0:T(128)}, u32[]{:S(2)}) copy-start(s32[16]{0:T(128)} %param.12) | copy-start | bytes 196
  7.2 108.6 %all-gather.7.cloned.1.call-start = ((), (), s32[]{:S(2)}) async-start(), calls=%async_computation.2 | async-start | bytes 13369344 | tf_op jit(solution)/shard_map/all_gather | solution.py:145
  9.5 127.4 %all-gather.9.cloned.1.call-start = ((), (), s32[]{:S(2)}) async-start(), calls=%async_computation.3 | async-start | bytes 6684672 | tf_op jit(solution)/shard_map/all_gather | solution.py:155
  11.5 13.6 %copy-start.7 = (s32[4]{0:T(128)S(1)}, s32[4]{0:T(128)}, u32[]{:S(2)}) copy-start(s32[4]{0:T(128)} %param.11) | copy-start | bytes 52
  11.5 12.4 %collective-permute-start.2 = (f32[24,4096]{1,0:T(8,128)S(1)}, f32[24,4096]{1,0:T(8,128)S(1)}, u32[]{:S(2)}, u32[]{:S(2)}) collective-permute-start(f32[24,4096]{1,0:T(8,128)S(1)} %get-tuple-element.46), channel_id=1, source_target_pairs={{0,8},{1,9},{2,10},{3,11},{4,12},{5,13},{6,14},{7,15},{8,0},{9,1},... | collective-permute-start | bytes 1179656 | tf_op jit(solution)/shard_map/ppermute | solution.py:136
  13.7 10.6 %collective-permute-start.3 = (f32[24,4096]{1,0:T(8,128)S(1)}, f32[24,4096]{1,0:T(8,128)S(1)}, u32[]{:S(2)}, u32[]{:S(2)}) collective-permute-start(f32[24,4096]{1,0:T(8,128)S(1)} %get-tuple-element.45), channel_id=1, source_target_pairs={{0,1},{1,0},{2,3},{3,2},{4,5},{5,4},{6,7},{7,6},{8,9},{9,8},{10,11... | collective-permute-start | bytes 1179656 | tf_op jit(solution)/shard_map/ppermute | solution.py:139
  47.5 48.2 %collective-permute-start = (f32[128,4096]{1,0:T(8,128)}, f32[128,4096]{1,0:T(8,128)}, u32[]{:S(2)}, u32[]{:S(2)}) collective-permute-start(f32[128,4096]{1,0:T(8,128)} %bitcast_add_fusion.3), channel_id=1, source_target_pairs={{0,8},{1,9},{2,10},{3,11},{4,12},{5,13},{6,14},{7,15},{8,0},{9,1},... | collective-permute-start | bytes 6291464 | tf_op jit(solution)/shard_map/ppermute | solution.py:137
  57.0 5.7 %copy-start.1 = (f32[1,128,4096]{2,1,0:T(8,128)S(1)}, f32[1,128,4096]{2,1,0:T(8,128)}, u32[]{:S(2)}) copy-start(f32[1,128,4096]{2,1,0:T(8,128)} %get-tuple-element.40) | copy-start | bytes 6291460
  61.1 46.5 %collective-permute-start.1 = (f32[128,4096]{1,0:T(8,128)}, f32[128,4096]{1,0:T(8,128)}, u32[]{:S(2)}, u32[]{:S(2)}) collective-permute-start(f32[128,4096]{1,0:T(8,128)} %bitcast_add_fusion.2), channel_id=1, source_target_pairs={{0,1},{1,0},{2,3},{3,2},{4,5},{5,4},{6,7},{7,6},{8,9},{9,8},{10,11... | collective-permute-start | bytes 6291464 | tf_op jit(solution)/shard_map/ppermute | solution.py:140
  84.9 3.4 %copy-start = (f32[1,128,4096]{1,2,0:T(8,128)S(1)}, f32[1,128,4096]{1,2,0:T(8,128)}, u32[]{:S(2)}) copy-start(f32[1,128,4096]{1,2,0:T(8,128)} %copy.48) | copy-start | bytes 6291460
  84.9 3.4 %copy-start.2 = (f32[128,64,64]{0,2,1:T(8,128)S(1)}, f32[128,64,64]{0,2,1:T(8,128)}, u32[]{:S(2)}) copy-start(f32[128,64,64]{0,2,1:T(8,128)} %copy.35) | copy-start | bytes 6291460
  88.3 19.2 %copy-start.4 = (f32[128,4096]{1,0:T(8,128)S(1)}, f32[128,4096]{1,0:T(8,128)}, u32[]{:S(2)}) copy-start(f32[128,4096]{1,0:T(8,128)} %copy.45) | copy-start | bytes 6291460
  115.8 11.0 %copy-start.3 = (f32[1,128,4096]{1,2,0:T(8,128)S(1)}, f32[1,128,4096]{1,2,0:T(8,128)}, u32[]{:S(2)}) copy-start(f32[1,128,4096]{1,2,0:T(8,128)} %bitcast_add_fusion.5) | copy-start | bytes 6291460
  143.5 6.7 %copy-start.11 = (s32[8,2]{0,1:T(2,128)S(1)}, s32[8,2]{0,1:T(2,128)}, u32[]{:S(2)}) copy-start(s32[8,2]{0,1:T(2,128)} %param.13) | copy-start | bytes 196
  143.5 6.7 %copy-start.10 = (f32[200]{0:T(256)S(1)}, f32[200]{0:T(256)}, u32[]{:S(2)}) copy-start(f32[200]{0:T(256)} %param.14) | copy-start | bytes 2404
  143.5 13.3 %copy-start.9 = (f32[384]{0:T(512)S(1)}, f32[384]{0:T(512)}, u32[]{:S(2)}) copy-start(f32[384]{0:T(512)} %param.15) | copy-start | bytes 4612
  143.5 13.2 %all-to-all-start = ((f32[16,8,384]{2,1,0:T(8,128)}), f32[16,8,384]{2,1,0:T(8,128)S(1)}, u32[]{:S(2)}, u32[]{:S(2)}) async-start(f32[16,8,384]{2,1,0:T(8,128)} %bitcast.42), calls=%async_computation | async-start | bytes 393216 | tf_op jit(solution)/shard_map/all_to_all | solution.py:168
  156.8 0.7 copy-start.6
Sparse Core Ops, SparseCore 0:
  9.8 78.5 all-gather.6
  90.2 44.5 all-gather.8

commit v10 on v7

--- a/solution.py
+++ b/solution.py
@@ -6,7 +6,7 @@
 from jax.sharding import PartitionSpec as P
 
 TILE = 64
-CHUNK = 1024
+CHUNK = 512
 
 
 def _split(x):

time: 165 us -> 167 us (1.012)
  Pallas kernels: 6.54 us -> 8.47 us
    pallas_call x1, Pallas kernels: 6.54 us -> 8.47 us  [three_pass_product(): pl.pallas_call(_three_pass_kernel, grid=(steps,), in_specs=[pl.BlockSpec(...]
where the time goes in v10:
time: 167 us; the launch traced here: 165 us
  local copies, waits for them, and re-layouts  38.7 us (23%)
  waiting for transfers between devices  30.1 us (18%)
  other arithmetic  29.8 us (18%)
  between operations  21.9 us (13%)
  matrix products  21.4 us (13%)
  starting transfers between devices  14.6 us (9%)
  Pallas kernels  8.47 us (5%)
    mul x10, local copies, waits for them, and re-layouts, symmetric_amps(): return amp_rows + flag.astype(jnp.float32) * swap_in_tile(amp_rows)  24.6 us
    dot_general x2, matrix products, tile_product(): lax.dot_general(amp_tile, int_rows, (((1,), (1,)), ((), ())), precision=p...  21.4 us
    add x4, other arithmetic, symmetric_amps(): return amp_rows + flag.astype(jnp.float32) * swap_in_tile(amp_rows)  12.1 us
    ppermute x1, waiting for transfers between devices, on_device(): lax.ppermute(symmetric_amps(amplitudes[3], tile_flags[3]), 'virt', perm_y)  12 us
    mul x4, other arithmetic, symmetric_amps(): return amp_rows + flag.astype(jnp.float32) * swap_in_tile(amp_rows)  11.6 us
    pallas_call x1, Pallas kernels, three_pass_product(): pl.pallas_call(_three_pass_kernel, grid=(steps,), in_specs=[pl.BlockSpec(...  8.47 us
    all_to_all x1, starting transfers between devices, on_device(): received = lax.all_to_all(blocks, 'virt', 0, 0, tiled=False)  7.41 us
    unnamed x27, local copies, waits for them, and re-layouts  6.76 us
  transfers between devices with their start and end apart: 7, of which 6 were waited for; matrix products, arithmetic and copies ran while one was open for 53% of the time, Pallas kernels for 0%

profile of v10, /device:TPU:2, one launch (start us, length us, event | category | flops | bytes accessed | tf_op | source)
XLA Modules:
  0.0 165.0 jit_solution(3321822448331434169)
XLA Ops:
  7.2 0.0 copy-start.5
  7.2 0.0 all-gather.7.cloned.1.call-start
  7.2 2.2 %slice.66 = f32[2,24,4096]{2,1,0:T(8,128)} slice(f32[4,24,4096]{2,1,0:T(8,128)} %param.10), slice={[0:2], [0:24], [0:4096]} | slice | bytes 1572864 | tf_op jit(solution)/shard_map/slice | solution.py:120
  9.4 0.0 all-gather.7.cloned.1.call-update
  9.5 0.0 all-gather.9.cloned.1.call-start
  9.5 0.6 dynamic_slice.27
  11.4 0.0 copy-done.5
  11.4 0.1 slice_bitcast_fusion.8
  11.5 0.0 copy-start.7
  11.5 2.2 %collective-permute-start.2 = (f32[24,4096]{1,0:T(8,128)S(1)}, f32[24,4096]{1,0:T(8,128)S(1)}, u32[]{:S(2)}, u32[]{:S(2)}) collective-permute-start(f32[24,4096]{1,0:T(8,128)S(1)} %get-tuple-element.42), channel_id=1, source_target_pairs={{0,8},{1,9},{2,10},{3,11},{4,12},{5,13},{6,14},{7,15},{8,0},{9,1},... | collective-permute-start | bytes 1179656 | tf_op jit(solution)/shard_map/ppermute | solution.py:111
  13.7 1.6 collective-permute-start.3
  15.3 0.1 fusion.26
  15.4 0.1 fusion.23
  15.4 0.6 dynamic_slice.25
  16.0 0.7 gather_fusion
  16.7 0.7 gather_fusion.1
  17.4 0.6 fusion.24
  18.0 0.7 gather_fusion.2
  18.7 0.6 dynamic_slice.26
  20.5 3.5 %collective-permute-done.2 = f32[24,4096]{1,0:T(8,128)S(1)} collective-permute-done((f32[24,4096]{1,0:T(8,128)S(1)}, f32[24,4096]{1,0:T(8,128)S(1)}, u32[]{:S(2)}, u32[]{:S(2)}) %collective-permute-start.2) | collective-permute-done | bytes 393248 | tf_op jit(solution)/shard_map/ppermute | solution.py:111
  23.9 0.3 collective-permute-done.3
  24.3 0.8 fusion.21
  25.1 0.0 all-gather.9.cloned.1.call-update
  25.1 0.0 copy-done.7
  25.1 0.7 fusion.25
  27.1 7.9 %slice_multiply_fusion.1 = (f32[1,128,4096]{2,1,0:T(8,128)}, f32[1,128,4096]{2,1,0:T(8,128)}, f32[1,128,4096]{2,1,0:T(8,128)}, f32[1,128,4096]{2,1,0:T(8,128)}, f32[1,128,4096]{2,1,0:T(8,128)S(1)}) fusion(f32[4,128,4096]{2,1,0:T(8,128)} %param.9, f32[]{:T(128)} %bitcast.35, f32[]{:T(128)} %bitcast.30, s32[]{:T(128)S(6)} %select_n.101), kind=kLoop, calls=%fused_computation.23 | loop fusion | flops 1048576 | bytes 20971532 | tf_op jit(solution)/shard_map/mul | solution.py:69
  35.0 1.8 %copy.49 = f32[1,128,4096]{1,2,0:T(8,128)} copy(f32[1,128,4096]{2,1,0:T(8,128)S(1)} %get-tuple-element.40) | data formatting | bytes 4194304
  37.4 1.8 %broadcast_multiply_fusion = f32[1,128,4096]{1,2,0:T(8,128)S(1)} fusion(f32[1,128,4096]{1,2,0:T(8,128)} %copy.49, f32[]{:T(128)} %bitcast.25), kind=kLoop, calls=%fused_computation.27 | loop fusion | flops 524288 | bytes 4194308 | tf_op jit(solution)/shard_map/mul | solution.py:69
  39.2 2.5 %copy.38 = f32[128,64,64]{0,2,1:T(8,128)} copy(f32[128,64,64]{0,1,2:T(8,128)S(1)} %bitcast.95) | data formatting | bytes 4194304 | tf_op jit(solution)/shard_map/mul | solution.py:69
  41.7 2.9 %copy.39 = f32[128,4096]{1,0:T(8,128)} copy(f32[128,4096]{0,1:T(8,128)} %bitcast.96) | data formatting | bytes 4194304 | tf_op jit(solution)/shard_map/mul | solution.py:69
  44.6 3.1 %bitcast_add_fusion.3 = f32[128,4096]{1,0:T(8,128)} fusion(f32[128,4096]{1,0:T(8,128)} %copy.39, f32[1,128,4096]{2,1,0:T(8,128)S(1)} %get-tuple-element.40), kind=kLoop, calls=%fused_computation.18 | loop fusion | flops 524288 | bytes 6291456 | tf_op jit(solution)/shard_map/add | solution.py:69
  47.7 1.8 %collective-permute-start = (f32[128,4096]{1,0:T(8,128)}, f32[128,4096]{1,0:T(8,128)}, u32[]{:S(2)}, u32[]{:S(2)}) collective-permute-start(f32[128,4096]{1,0:T(8,128)} %bitcast_add_fusion.3), channel_id=1, source_target_pairs={{0,8},{1,9},{2,10},{3,11},{4,12},{5,13},{6,14},{7,15},{8,0},{9,1},... | collective-permute-start | bytes 6291464 | tf_op jit(solution)/shard_map/ppermute | solution.py:112
  49.5 2.0 %copy.40 = f32[1,128,4096]{1,2,0:T(8,128)S(1)} copy(f32[1,128,4096]{2,1,0:T(8,128)} %get-tuple-element.37) | data formatting | bytes 4194304 | tf_op jit(solution)/shard_map/mul | solution.py:69
  51.5 2.6 %copy.41 = f32[128,64,64]{0,2,1:T(8,128)} copy(f32[128,64,64]{0,1,2:T(8,128)S(1)} %bitcast.97) | data formatting | bytes 4194304 | tf_op jit(solution)/shard_map/mul | solution.py:69
  54.1 3.0 %copy.42 = f32[128,4096]{1,0:T(8,128)} copy(f32[128,4096]{0,1:T(8,128)} %bitcast.98) | data formatting | bytes 4194304 | tf_op jit(solution)/shard_map/mul | solution.py:69
  57.1 4.1 %bitcast_add_fusion.2 = f32[128,4096]{1,0:T(8,128)} fusion(f32[128,4096]{1,0:T(8,128)} %copy.42, f32[4,128,4096]{2,1,0:T(8,128)} %param.9), kind=kLoop, calls=%fused_computation.17 | loop fusion | flops 524288 | bytes 6291456 | tf_op jit(solution)/shard_map/add | solution.py:69
  61.2 1.5 collective-permute-start.1
  62.8 0.0 copy-done.1
  62.8 1.8 %copy.43 = f32[1,128,4096]{1,2,0:T(8,128)} copy(f32[1,128,4096]{2,1,0:T(8,128)S(1)} %copy-done.1) | data formatting | bytes 4194304 | tf_op jit(solution)/shard_map/mul | solution.py:69
  64.6 2.8 %copy.44 = f32[128,64,64]{0,2,1:T(8,128)S(1)} copy(f32[128,64,64]{0,1,2:T(8,128)} %bitcast.99) | data formatting | bytes 4194304 | tf_op jit(solution)/shard_map/mul | solution.py:69
  67.5 1.8 %copy.45 = f32[128,4096]{1,0:T(8,128)} copy(f32[128,4096]{0,1:T(8,128)S(1)} %bitcast.100) | data formatting | bytes 4194304 | tf_op jit(solution)/shard_map/mul | solution.py:69
  69.3 0.6 dynamic_slice.24
  69.9 1.9 %copy.47 = f32[1,128,4096]{1,2,0:T(8,128)S(1)} copy(f32[1,128,4096]{2,1,0:T(8,128)} %get-tuple-element.39) | data formatting | bytes 4194304
  72.4 0.1 broadcast_multiply_fusion.2
  72.6 2.5 %copy.33 = f32[128,64,64]{0,2,1:T(8,128)} copy(f32[128,64,64]{0,1,2:T(8,128)S(1)} %bitcast.101) | data formatting | bytes 4194304 | tf_op jit(solution)/shard_map/mul | solution.py:69
  75.1 3.0 %copy.48 = f32[1,128,4096]{1,2,0:T(8,128)} copy(f32[1,128,4096]{2,1,0:T(8,128)} %get-tuple-element.38) | data formatting | bytes 4194304
  78.7 1.8 %broadcast_multiply_fusion.1 = f32[1,128,4096]{1,2,0:T(8,128)S(1)} fusion(f32[1,128,4096]{1,2,0:T(8,128)} %copy.48, f32[]{:T(128)} %bitcast.14), kind=kLoop, calls=%fused_computation.28 | loop fusion | flops 524288 | bytes 4194308 | tf_op jit(solution)/shard_map/mul | solution.py:69
  80.6 2.5 %copy.35 = f32[128,64,64]{0,2,1:T(8,128)} copy(f32[128,64,64]{0,1,2:T(8,128)S(1)} %bitcast.102) | data formatting | bytes 4194304 | tf_op jit(solution)/shard_map/mul | solution.py:69
  85.1 3.4 %bitcast_add_fusion.5 = f32[1,128,4096]{1,2,0:T(8,128)} fusion(f32[1,128,4096]{1,2,0:T(8,128)S(1)} %copy.47, f32[128,64,64]{0,2,1:T(8,128)} %copy.33), kind=kLoop, calls=%fused_computation.22 | loop fusion | flops 524288 | bytes 6291456 | tf_op jit(solution)/shard_map/add | solution.py:69
  88.4 0.0 copy-done.2
  88.4 1.5 bitcast_add_fusion.4
  89.9 5.9 %collective-permute-done = f32[128,4096]{1,0:T(8,128)} collective-permute-done((f32[128,4096]{1,0:T(8,128)}, f32[128,4096]{1,0:T(8,128)}, u32[]{:S(2)}, u32[]{:S(2)}) %collective-permute-start) | collective-permute-done | bytes 2097184 | tf_op jit(solution)/shard_map/ppermute | solution.py:112
  95.9 12.0 %collective-permute-done.1 = f32[128,4096]{1,0:T(8,128)} collective-permute-done((f32[128,4096]{1,0:T(8,128)}, f32[128,4096]{1,0:T(8,128)}, u32[]{:S(2)}, u32[]{:S(2)}) %collective-permute-start.1) | collective-permute-done | bytes 2097184 | tf_op jit(solution)/shard_map/ppermute | solution.py:115
  107.9 3.6 %fusion.12.a_ref = f32[128,4096]{1,0:T(8,128)} fusion(f32[128,4096]{1,0:T(8,128)} %collective-permute-done, f32[128,4096]{1,0:T(8,128)} %collective-permute-done.1, f32[128,4096]{1,0:T(8,128)S(1)} %copy-done.4, f32[4,128,4096]{2,1,0:T(8,128)} %param.9, pred[]{:T(512)} %bitcast.21, pred[]{:T(512)} %bitcast.20, pred[]{:T(512)S(6)} %or.7), kind=kLoop, calls=%fused_computation.16 | loop fusion | flops 2097152 | bytes 10485763 | tf_op jit(solution)/shard_map/jit(_where)/select_n | solution.py:128
  111.6 11.0 %fusion.18 = f32[128,384]{1,0:T(8,128)S(1)} fusion(f32[2,384,4096]{2,1,0:T(8,128)} %all-gather.7.cloned.1.call-done, f32[1,128,4096]{1,2,0:T(8,128)} %bitcast_add_fusion.4, pred[]{:T(512)S(6)} %gt.29), kind=kOutput, calls=%fused_computation.26 | convolution fusion | flops 2415968256 | bytes 8585217 | tf_op jit(solution)/shard_map/dot_general | solution.py:73
  122.6 10.3 %fusion.15.init_ref = f32[128,384]{1,0:T(8,128)} fusion(f32[128,384]{1,0:T(8,128)S(1)} %fusion.18, f32[2,384,4096]{2,1,0:T(8,128)} %all-gather.7.cloned.1.call-done, f32[1,128,4096]{1,2,0:T(8,128)S(1)} %copy-done.3), kind=kOutput, calls=%fused_computation.25 | convolution fusion | flops 2415968256 | bytes 8781824 | tf_op jit(solution)/shard_map/dot_general | solution.py:73
  133.0 1.9 %all-gather.9.cloned.1.call-done.g_ref = f32[384,4096]{1,0:T(8,128)} async-done(((f32[24,4096]{1,0:T(8,128)}), f32[384,4096]{1,0:T(8,128)}) %all-gather.9.cloned.1.call-update) | async-done | bytes 6291472 | tf_op jit(solution)/shard_map/all_gather | solution.py:130
  134.9 8.5 %shard_map.86 = f32[128,384]{1,0:T(8,128)} custom-call(f32[128,384]{1,0:T(8,128)} %fusion.15.init_ref, f32[128,4096]{1,0:T(8,128)} %fusion.12.a_ref, f32[384,4096]{1,0:T(8,128)} %all-gather.9.cloned.1.call-done.g_ref), custom_call_target="tpu_custom_call" | custom-call | flops 1207959552 | bytes 8781824 | tf_op jit(solution)/shard_map/pallas_call | solution.py:43
  143.4 7.4 %all-to-all-start = ((f32[16,8,384]{2,1,0:T(8,128)}), f32[16,8,384]{2,1,0:T(8,128)S(1)}, u32[]{:S(2)}, u32[]{:S(2)}) async-start(f32[16,8,384]{2,1,0:T(8,128)} %bitcast.42), calls=%async_computation | async-start | bytes 393216 | tf_op jit(solution)/shard_map/all_to_all | solution.py:143
  150.8 0.0 copy-done.11
  150.8 0.2 select_reduce_fusion.1
  151.0 6.4 %all-to-all-done = f32[16,8,384]{2,1,0:T(8,128)S(1)} async-done(((f32[16,8,384]{2,1,0:T(8,128)}), f32[16,8,384]{2,1,0:T(8,128)S(1)}, u32[]{:S(2)}, u32[]{:S(2)}) %all-to-all-start) | async-done | bytes 196640 | tf_op jit(solution)/shard_map/all_to_all | solution.py:143
  157.4 0.0 copy-start.6
  157.4 0.7 subtract_divide_fusion
  (22 shorter events, 0.1 us)
Async XLA Ops:
  7.2 4.2 %copy-start.5 = (f32[4,24,4096]{2,1,0:T(8,128)S(1)}, f32[4,24,4096]{2,1,0:T(8,128)}, u32[]{:S(2)}) copy-start(f32[4,24,4096]{2,1,0:T(8,128)} %param.10) | copy-start | bytes 4718596
  7.2 2.3 %copy-start.8 = (s32[16]{0:T(128)S(1)}, s32[16]{0:T(128)}, u32[]{:S(2)}) copy-start(s32[16]{0:T(128)} %param.12) | copy-start | bytes 196
  7.2 104.4 %all-gather.7.cloned.1.call-start = ((), (), s32[]{:S(2)}) async-start(), calls=%async_computation.2 | async-start | bytes 13369344 | tf_op jit(solution)/shard_map/all_gather | solution.py:120
  9.5 125.4 %all-gather.9.cloned.1.call-start = ((), (), s32[]{:S(2)}) async-start(), calls=%async_computation.3 | async-start | bytes 6684672 | tf_op jit(solution)/shard_map/all_gather | solution.py:130
  11.5 13.6 %copy-start.7 = (s32[4]{0:T(128)S(1)}, s32[4]{0:T(128)}, u32[]{:S(2)}) copy-start(s32[4]{0:T(128)} %param.11) | copy-start | bytes 52
  11.5 12.4 %collective-permute-start.2 = (f32[24,4096]{1,0:T(8,128)S(1)}, f32[24,4096]{1,0:T(8,128)S(1)}, u32[]{:S(2)}, u32[]{:S(2)}) collective-permute-start(f32[24,4096]{1,0:T(8,128)S(1)} %get-tuple-element.42), channel_id=1, source_target_pairs={{0,8},{1,9},{2,10},{3,11},{4,12},{5,13},{6,14},{7,15},{8,0},{9,1},... | collective-permute-start | bytes 1179656 | tf_op jit(solution)/shard_map/ppermute | solution.py:111
  13.7 10.6 %collective-permute-start.3 = (f32[24,4096]{1,0:T(8,128)S(1)}, f32[24,4096]{1,0:T(8,128)S(1)}, u32[]{:S(2)}, u32[]{:S(2)}) collective-permute-start(f32[24,4096]{1,0:T(8,128)S(1)} %get-tuple-element.41), channel_id=1, source_target_pairs={{0,1},{1,0},{2,3},{3,2},{4,5},{5,4},{6,7},{7,6},{8,9},{9,8},{10,11... | collective-permute-start | bytes 1179656 | tf_op jit(solution)/shard_map/ppermute | solution.py:114
  47.7 48.2 %collective-permute-start = (f32[128,4096]{1,0:T(8,128)}, f32[128,4096]{1,0:T(8,128)}, u32[]{:S(2)}, u32[]{:S(2)}) collective-permute-start(f32[128,4096]{1,0:T(8,128)} %bitcast_add_fusion.3), channel_id=1, source_target_pairs={{0,8},{1,9},{2,10},{3,11},{4,12},{5,13},{6,14},{7,15},{8,0},{9,1},... | collective-permute-start | bytes 6291464 | tf_op jit(solution)/shard_map/ppermute | solution.py:112
  57.1 5.7 %copy-start.1 = (f32[1,128,4096]{2,1,0:T(8,128)S(1)}, f32[1,128,4096]{2,1,0:T(8,128)}, u32[]{:S(2)}) copy-start(f32[1,128,4096]{2,1,0:T(8,128)} %get-tuple-element.36) | copy-start | bytes 6291460
  61.2 46.7 %collective-permute-start.1 = (f32[128,4096]{1,0:T(8,128)}, f32[128,4096]{1,0:T(8,128)}, u32[]{:S(2)}, u32[]{:S(2)}) collective-permute-start(f32[128,4096]{1,0:T(8,128)} %bitcast_add_fusion.2), channel_id=1, source_target_pairs={{0,1},{1,0},{2,3},{3,2},{4,5},{5,4},{6,7},{7,6},{8,9},{9,8},{10,11... | collective-permute-start | bytes 6291464 | tf_op jit(solution)/shard_map/ppermute | solution.py:115
  85.0 3.4 %copy-start = (f32[1,128,4096]{1,2,0:T(8,128)S(1)}, f32[1,128,4096]{1,2,0:T(8,128)}, u32[]{:S(2)}) copy-start(f32[1,128,4096]{1,2,0:T(8,128)} %copy.48) | copy-start | bytes 6291460
  85.0 3.4 %copy-start.2 = (f32[128,64,64]{0,2,1:T(8,128)S(1)}, f32[128,64,64]{0,2,1:T(8,128)}, u32[]{:S(2)}) copy-start(f32[128,64,64]{0,2,1:T(8,128)} %copy.35) | copy-start | bytes 6291460
  88.4 19.5 %copy-start.4 = (f32[128,4096]{1,0:T(8,128)S(1)}, f32[128,4096]{1,0:T(8,128)}, u32[]{:S(2)}) copy-start(f32[128,4096]{1,0:T(8,128)} %copy.45) | copy-start | bytes 6291460
  111.6 11.0 %copy-start.3 = (f32[1,128,4096]{1,2,0:T(8,128)S(1)}, f32[1,128,4096]{1,2,0:T(8,128)}, u32[]{:S(2)}) copy-start(f32[1,128,4096]{1,2,0:T(8,128)} %bitcast_add_fusion.5) | copy-start | bytes 6291460
  143.3 7.4 %copy-start.11 = (s32[8,2]{0,1:T(2,128)S(1)}, s32[8,2]{0,1:T(2,128)}, u32[]{:S(2)}) copy-start(s32[8,2]{0,1:T(2,128)} %param.13) | copy-start | bytes 196
  143.3 7.5 %copy-start.10 = (f32[200]{0:T(256)S(1)}, f32[200]{0:T(256)}, u32[]{:S(2)}) copy-start(f32[200]{0:T(256)} %param.14) | copy-start | bytes 2404
  143.3 14.1 %copy-start.9 = (f32[384]{0:T(512)S(1)}, f32[384]{0:T(512)}, u32[]{:S(2)}) copy-start(f32[384]{0:T(512)} %param.15) | copy-start | bytes 4612
  143.4 14.0 %all-to-all-start = ((f32[16,8,384]{2,1,0:T(8,128)}), f32[16,8,384]{2,1,0:T(8,128)S(1)}, u32[]{:S(2)}, u32[]{:S(2)}) async-start(f32[16,8,384]{2,1,0:T(8,128)} %bitcast.42), calls=%async_computation | async-start | bytes 393216 | tf_op jit(solution)/shard_map/all_to_all | solution.py:143
  157.4 0.7 copy-start.6
Sparse Core Ops, SparseCore 0:
  9.8 78.5 all-gather.6
  90.2 44.5 all-gather.8
